TPU v7x, 768 devices: a whole 4x8x12 slice. The times are simulated.
768 devices in a mesh: mem: 24 (over z_lo, x), lon: 32 (over z_hi, y, core).
Axes of the slice: x: 4, y: 8, z: 12 (z_hi: 2, z_lo: 6; z = z_hi * 6 + z_lo), core: 2. Of those that a mesh axis runs over, the one named last changes fastest.
Arguments:
- state: float32 [768, 32, 96, 128], P('mem', None, 'lon'), may hold values from -6 to 6
- courant: float32 [32, 96, 128], P(None, 'lon'), may hold values from -0.95 to 0.95
- weighting: float32 [32, 32], replicated, may hold values from -1 to 1
- bias_in: bfloat16 [48, 1024], replicated, may hold values from -0.875 to 0.875
- bias_offset: float32 [1024], replicated, may hold values from -3 to 3
- bias_out: bfloat16 [1024, 32], replicated, may hold values from -0.1875 to 0.1875
- predictors: bfloat16 [24, 32, 16, 16], P('mem', 'lon'), may hold values from -6 to 6
- obs_column: int32 [24, 32, 256], P('mem', 'lon'), may hold values from 0 to 15
- obs_channel: int32 [24, 32, 256], P('mem', 'lon'), may hold values from 0 to 31
- obs_value: float32 [24, 32, 256], P('mem', 'lon'), may hold values from -18 to 18
- obs_error: float32 [32], replicated, may hold values from 1 to 3
Outputs:
- analysis: float32 [768, 32, 96, 128], P('mem', None, 'lon')
All inputs are finite; a program needn't handle non-finite values.
Results may differ from a plain program's by a relative error of at most 0.0014.
Values sent between devices are 32-bit elements; how exact they have to be, the bound alone decides.
No kernel may reach another device: no remote copies, remote signals or barrier semaphores. Data moves between devices by JAX's collectives and lax.ppermute only.
A program may use at most 64 MiB of HBM per device.

v0:
```python
import math

import jax
import jax.numpy as jnp
from jax import lax
from jax.sharding import PartitionSpec as P

highest = lax.Precision.HIGHEST


def padded_2(block, sides, width):
    for axis, dim in sides:
        count = lax.axis_size(axis)
        forward = [(i, i + 1) for i in range(count - 1)]
        forward.append((count - 1, 0))
        backward = [(target, source) for source, target in forward]
        low = lax.ppermute(
            lax.slice_in_dim(block, block.shape[dim] - width, None, axis=dim), axis, forward
        )
        high = lax.ppermute(lax.slice_in_dim(block, 0, width, axis=dim), axis, backward)
        block = jnp.concatenate([low, block, high], axis=dim)
    return block


def chebyshev_root(low_end, high_end):
    points = [
        0.5 * (high_end + low_end)
        + 0.5 * (high_end - low_end) * math.cos(math.pi * (index + 0.5) / 4.0)
        for index in range(4)
    ]
    coefficients = [0.0, 0.0, 0.0, 0.0]
    for index in range(4):
        basis_poly = [1.0]
        denominator = 1.0
        for other in range(4):
            if other != index:
                widened = [0.0] * (len(basis_poly) + 1)
                for power in range(len(basis_poly)):
                    widened[power + 1] += basis_poly[power]
                    widened[power] -= points[other] * basis_poly[power]
                basis_poly = widened
                denominator *= points[index] - points[other]
        factor = points[index] ** (-0.5) / denominator
        for power in range(4):
            coefficients[power] += factor * basis_poly[power]
    return tuple(coefficients)


def advect(padded, courant):
    east = padded[:, :, 2:, :]
    west = padded[:, :, :-2, :]
    centre = padded[:, :, 1:-1, :]
    return (
        centre
        - 0.5 * courant * (east - west)
        + 0.5 * courant * courant * (east - 2.0 * centre + west)
    )


def two_passes(field, courant):
    for repeat in range(2):
        padded = padded_2(field, (("lon", 2),), 1)
        field = advect(padded, courant)
    return field


def apply_root(multiply, vectors):
    root_coefs = chebyshev_root(0.5, 12.0)
    result = root_coefs[3] * vectors
    for degree in (2, 1, 0):
        result = multiply(result) + root_coefs[degree] * vectors
    return result


def analyse(
    patch_state,
    predictors,
    obs_column,
    obs_channel,
    obs_value,
    weighting,
    bias_in,
    bias_offset,
    bias_out,
    obs_error,
):
    members, levels, columns = patch_state.shape
    channels = weighting.shape[0]
    profile = jnp.transpose(patch_state, (0, 2, 1))
    phys = jnp.einsum("kcl,hl->kch", profile, weighting, precision=highest)
    extra = jnp.broadcast_to(predictors[None], (members, columns, predictors.shape[1]))
    net_in = jnp.concatenate([profile.astype(jnp.bfloat16), extra], axis=2)
    total_rows = members * columns
    block = 512
    blocks = net_in.reshape(total_rows // block, block, net_in.shape[2])

    def run_block(piece):
        hidden = jnp.tanh(
            jnp.dot(piece, bias_in, preferred_element_type=jnp.float32) + bias_offset
        ).astype(jnp.bfloat16)
        return jnp.dot(hidden, bias_out, preferred_element_type=jnp.float32)

    network = lax.map(run_block, blocks).reshape(members, columns, channels)
    table = (phys + network).reshape(members, columns * channels)
    picks = obs_column * channels + obs_channel
    hx = jnp.take(table, picks, axis=1)
    onehot = (obs_channel[:, None] == jnp.arange(channels, dtype=jnp.int32)[None, :]).astype(
        jnp.float32
    )
    sigma = jnp.sum(onehot * obs_error[None, :], axis=1)
    hmean = jnp.mean(hx, axis=0)
    root_count = math.sqrt(members - 1)
    spread = ((hx - hmean) / (sigma * root_count)).astype(jnp.bfloat16)
    innov = (obs_value - hmean) / sigma
    spread_wide = spread.astype(jnp.float32)
    scale = 1.0 + jnp.sum(spread_wide * spread_wide) / members
    gram = jnp.dot(spread, spread.T, preferred_element_type=jnp.float32)
    mtx = (jnp.eye(members, dtype=jnp.float32) + gram) / scale

    def multiply(vectors):
        return jnp.dot(mtx, vectors, precision=highest)

    drive = jnp.dot(spread_wide, innov, precision=highest)
    mean_weights = apply_root(multiply, apply_root(multiply, drive)) / (scale * root_count)
    flat = patch_state.reshape(members, levels * columns)
    xmean = jnp.mean(flat, axis=0)
    pert = flat - xmean
    spread_part = apply_root(multiply, pert)
    shift_part = jnp.dot(mean_weights, pert, precision=highest)
    result = xmean + spread_part / jnp.sqrt(scale) + shift_part
    return result.reshape(members, levels, columns)


def shards(
    state,
    courant,
    weighting,
    bias_in,
    bias_offset,
    bias_out,
    predictors,
    obs_column,
    obs_channel,
    obs_value,
    obs_error,
):
    mem_local, levels, lon_local, lat_rows = state.shape
    groups = lax.axis_size("mem")
    field = two_passes(state, courant)
    patch_cols = lon_local * lat_rows // groups
    outgoing = field.reshape(mem_local, levels, groups, patch_cols)
    arrived = lax.all_to_all(outgoing, "mem", split_axis=2, concat_axis=0, tiled=True)
    patch_state = arrived.reshape(mem_local * groups, levels, patch_cols)
    analysed = analyse(
        patch_state,
        predictors[0, 0],
        obs_column[0, 0],
        obs_channel[0, 0],
        obs_value[0, 0],
        weighting,
        bias_in,
        bias_offset,
        bias_out,
        obs_error,
    )
    returning = analysed.reshape(mem_local * groups, levels, 1, patch_cols)
    restored = lax.all_to_all(returning, "mem", split_axis=0, concat_axis=2, tiled=True)
    restored = restored.reshape(mem_local, levels, lon_local, lat_rows)
    return two_passes(restored, courant)


def solution(mesh):
    placed = (
        P("mem", None, "lon", None),
        P(None, "lon", None),
        P(),
        P(),
        P(),
        P(),
        P("mem", "lon", None, None),
        P("mem", "lon", None),
        P("mem", "lon", None),
        P("mem", "lon", None),
        P(),
    )
    return jax.shard_map(
        shards, mesh=mesh, in_specs=placed, out_specs=P("mem", None, "lon", None), check_vma=False
    )
```

profile of v0, /device:TPU:61, one launch (start us, length us, event | category | flops | bytes accessed | tf_op | source)
XLA Modules:
  0.0 506.1 jit_solution(9407611006565425331)
XLA Ops:
  4.0 14.1 %collective-permute-start.1 = (f32[32,32,1,128]{3,1,2,0:T(8,128)S(1)}, f32[32,32,1,128]{3,1,2,0:T(8,128)}, u32[]{:S(2)}, u32[]{:S(2)}) collective-permute-start(f32[32,32,1,128]{3,1,2,0:T(8,128)S(1)} %get-tuple-element.63), channel_id=1, source_target_pairs={{0,1},{1,2},{2,3},{3,4},{4,5},{5,6},{6,7},{7,8},{8,9},{9,10},{10,1... | collective-permute-start | bytes 1572872 | tf_op jit(solution)/shard_map/ppermute | solution.py:17
  18.1 4.0 copy.143
  24.6 2.7 pad_maximum_fusion.7
  27.3 5.0 copy.177
  32.3 3.9 copy.178
  36.2 7.7 %multiply_add_fusion.3 = f32[32,32,3,128]{1,3,2,0:T(8,128)S(1)} fusion(f32[32,32,3,128]{1,3,2,0:T(8,128)} %copy.178, f32[32,32,3,128]{1,3,2,0:T(8,128)} %copy.177, f32[32,32,3,128]{1,3,2,0:T(8,128)} %copy.143, f32[32,3,128]{0,2,1:T(8,128)S(1)} %copy.144, f32[32,3,128]{0,2,1:T(8,128)S(1)} %copy.140), kind=kLoop, calls=%fused_computation.18 | loop fusion | flops 3145728 | bytes 6389760 | tf_op jit(solution)/shard_map/add | solution.py:54
  49.4 12.7 %collective-permute-start.3 = (f32[32,32,1,128]{3,1,2,0:T(8,128)S(1)}, f32[32,32,1,128]{3,1,2,0:T(8,128)S(1)}, u32[]{:S(2)}, u32[]{:S(2)}) collective-permute-start(f32[32,32,1,128]{3,1,2,0:T(8,128)S(1)} %copy.148), channel_id=1, source_target_pairs={{0,1},{1,2},{2,3},{3,4},{4,5},{5,6},{6,7},{7,8},{8,9},{9,10},{10,1... | collective-permute-start | bytes 1572872 | tf_op jit(solution)/shard_map/ppermute | solution.py:17
  65.4 2.8 collective-permute-done.3
  68.8 13.9 %collective-permute-done.2 = f32[32,32,1,128]{3,1,2,0:T(8,128)} collective-permute-done((f32[32,32,1,128]{3,1,2,0:T(8,128)}, f32[32,32,1,128]{3,1,2,0:T(8,128)}, u32[]{:S(2)}, u32[]{:S(2)}) %collective-permute-start.2) | collective-permute-done | bytes 524320 | tf_op jit(solution)/shard_map/ppermute | solution.py:20
  82.8 3.0 copy.147
  85.8 7.0 %multiply_add_fusion.2 = f32[32,32,3,128]{1,3,2,0:T(8,128)S(1)} fusion(f32[32,32,3,128]{1,3,2,0:T(8,128)} %copy-done.4, f32[32,32,1,128]{1,3,2,0:T(8,128)} %copy.147, f32[32,32,1,128]{1,3,2,0:T(8,128)S(1)} %copy.149, f32[32,3,128]{0,2,1:T(8,128)S(1)} %copy.144, f32[32,3,128]{0,2,1:T(8,128)S(1)} %copy.140), kind=kLoop, calls=%fused_computation.17 | loop fusion | flops 3932160 | bytes 4292608 | tf_op jit(solution)/shard_map/add | solution.py:54
  92.8 3.3 copy.180
  96.1 5.9 %reshape.125 = f32[24,1,16384]{2,1,0:T(1,128)} reshape(f32[24,32,16,32]{3,2,1,0:T(8,128)} %bitcast.92) | data formatting | bytes 3145728
  102.0 24.6 %all-to-all-start = ((f32[24,1,16384]{2,1,0:T(1,128)}), f32[24,1,16384]{2,1,0:T(1,128)S(1)}, u32[]{:S(2)}, u32[]{:S(2)}) async-start(f32[24,1,16384]{2,1,0:T(1,128)} %reshape.125), calls=%async_computation | async-start | bytes 3145728 | tf_op jit(solution)/shard_map/all_to_all | solution.py:152
  128.4 32.8 %all-to-all-done = f32[24,1,16384]{2,1,0:T(1,128)S(1)} async-done(((f32[24,1,16384]{2,1,0:T(1,128)}), f32[24,1,16384]{2,1,0:T(1,128)S(1)}, u32[]{:S(2)}, u32[]{:S(2)}) %all-to-all-start) | async-done | bytes 1572896 | tf_op jit(solution)/shard_map/all_to_all | solution.py:152
  161.8 4.5 reduce.17
  166.2 4.0 reshape.126
  170.3 3.8 bitcast_reduce_fusion
  174.9 3.3 bitcast_bitcast_fusion
  178.9 5.1 %copy.174 = f32[768,32,16]{0,1,2:T(8,128)S(1)} copy(f32[768,32,16]{1,2,0:T(8,128)} %bitcast.86) | data formatting | bytes 3145728 | tf_op jit(solution)/shard_map/reshape | solution.py:153
  184.9 3.9 copy.154
  188.8 52.2 %while.10 = (s32[]{:T(128)}, f32[24,512,32]{1,2,0:T(8,128)}, bf16[24,512,48]{2,1,0:T(8,128)(2,1)}, bf16[48,1024]{1,0:T(8,128)(2,1)S(1)}, f32[1024]{0:T(1024)S(1)}, /*index=5*/bf16[1024,32]{0,1:T(8,128)(2,1)S(1)}, s32[]{:T(128)}) while((s32[]{:T(128)}, f32[24,512,32]{1,2,0:T(8,128)}, bf16[24,512,48]{2,1,0:T(8,128)(2,1)}, ...), condition=%wide.region_2.3_spmd, body=%wide.region_1.2_spmd.sunk | while | flops 84934656 | bytes 365653 | solution.py:103
  241.0 5.0 copy.155
  246.0 6.5 %copy.156 = f32[768,16,32]{0,2,1:T(8,128)} copy(f32[768,16,32]{2,1,0:T(8,128)} %bitcast.94) | data formatting | bytes 3145728 | tf_op jit(solution)/shard_map/reshape | solution.py:103
  252.5 2.9 fusion.20
  272.2 9.1 %copy.157 = f32[24,32,32,1,16]{1,0,4,2,3:T(8,128)} copy(f32[24,32,32,1,16]{2,4,1,0,3:T(8,128)} %bitcast_bitcast_fusion) | data formatting | bytes 3145728 | tf_op jit(solution)/shard_map/all_to_all | solution.py:152
  281.3 5.2 %reshape_reshape.6 = f32[768,512]{0,1:T(8,128)} reshape(f32[24,32,32,1,16]{1,0,4,2,3:T(8,128)} %copy.157) | data formatting | bytes 3145728 | tf_op jit(solution)/shard_map/reshape;reshape | solution.py:125
  286.5 3.0 copy.158
  289.5 5.5 %fusion.18 = f32[768,512]{1,0:T(8,128)S(1)} fusion(f32[768,768]{1,0:T(8,128)S(1)} %add_divide_fusion, f32[768,512]{1,0:T(8,128)} %copy.158, f32[512]{0:T(512)S(1)} %copy-done.9), kind=kOutput, calls=%fused_computation.33 | convolution fusion | flops 3624665088 | bytes 5507072 | tf_op jit(solution)/shard_map/dot_general | solution.py:121
  295.9 4.0 fusion.15
  299.9 5.6 %add_add_fusion = f32[768,512]{1,0:T(8,128)} fusion(f32[768,768]{1,0:T(8,128)S(1)} %add_divide_fusion, f32[768,512]{1,0:T(8,128)S(1)} %fusion.15, f32[768,512]{1,0:T(8,128)S(1)} %copy-done.5, f32[512]{0:T(512)S(1)} %bitcast.104, f32[]{:T(128)S(6)} %sqrt.3, f32[512]{0:T(512)S(1)} %copy-done.9), kind=kOutput, calls=%fused_computation.26 | convolution fusion | flops 3627417600 | bytes 7081988 | tf_op jit(solution)/shard_map/dot_general | solution.py:121
  307.4 5.2 %copy.161 = f32[768,32,1,16]{1,3,2,0:T(8,128)} copy(f32[768,32,1,16]{0,3,1,2:T(8,128)S(1)} %bitcast.96) | data formatting | bytes 3145728 | tf_op jit(solution)/shard_map/reshape;reshape | solution.py:166
  312.6 5.0 reshape.127
  317.6 59.1 %all_to_all.30 = f32[24,1,16384]{2,1,0:T(1,128)S(1)} all-to-all(f32[24,1,16384]{2,1,0:T(1,128)S(1)} %reshape.127), channel_id=1, replica_groups=mesh['mem'=24,'lon'=32] {'mem'}, dimensions={0} | all-to-all | bytes 3145728 | tf_op jit(solution)/shard_map/all_to_all | solution.py:167
  376.7 4.5 reduce.18
  381.2 4.1 reshape.128
  385.2 9.1 %copy.175 = f32[24,32,32,1,16]{1,0,4,2,3:T(8,128)} copy(f32[24,32,32,1,16]{2,4,1,0,3:T(8,128)} %bitcast.93) | data formatting | bytes 3145728 | tf_op jit(solution)/shard_map/all_to_all | solution.py:167
  394.3 9.4 %copy.163 = f32[32,32,24,1,16]{1,4,2,0,3:T(8,128)} copy(f32[32,32,24,1,16]{0,2,4,1,3:T(8,128)} %bitcast.91) | data formatting | bytes 3145728 | tf_op jit(solution)/shard_map/all_to_all | solution.py:167
  403.7 3.9 fusion.44
  415.5 13.6 %collective-permute-done.5 = f32[32,32,1,128]{3,1,2,0:T(8,128)S(1)} collective-permute-done((f32[32,32,1,128]{3,1,2,0:T(8,128)S(1)}, f32[32,32,1,128]{3,1,2,0:T(8,128)S(1)}, u32[]{:S(2)}, u32[]{:S(2)}) %collective-permute-start.5) | collective-permute-done | bytes 524320 | tf_op jit(solution)/shard_map/ppermute | solution.py:17
  429.8 13.8 %collective-permute-done.4 = f32[32,32,1,128]{3,1,2,0:T(8,128)} collective-permute-done((f32[32,32,1,128]{3,1,2,0:T(8,128)}, f32[32,32,1,128]{3,1,2,0:T(8,128)}, u32[]{:S(2)}, u32[]{:S(2)}) %collective-permute-start.4) | collective-permute-done | bytes 524320 | tf_op jit(solution)/shard_map/ppermute | solution.py:20
  443.6 3.0 copy.165
  446.6 7.3 %multiply_add_fusion.1 = f32[32,32,3,128]{1,3,2,0:T(8,128)S(1)} fusion(f32[32,32,3,128]{1,3,2,0:T(8,128)} %bitcast.88, f32[32,32,1,128]{1,3,2,0:T(8,128)} %copy.165, f32[32,32,1,128]{1,3,2,0:T(8,128)S(1)} %copy.167, f32[32,3,128]{0,2,1:T(8,128)S(1)} %copy.144, f32[32,3,128]{0,2,1:T(8,128)S(1)} %copy.140), kind=kLoop, calls=%fused_computation.16 | loop fusion | flops 3932160 | bytes 4292608 | tf_op jit(solution)/shard_map/add | solution.py:54
  465.0 8.7 %collective-permute-done.7 = f32[32,32,1,128]{3,1,2,0:T(8,128)S(1)} collective-permute-done((f32[32,32,1,128]{3,1,2,0:T(8,128)S(1)}, f32[32,32,1,128]{3,1,2,0:T(8,128)S(1)}, u32[]{:S(2)}, u32[]{:S(2)}) %collective-permute-start.7) | collective-permute-done | bytes 524320 | tf_op jit(solution)/shard_map/ppermute | solution.py:17
  474.4 13.9 %collective-permute-done.6 = f32[32,32,1,128]{3,1,2,0:T(8,128)} collective-permute-done((f32[32,32,1,128]{3,1,2,0:T(8,128)}, f32[32,32,1,128]{3,1,2,0:T(8,128)}, u32[]{:S(2)}, u32[]{:S(2)}) %collective-permute-start.6) | collective-permute-done | bytes 524320 | tf_op jit(solution)/shard_map/ppermute | solution.py:20
  488.2 3.0 copy.169
  491.2 8.9 %multiply_add_fusion = f32[32,32,3,128]{1,3,2,0:T(8,128)} fusion(f32[32,32,3,128]{1,3,2,0:T(8,128)} %copy-done.3, f32[32,32,1,128]{1,3,2,0:T(8,128)} %copy.169, f32[32,32,1,128]{1,3,2,0:T(8,128)S(1)} %copy.171, f32[32,3,128]{0,2,1:T(8,128)S(1)} %copy.144, f32[32,3,128]{0,2,1:T(8,128)S(1)} %copy.140), kind=kLoop, calls=%fused_computation.15 | loop fusion | flops 3932160 | bytes 4292608 | tf_op jit(solution)/shard_map/add | solution.py:54
  500.1 5.5 %copy.172 = f32[32,32,3,128]{3,1,2,0:T(8,128)} copy(f32[32,32,3,128]{1,3,2,0:T(8,128)} %multiply_add_fusion) | data formatting | bytes 3145728 | tf_op jit(solution)/shard_map/add | solution.py:54
  (128 shorter events, 111.6 us)
Async XLA Ops:
  0.0 252.5 %copy-start = (f32[32,32]{1,0:T(8,128)S(1)}, f32[32,32]{1,0:T(8,128)}, u32[]{:S(2)}) copy-start(f32[32,32]{1,0:T(8,128)} %param.15) | copy-start | bytes 12292
  0.0 18.1 %copy-start.6 = (f32[32,32,3,128]{3,1,2,0:T(8,128)S(1)}, f32[32,32,3,128]{3,1,2,0:T(8,128)}, u32[]{:S(2)}) copy-start(f32[32,32,3,128]{3,1,2,0:T(8,128)} %param.13) | copy-start | bytes 4718596
  1.4 22.4 %collective-permute-start = (f32[32,32,1,128]{3,1,2,0:T(8,128)S(1)}, f32[32,32,1,128]{3,1,2,0:T(8,128)S(1)}, u32[]{:S(2)}, u32[]{:S(2)}) collective-permute-start(f32[32,32,1,128]{3,1,2,0:T(8,128)S(1)} %get-tuple-element.62), channel_id=1, source_target_pairs={{1,0},{2,1},{3,2},{4,3},{5,4},{6,5},{7,6},{8,7},{9,8},{10,9},{11,1... | collective-permute-start | bytes 1572872 | tf_op jit(solution)/shard_map/ppermute | solution.py:20
  4.0 18.1 %copy-start.8 = (f32[32,3,128]{2,0,1:T(8,128)S(1)}, f32[32,3,128]{2,0,1:T(8,128)}, u32[]{:S(2)}) copy-start(f32[32,3,128]{2,0,1:T(8,128)} %param.14) | copy-start | bytes 147460
  4.0 20.6 %collective-permute-start.1 = (f32[32,32,1,128]{3,1,2,0:T(8,128)S(1)}, f32[32,32,1,128]{3,1,2,0:T(8,128)}, u32[]{:S(2)}, u32[]{:S(2)}) collective-permute-start(f32[32,32,1,128]{3,1,2,0:T(8,128)S(1)} %get-tuple-element.63), channel_id=1, source_target_pairs={{0,1},{1,2},{2,3},{3,4},{4,5},{5,6},{6,7},{7,8},{8,9},{9,10},{10,1... | collective-permute-start | bytes 1572872 | tf_op jit(solution)/shard_map/ppermute | solution.py:17
  23.8 0.8 copy-start.7
  43.9 3.3 copy-start.4
  49.4 18.9 %collective-permute-start.3 = (f32[32,32,1,128]{3,1,2,0:T(8,128)S(1)}, f32[32,32,1,128]{3,1,2,0:T(8,128)S(1)}, u32[]{:S(2)}, u32[]{:S(2)}) collective-permute-start(f32[32,32,1,128]{3,1,2,0:T(8,128)S(1)} %copy.148), channel_id=1, source_target_pairs={{0,1},{1,2},{2,3},{3,4},{4,5},{5,6},{6,7},{7,8},{8,9},{9,10},{10,1... | collective-permute-start | bytes 1572872 | tf_op jit(solution)/shard_map/ppermute | solution.py:17
  63.5 19.3 %collective-permute-start.2 = (f32[32,32,1,128]{3,1,2,0:T(8,128)}, f32[32,32,1,128]{3,1,2,0:T(8,128)}, u32[]{:S(2)}, u32[]{:S(2)}) collective-permute-start(f32[32,32,1,128]{3,1,2,0:T(8,128)} %copy.146), channel_id=1, source_target_pairs={{1,0},{2,1},{3,2},{4,3},{5,4},{6,5},{7,6},{8,7},{9,8},{10,9},{11,1... | collective-permute-start | bytes 1572872 | tf_op jit(solution)/shard_map/ppermute | solution.py:20
  102.0 24.6 %copy-start.10 = (s32[1,1,256]{2,1,0:T(1,128)S(1)}, s32[1,1,256]{2,1,0:T(1,128)}, u32[]{:S(2)}) copy-start(s32[1,1,256]{2,1,0:T(1,128)} %param.21) | copy-start | bytes 3076
  102.0 24.6 %copy-start.13 = (s32[1,1,256]{2,1,0:T(1,128)S(1)}, s32[1,1,256]{2,1,0:T(1,128)}, u32[]{:S(2)}) copy-start(s32[1,1,256]{2,1,0:T(1,128)} %param.20) | copy-start | bytes 3076
  102.0 25.3 %copy-start.16 = (f32[32]{0:T(128)S(1)}, f32[32]{0:T(128)}, u32[]{:S(2)}) copy-start(f32[32]{0:T(128)} %param.23) | copy-start | bytes 388
  102.0 59.2 %all-to-all-start = ((f32[24,1,16384]{2,1,0:T(1,128)}), f32[24,1,16384]{2,1,0:T(1,128)S(1)}, u32[]{:S(2)}, u32[]{:S(2)}) async-start(f32[24,1,16384]{2,1,0:T(1,128)} %reshape.125), calls=%async_computation | async-start | bytes 3145728 | tf_op jit(solution)/shard_map/all_to_all | solution.py:152
  170.3 4.6 copy-start.2
  184.0 0.7 copy-start.12
  184.9 3.9 copy-start.17
  184.9 3.9 copy-start.18
  184.9 3.9 copy-start.19
  255.4 1.4 copy-start.11
  255.4 1.6 copy-start.14
  255.4 1.6 copy-start.15
  286.5 3.0 copy-start.9
  289.5 5.5 %copy-start.5 = (f32[768,512]{1,0:T(8,128)S(1)}, f32[768,512]{1,0:T(8,128)}, u32[]{:S(2)}) copy-start(f32[768,512]{1,0:T(8,128)} %copy.158) | copy-start | bytes 4718596
  409.8 19.3 %collective-permute-start.5 = (f32[32,32,1,128]{3,1,2,0:T(8,128)S(1)}, f32[32,32,1,128]{3,1,2,0:T(8,128)S(1)}, u32[]{:S(2)}, u32[]{:S(2)}) collective-permute-start(f32[32,32,1,128]{3,1,2,0:T(8,128)S(1)} %copy.166), channel_id=1, source_target_pairs={{0,1},{1,2},{2,3},{3,4},{4,5},{5,6},{6,7},{7,8},{8,9},{9,10},{10,1... | collective-permute-start | bytes 1572872 | tf_op jit(solution)/shard_map/ppermute | solution.py:17
  413.1 30.5 %collective-permute-start.4 = (f32[32,32,1,128]{3,1,2,0:T(8,128)}, f32[32,32,1,128]{3,1,2,0:T(8,128)}, u32[]{:S(2)}, u32[]{:S(2)}) collective-permute-start(f32[32,32,1,128]{3,1,2,0:T(8,128)} %copy.164), channel_id=1, source_target_pairs={{1,0},{2,1},{3,2},{4,3},{5,4},{6,5},{7,6},{8,7},{9,8},{10,9},{11,1... | collective-permute-start | bytes 1572872 | tf_op jit(solution)/shard_map/ppermute | solution.py:20
  453.9 3.3 copy-start.3
  459.3 14.5 %collective-permute-start.7 = (f32[32,32,1,128]{3,1,2,0:T(8,128)S(1)}, f32[32,32,1,128]{3,1,2,0:T(8,128)S(1)}, u32[]{:S(2)}, u32[]{:S(2)}) collective-permute-start(f32[32,32,1,128]{3,1,2,0:T(8,128)S(1)} %copy.170), channel_id=1, source_target_pairs={{0,1},{1,2},{2,3},{3,4},{4,5},{5,6},{6,7},{7,8},{8,9},{9,10},{10,1... | collective-permute-start | bytes 1572872 | tf_op jit(solution)/shard_map/ppermute | solution.py:17
  462.6 25.6 %collective-permute-start.6 = (f32[32,32,1,128]{3,1,2,0:T(8,128)}, f32[32,32,1,128]{3,1,2,0:T(8,128)}, u32[]{:S(2)}, u32[]{:S(2)}) collective-permute-start(f32[32,32,1,128]{3,1,2,0:T(8,128)} %copy.168), channel_id=1, source_target_pairs={{1,0},{2,1},{3,2},{4,3},{5,4},{6,5},{7,6},{8,7},{9,8},{10,9},{11,1... | collective-permute-start | bytes 1572872 | tf_op jit(solution)/shard_map/ppermute | solution.py:20
  491.2 14.4 %copy-start.1 = (f32[32,32]{1,0:T(8,128)S(1)}, f32[32,32]{1,0:T(8,128)}, u32[]{:S(2)}) copy-start(f32[32,32]{1,0:T(8,128)} %param.15) | copy-start | bytes 12292
where the time goes:
time: 515 us; the launch traced here: 506 us
  local copies, waits for them, and re-layouts  147 us (29%)
  waiting for transfers between devices  99.7 us (19%)
  matrix products  84.3 us (16%)
  starting transfers between devices  64.6 us (13%)
  blocking collectives  59.1 us (11%)
  other arithmetic  50 us (10%)
    all_to_all x1, blocking collectives, shards(): lax.all_to_all(returning, 'mem', split_axis=0, concat_axis=2, tiled=True)  59.1 us
    dot_general x24, matrix products, run_block(): return jnp.dot(hidden, bias_out, preferred_element_type=jnp.float32)  52.2 us
    ppermute x4, waiting for transfers between devices, padded_2(): lax.ppermute(lax.slice_in_dim(block, 0, width, axis=dim), axis, backward)  41.6 us
    unnamed x47, local copies, waits for them, and re-layouts  36.8 us
    all_to_all x1, waiting for transfers between devices, shards(): lax.all_to_all(outgoing, 'mem', split_axis=2, concat_axis=0, tiled=True)  32.8 us
    add x4, other arithmetic, advect(): centre - 0.5 * courant * (east - west)  30.9 us
    ppermute x4, starting transfers between devices, padded_2(): lax.ppermute(lax.slice_in_dim(block, block.shape[dim] - width, None, axis...  30.7 us
    dot_general x9, matrix products, multiply(): return jnp.dot(mtx, vectors, precision=highest)  27.5 us
  transfers between devices with their start and end apart: 9, of which 7 were waited for; matrix products, arithmetic and copies ran while one was open for 3% of the time, Pallas kernels for 0%

commit v1 on v0

v1 whole, which is shorter than its diff:
```python
import functools
import math

import jax
import jax.numpy as jnp
from jax import lax
from jax.experimental import pallas as pl
from jax.experimental.pallas import tpu as pltpu
from jax.sharding import PartitionSpec as P

highest = lax.Precision.HIGHEST


def chebyshev_root(low_end, high_end):
    points = [
        0.5 * (high_end + low_end)
        + 0.5 * (high_end - low_end) * math.cos(math.pi * (index + 0.5) / 4.0)
        for index in range(4)
    ]
    coefficients = [0.0, 0.0, 0.0, 0.0]
    for index in range(4):
        basis_poly = [1.0]
        denominator = 1.0
        for other in range(4):
            if other != index:
                widened = [0.0] * (len(basis_poly) + 1)
                for power in range(len(basis_poly)):
                    widened[power + 1] += basis_poly[power]
                    widened[power] -= points[other] * basis_poly[power]
                basis_poly = widened
                denominator *= points[index] - points[other]
        factor = points[index] ** (-0.5) / denominator
        for power in range(4):
            coefficients[power] += factor * basis_poly[power]
    return tuple(coefficients)


def ring_shift(block, axis, step):
    count = lax.axis_size(axis)
    pairs = [(i, (i + step) % count) for i in range(count)]
    return lax.ppermute(block, axis, pairs)


def advect_step(west, centre, east, courant):
    return (
        centre
        - 0.5 * courant * (east - west)
        + 0.5 * courant * courant * (east - 2.0 * centre + west)
    )


def two_passes(field, courant_padded):
    width = field.shape[1]
    from_left = ring_shift(field[:, width - 2 :], "lon", 1)
    from_right = ring_shift(field[:, :2], "lon", -1)
    padded = jnp.concatenate([from_left, field, from_right], axis=1)
    first = advect_step(
        padded[:, : width + 2], padded[:, 1 : width + 3], padded[:, 2 : width + 4], courant_padded
    )
    return advect_step(
        first[:, :width], first[:, 1 : width + 1], first[:, 2 : width + 2], courant_padded[1:-1]
    )


def apply_root(multiply, vectors):
    root_coefs = chebyshev_root(0.5, 12.0)
    result = root_coefs[3] * vectors
    for degree in (2, 1, 0):
        result = multiply(result) + root_coefs[degree] * vectors
    return result


def network_kernel(x_ref, w_in_ref, offset_ref, w_out_ref, out_ref):
    pre = jnp.dot(x_ref[...], w_in_ref[...], preferred_element_type=jnp.float32)
    hidden = jnp.tanh(pre + offset_ref[...]).astype(jnp.bfloat16)
    out_ref[...] = jnp.dot(hidden, w_out_ref[...], preferred_element_type=jnp.float32)


def network(net_in, bias_in, bias_offset, bias_out, rows=512):
    total, nin = net_in.shape
    hid = bias_in.shape[1]
    channels = bias_out.shape[1]
    return pl.pallas_call(
        network_kernel,
        out_shape=jax.ShapeDtypeStruct((total, channels), jnp.float32),
        grid=(total // rows,),
        in_specs=[
            pl.BlockSpec((rows, nin), lambda i: (i, 0)),
            pl.BlockSpec((nin, hid), lambda i: (0, 0)),
            pl.BlockSpec((1, hid), lambda i: (0, 0)),
            pl.BlockSpec((hid, channels), lambda i: (0, 0)),
        ],
        out_specs=pl.BlockSpec((rows, channels), lambda i: (i, 0)),
        cost_estimate=pl.CostEstimate(
            flops=2 * total * hid * (nin + channels),
            transcendentals=total * hid,
            bytes_accessed=total * (nin * 2 + channels * 4),
        ),
    )(net_in, bias_in, bias_offset.reshape(1, hid), bias_out)


def analyse(
    flat,
    predictors,
    obs_column,
    obs_channel,
    obs_value,
    weighting,
    bias_in,
    bias_offset,
    bias_out,
    obs_error,
    levels,
    columns,
):
    members = flat.shape[0]
    channels = weighting.shape[0]
    profile = jnp.transpose(flat.reshape(members, levels, columns), (0, 2, 1))
    rows = profile.reshape(members * columns, levels)
    phys = jnp.dot(rows, weighting.T, precision=highest)
    extra = jnp.broadcast_to(predictors[None], (members, columns, predictors.shape[1]))
    net_in = jnp.concatenate([profile.astype(jnp.bfloat16), extra], axis=2)
    net_in = net_in.reshape(members * columns, net_in.shape[2])
    evolved = phys + network(net_in, bias_in, bias_offset, bias_out)
    table = evolved.reshape(members, columns * channels)
    picks = obs_column * channels + obs_channel
    hx = jnp.take(table, picks, axis=1)
    onehot = (obs_channel[:, None] == jnp.arange(channels, dtype=jnp.int32)[None, :]).astype(
        jnp.float32
    )
    sigma = jnp.sum(onehot * obs_error[None, :], axis=1)
    hmean = jnp.mean(hx, axis=0)
    root_count = math.sqrt(members - 1)
    spread = ((hx - hmean) / (sigma * root_count)).astype(jnp.bfloat16)
    innov = (obs_value - hmean) / sigma
    spread_wide = spread.astype(jnp.float32)
    scale = 1.0 + jnp.sum(spread_wide * spread_wide) / members
    gram = jnp.dot(spread, spread.T, preferred_element_type=jnp.float32)
    mtx = (jnp.eye(members, dtype=jnp.float32) + gram) / scale

    def multiply(vectors):
        return jnp.dot(mtx, vectors, precision=highest)

    drive = jnp.dot(spread_wide, innov, precision=highest)
    mean_weights = apply_root(multiply, apply_root(multiply, drive)) / (scale * root_count)
    xmean = jnp.mean(flat, axis=0)
    pert = flat - xmean
    spread_part = apply_root(multiply, pert)
    shift_part = jnp.dot(mean_weights, pert, precision=highest)
    return xmean + spread_part / jnp.sqrt(scale) + shift_part


def shards(
    state,
    courant,
    weighting,
    bias_in,
    bias_offset,
    bias_out,
    predictors,
    obs_column,
    obs_channel,
    obs_value,
    obs_error,
):
    mem_local, levels, lon_local, lat_rows = state.shape
    groups = lax.axis_size("mem")
    patch_cols = lon_local * lat_rows // groups
    blocks = lat_rows // patch_cols
    field = jnp.transpose(state, (0, 2, 1, 3))
    wind = jnp.transpose(courant, (1, 0, 2))
    wind_padded = jnp.concatenate(
        [ring_shift(wind[-1:], "lon", 1), wind, ring_shift(wind[:1], "lon", -1)], axis=0
    )
    field = two_passes(field, wind_padded)
    outgoing = field.reshape(mem_local, lon_local, levels, blocks, patch_cols)
    outgoing = jnp.transpose(outgoing, (1, 3, 0, 2, 4)).reshape(
        groups, mem_local, levels * patch_cols
    )
    arrived = lax.all_to_all(outgoing, "mem", split_axis=0, concat_axis=0, tiled=True)
    flat = arrived.reshape(groups * mem_local, levels * patch_cols)
    analysed = analyse(
        flat,
        predictors[0, 0],
        obs_column[0, 0],
        obs_channel[0, 0],
        obs_value[0, 0],
        weighting,
        bias_in,
        bias_offset,
        bias_out,
        obs_error,
        levels,
        patch_cols,
    )
    returning = analysed.reshape(groups, mem_local, levels * patch_cols)
    restored = lax.all_to_all(returning, "mem", split_axis=0, concat_axis=0, tiled=True)
    restored = restored.reshape(lon_local, blocks, mem_local, levels, patch_cols)
    restored = jnp.transpose(restored, (2, 0, 3, 1, 4)).reshape(
        mem_local, lon_local, levels, lat_rows
    )
    field = two_passes(restored, wind_padded)
    return jnp.transpose(field, (0, 2, 1, 3))


def solution(mesh):
    placed = (
        P("mem", None, "lon", None),
        P(None, "lon", None),
        P(),
        P(),
        P(),
        P(),
        P("mem", "lon", None, None),
        P("mem", "lon", None),
        P("mem", "lon", None),
        P("mem", "lon", None),
        P(),
    )
    return jax.shard_map(
        shards, mesh=mesh, in_specs=placed, out_specs=P("mem", None, "lon", None), check_vma=False
    )
```

time: 515 us -> 338 us (0.66)
  the two profiles are of different devices: /device:TPU:61 before, /device:TPU:128 now
where the time goes in v1:
time: 338 us; the launch traced here: 333 us
  local copies, waits for them, and re-layouts  76.9 us (23%)
  starting transfers between devices  71.7 us (21%)
  waiting for transfers between devices  62.9 us (19%)
  blocking collectives  50.4 us (15%)
  matrix products  35.8 us (11%)
  Pallas kernels  23.7 us (7%)
  other arithmetic  10.3 us (3%)
    all_to_all x1, blocking collectives, shards(): lax.all_to_all(returning, 'mem', split_axis=0, concat_axis=0, tiled=True)  50.4 us
    ppermute x6, starting transfers between devices, ring_shift(): return lax.ppermute(block, axis, pairs)  44.9 us
    ppermute x6, waiting for transfers between devices, ring_shift(): return lax.ppermute(block, axis, pairs)  35.2 us
    all_to_all x1, waiting for transfers between devices, shards(): lax.all_to_all(outgoing, 'mem', split_axis=0, concat_axis=0, tiled=True)  27.7 us
    all_to_all x1, starting transfers between devices, shards(): lax.all_to_all(outgoing, 'mem', split_axis=0, concat_axis=0, tiled=True)  26.7 us
    dot_general x9, matrix products, multiply(): return jnp.dot(mtx, vectors, precision=highest)  24.5 us
    pallas_call x1, Pallas kernels, network(): pl.pallas_call(network_kernel, out_shape=jax.ShapeDtypeStruct((total, cha...  23.7 us
    slice x3, local copies, waits for them, and re-layouts, two_passes(): from_left = ring_shift(field[:, width - 2:], 'lon', 1)  13.5 us
  transfers between devices with their start and end apart: 7, of which 5 were waited for; matrix products, arithmetic and copies ran while one was open for 3% of the time, Pallas kernels for 0%

profile of v1, /device:TPU:128, one launch (start us, length us, event | category | flops | bytes accessed | tf_op | source)
XLA Modules:
  0.0 333.1 jit_solution(4237137052298081244)
XLA Ops:
  0.0 1.9 fusion.21
  2.0 1.9 collective-permute-start
  3.9 15.1 %collective-permute-start.1 = (f32[32,2,32,128]{3,2,1,0:T(8,128)S(1)}, f32[32,2,32,128]{3,2,1,0:T(8,128)S(1)}, u32[]{:S(2)}, u32[]{:S(2)}) collective-permute-start(f32[32,2,32,128]{3,2,1,0:T(8,128)S(1)} %get-tuple-element.12), channel_id=1, source_target_pairs={{0,31},{1,0},{2,1},{3,2},{4,3},{5,4},{6,5},{7,6},{8,7},{9,8},{10,9... | collective-permute-start | bytes 3145736 | tf_op jit(solution)/shard_map/ppermute | solution.py:41
  19.0 1.9 collective-permute-start.2
  20.9 12.1 %collective-permute-start.3 = (f32[1,32,128]{2,1,0:T(8,128)S(1)}, f32[1,32,128]{2,1,0:T(8,128)S(1)}, u32[]{:S(2)}, u32[]{:S(2)}) collective-permute-start(f32[1,32,128]{2,1,0:T(8,128)S(1)} %get-tuple-element.18), channel_id=1, source_target_pairs={{0,31},{1,0},{2,1},{3,2},{4,3},{5,4},{6,5},{7,6},{8,7},{9,8},{10,9... | collective-permute-start | bytes 49160 | tf_op jit(solution)/shard_map/ppermute | solution.py:41
  33.0 3.5 %collective-permute-done.2 = f32[1,32,128]{2,1,0:T(8,128)S(1)} collective-permute-done((f32[1,32,128]{2,1,0:T(8,128)S(1)}, f32[1,32,128]{2,1,0:T(8,128)S(1)}, u32[]{:S(2)}, u32[]{:S(2)}) %collective-permute-start.2) | collective-permute-done | bytes 16416 | tf_op jit(solution)/shard_map/ppermute | solution.py:41
  36.5 1.5 collective-permute-done.3
  38.1 1.1 multiply_add_fusion.1
  39.7 4.0 %copy.108 = f32[32,3,32,128]{2,3,1,0:T(8,128)} copy(f32[32,3,32,128]{3,2,1,0:T(8,128)S(1)} %multiply_add_fusion.2) | data formatting | bytes 3145728 | tf_op jit(solution)/shard_map/add | solution.py:46
  43.6 8.1 %copy.109 = f32[3,8,32,32,16]{2,4,3,1,0:T(8,128)} copy(f32[3,8,32,32,16]{3,4,1,0,2:T(8,128)} %bitcast.61) | data formatting | bytes 3145728 | tf_op jit(solution)/shard_map/transpose | solution.py:177
  51.7 5.5 %copy.110 = f32[24,32,512]{2,1,0:T(8,128)} copy(f32[24,32,512]{1,2,0:T(8,128)} %bitcast.62) | data formatting | bytes 3145728 | tf_op jit(solution)/shard_map/reshape | solution.py:177
  57.3 26.7 %all-to-all-start = ((f32[24,32,512]{2,1,0:T(8,128)}), f32[24,32,512]{2,1,0:T(8,128)S(1)}, u32[]{:S(2)}, u32[]{:S(2)}) async-start(f32[24,32,512]{2,1,0:T(8,128)} %copy.110), calls=%async_computation | async-start | bytes 3145728 | tf_op jit(solution)/shard_map/all_to_all | solution.py:180
  84.1 0.8 copy.115.w_out_ref
  85.1 27.7 %all-to-all-done = f32[24,32,512]{2,1,0:T(8,128)S(1)} async-done(((f32[24,32,512]{2,1,0:T(8,128)}), f32[24,32,512]{2,1,0:T(8,128)S(1)}, u32[]{:S(2)}, u32[]{:S(2)}) %all-to-all-start) | async-done | bytes 1572896 | tf_op jit(solution)/shard_map/all_to_all | solution.py:180
  112.8 4.2 %copy.111 = f32[24,32,512]{1,0,2:T(8,128)} copy(f32[24,32,512]{2,1,0:T(8,128)S(1)} %all-to-all-done) | data formatting | bytes 3145728 | tf_op jit(solution)/shard_map/all_to_all | solution.py:180
  117.0 4.2 %reshape_reshape.3 = f32[768,32,16]{0,2,1:T(8,128)S(1)} reshape(f32[24,32,512]{1,0,2:T(8,128)} %copy.111) | data formatting | bytes 3145728 | tf_op jit(solution)/shard_map/reshape;reshape | solution.py:118
  121.5 4.4 %copy.114 = bf16[768,16,48]{2,1,0:T(8,128)(2,1)} copy(bf16[768,16,48]{0,1,2:T(8,128)(2,1)S(1)} %pad_maximum_fusion.8) | data formatting | bytes 2359296 | tf_op jit(solution)/shard_map/concatenate | solution.py:122
  125.9 5.2 %copy.112 = f32[768,16,32]{2,1,0:T(8,128)} copy(f32[768,16,32]{0,1,2:T(8,128)S(1)} %bitcast.65) | data formatting | bytes 3145728 | tf_op jit(solution)/shard_map/transpose | solution.py:118
  131.1 23.7 %shard_map.109 = f32[12288,32]{1,0:T(8,128)} custom-call(bf16[12288,48]{1,0:T(8,128)(2,1)} %bitcast.68, bf16[48,1024]{1,0:T(8,128)(2,1)} %w_in_ref.1, f32[1,1024]{1,0:T(1,128)} %bitcast.80, bf16[1024,32]{1,0:T(8,128)(2,1)} %copy.115.w_out_ref), custom_call_target="tpu_custom_call" | custom-call | flops 2013265920 | bytes 2752512 | tf_op jit(solution)/shard_map/pallas_call | solution.py:83
  154.8 9.7 %convolution_add_fusion = f32[12288,32]{1,0:T(8,128)} fusion(f32[12288,32]{1,0:T(8,128)} %shard_map.109, f32[12288,32]{1,0:T(8,128)} %bitcast.64, f32[32,32]{1,0:T(8,128)S(1)} %copy-done), kind=kOutput, calls=%fused_computation.1 | convolution fusion | flops 151388160 | bytes 4722688 | tf_op jit(solution)/shard_map/dot_general | solution.py:120
  164.5 4.8 %reshape.145 = f32[768,512]{1,0:T(8,128)S(1)} reshape(f32[12288,32]{1,0:T(8,128)} %convolution_add_fusion) | data formatting | bytes 3145728 | tf_op jit(solution)/shard_map/reshape | solution.py:125
  169.8 1.1 gather_fusion
  171.2 1.0 multiply_reduce_fusion
  173.8 2.1 convolution_reduce_fusion.5
  175.9 2.1 convolution_reduce_fusion.4
  177.9 2.1 convolution_reduce_fusion.3
  180.0 2.1 convolution_reduce_fusion.2
  182.1 2.1 convolution_reduce_fusion.1
  184.2 2.1 convolution_reduce_fusion
  186.3 1.8 reduce_sum.36
  188.1 1.6 bitcast_subtract_fusion
  189.6 3.9 %fusion.6 = f32[768,512]{1,0:T(8,128)S(1)} fusion(f32[768,768]{1,0:T(8,128)S(1)} %add_divide_fusion, f32[768,512]{1,0:T(8,128)S(1)} %bitcast_subtract_fusion), kind=kOutput, calls=%fused_computation.23 | convolution fusion | flops 3624271872 | bytes 5505024 | tf_op jit(solution)/shard_map/dot_general | solution.py:142
  193.5 0.9 fusion.23
  194.4 3.9 %fusion.3 = f32[768,512]{1,0:T(8,128)S(1)} fusion(f32[768,768]{1,0:T(8,128)S(1)} %add_divide_fusion, f32[768,512]{1,0:T(8,128)S(1)} %fusion.6, f32[768,512]{1,0:T(8,128)S(1)} %bitcast_subtract_fusion), kind=kOutput, calls=%fused_computation.20 | convolution fusion | flops 3624665088 | bytes 7077888 | tf_op jit(solution)/shard_map/dot_general | solution.py:142
  198.4 4.3 %add_add_fusion = f32[768,512]{1,0:T(8,128)S(1)} fusion(f32[768,512]{1,0:T(8,128)S(1)} %bitcast_subtract_fusion, f32[768,768]{1,0:T(8,128)S(1)} %add_divide_fusion, f32[768,512]{1,0:T(8,128)S(1)} %fusion.3, f32[512]{0:T(512)S(1)} %bitcast.78, f32[]{:T(128)S(6)} %sqrt.3, f32[512]{0:T(512)S(1)} %broadcast_multiply_fusion.3), kind=kOutput, calls=%fused_computation.16 | convolution fusion | flops 3626631168 | bytes 7081988 | tf_op jit(solution)/shard_map/dot_general | solution.py:142
  202.7 50.4 %all_to_all.10 = f32[24,32,512]{2,1,0:T(8,128)S(1)} all-to-all(f32[24,32,512]{2,1,0:T(8,128)S(1)} %bitcast.69), channel_id=1, replica_groups=mesh['mem'=24,'lon'=32] {'mem'}, dimensions={0} | all-to-all | bytes 3145728 | tf_op jit(solution)/shard_map/all_to_all | solution.py:197
  253.1 3.9 %copy.118 = f32[24,32,512]{1,2,0:T(8,128)} copy(f32[24,32,512]{2,1,0:T(8,128)S(1)} %all_to_all.10) | data formatting | bytes 3145728 | tf_op jit(solution)/shard_map/all_to_all | solution.py:197
  257.0 8.4 %copy.119 = f32[32,3,32,8,16]{2,4,3,1,0:T(8,128)} copy(f32[32,3,32,8,16]{0,4,2,3,1:T(8,128)} %bitcast.63) | data formatting | bytes 3145728 | tf_op jit(solution)/shard_map/transpose | solution.py:199
  265.5 7.9 %fusion.20 = (f32[32,2,32,128]{2,3,1,0:T(8,128)}, f32[32,2,32,128]{2,3,1,0:T(8,128)}) fusion(f32[32,3,32,128]{2,3,1,0:T(8,128)} %bitcast.59), kind=kLoop, calls=%fused_computation.69 | loop fusion | bytes 4194304 | tf_op jit(solution)/shard_map/slice | solution.py:54
  273.4 3.6 %copy.120 = f32[32,2,32,128]{3,2,1,0:T(8,128)} copy(f32[32,2,32,128]{2,3,1,0:T(8,128)} %get-tuple-element.9) | data formatting | bytes 2097152 | tf_op jit(solution)/shard_map/slice | solution.py:54
  277.0 1.9 collective-permute-start.4
  278.9 3.6 %copy.121 = f32[32,2,32,128]{3,2,1,0:T(8,128)} copy(f32[32,2,32,128]{2,3,1,0:T(8,128)} %get-tuple-element.10) | data formatting | bytes 2097152 | tf_op jit(solution)/shard_map/slice | solution.py:55
  282.5 12.1 %collective-permute-start.5 = (f32[32,2,32,128]{3,2,1,0:T(8,128)}, f32[32,2,32,128]{3,2,1,0:T(8,128)}, u32[]{:S(2)}, u32[]{:S(2)}) collective-permute-start(f32[32,2,32,128]{3,2,1,0:T(8,128)} %copy.121), channel_id=1, source_target_pairs={{0,31},{1,0},{2,1},{3,2},{4,3},{5,4},{6,5},{7,6},{8,7},{9,8},{10,9... | collective-permute-start | bytes 3145736 | tf_op jit(solution)/shard_map/ppermute | solution.py:41
  294.6 4.4 %copy.122 = f32[32,3,32,128]{3,2,1,0:T(8,128)S(1)} copy(f32[32,3,32,128]{2,3,1,0:T(8,128)} %bitcast.60) | data formatting | bytes 3145728 | tf_op jit(solution)/shard_map/reshape | solution.py:199
  299.0 24.8 %collective-permute-done.4 = f32[32,2,32,128]{3,2,1,0:T(8,128)S(1)} collective-permute-done((f32[32,2,32,128]{3,2,1,0:T(8,128)}, f32[32,2,32,128]{3,2,1,0:T(8,128)S(1)}, u32[]{:S(2)}, u32[]{:S(2)}) %collective-permute-start.4) | collective-permute-done | bytes 1048608 | tf_op jit(solution)/shard_map/ppermute | solution.py:41
  323.8 5.3 %collective-permute-done.5 = f32[32,2,32,128]{3,2,1,0:T(8,128)} collective-permute-done((f32[32,2,32,128]{3,2,1,0:T(8,128)}, f32[32,2,32,128]{3,2,1,0:T(8,128)}, u32[]{:S(2)}, u32[]{:S(2)}) %collective-permute-start.5) | collective-permute-done | bytes 1048608 | tf_op jit(solution)/shard_map/ppermute | solution.py:41
  329.1 2.1 multiply_add_fusion
  331.2 1.6 add_bitcast_fusion
  (57 shorter events, 2.6 us)
Async XLA Ops:
  0.0 154.8 %copy-start = (f32[32,32]{1,0:T(8,128)S(1)}, f32[32,32]{1,0:T(8,128)}, u32[]{:S(2)}) copy-start(f32[32,32]{1,0:T(8,128)} %param.13) | copy-start | bytes 12292
  0.0 38.1 %copy-start.3 = (f32[32,32,3,128]{3,1,2,0:T(8,128)S(1)}, f32[32,32,3,128]{3,1,2,0:T(8,128)}, u32[]{:S(2)}) copy-start(f32[32,32,3,128]{3,1,2,0:T(8,128)} %param.11) | copy-start | bytes 4718596
  0.0 19.0 %copy-start.4 = (f32[32,3,128]{2,0,1:T(8,128)S(1)}, f32[32,3,128]{2,0,1:T(8,128)}, u32[]{:S(2)}) copy-start(f32[32,3,128]{2,0,1:T(8,128)} %param.12) | copy-start | bytes 147460
  2.0 36.1 %collective-permute-start = (f32[32,2,32,128]{3,2,1,0:T(8,128)S(1)}, f32[32,2,32,128]{3,2,1,0:T(8,128)S(1)}, u32[]{:S(2)}, u32[]{:S(2)}) collective-permute-start(f32[32,2,32,128]{3,2,1,0:T(8,128)S(1)} %get-tuple-element.11), channel_id=1, source_target_pairs={{0,1},{1,2},{2,3},{3,4},{4,5},{5,6},{6,7},{7,8},{8,9},{9,10},{10,1... | collective-permute-start | bytes 3145736 | tf_op jit(solution)/shard_map/ppermute | solution.py:41
  3.9 34.2 %collective-permute-start.1 = (f32[32,2,32,128]{3,2,1,0:T(8,128)S(1)}, f32[32,2,32,128]{3,2,1,0:T(8,128)S(1)}, u32[]{:S(2)}, u32[]{:S(2)}) collective-permute-start(f32[32,2,32,128]{3,2,1,0:T(8,128)S(1)} %get-tuple-element.12), channel_id=1, source_target_pairs={{0,31},{1,0},{2,1},{3,2},{4,3},{5,4},{6,5},{7,6},{8,7},{9,8},{10,9... | collective-permute-start | bytes 3145736 | tf_op jit(solution)/shard_map/ppermute | solution.py:41
  19.0 17.5 %collective-permute-start.2 = (f32[1,32,128]{2,1,0:T(8,128)S(1)}, f32[1,32,128]{2,1,0:T(8,128)S(1)}, u32[]{:S(2)}, u32[]{:S(2)}) collective-permute-start(f32[1,32,128]{2,1,0:T(8,128)S(1)} %get-tuple-element.17), channel_id=1, source_target_pairs={{0,1},{1,2},{2,3},{3,4},{4,5},{5,6},{6,7},{7,8},{8,9},{9,10},{10,1... | collective-permute-start | bytes 49160 | tf_op jit(solution)/shard_map/ppermute | solution.py:41
  20.9 17.1 %collective-permute-start.3 = (f32[1,32,128]{2,1,0:T(8,128)S(1)}, f32[1,32,128]{2,1,0:T(8,128)S(1)}, u32[]{:S(2)}, u32[]{:S(2)}) collective-permute-start(f32[1,32,128]{2,1,0:T(8,128)S(1)} %get-tuple-element.18), channel_id=1, source_target_pairs={{0,31},{1,0},{2,1},{3,2},{4,3},{5,4},{6,5},{7,6},{8,7},{9,8},{10,9... | collective-permute-start | bytes 49160 | tf_op jit(solution)/shard_map/ppermute | solution.py:41
  57.2 26.8 %copy-start.8 = (bf16[1,1,16,16]{3,2,1,0:T(8,128)(2,1)S(1)}, bf16[1,1,16,16]{3,2,1,0:T(8,128)(2,1)}, u32[]{:S(2)}) copy-start(bf16[1,1,16,16]{3,2,1,0:T(8,128)(2,1)} %param.17) | copy-start | bytes 1540
  57.2 26.9 %copy-start.5 = (bf16[1024,32]{0,1:T(8,128)(2,1)S(1)}, bf16[1024,32]{0,1:T(8,128)(2,1)}, u32[]{:S(2)}) copy-start(bf16[1024,32]{0,1:T(8,128)(2,1)} %param.16) | copy-start | bytes 196612
  57.2 27.7 %copy-start.6 = (s32[1,1,256]{2,1,0:T(1,128)S(1)}, s32[1,1,256]{2,1,0:T(1,128)}, u32[]{:S(2)}) copy-start(s32[1,1,256]{2,1,0:T(1,128)} %param.19) | copy-start | bytes 3076
  57.2 27.7 %copy-start.7 = (s32[1,1,256]{2,1,0:T(1,128)S(1)}, s32[1,1,256]{2,1,0:T(1,128)}, u32[]{:S(2)}) copy-start(s32[1,1,256]{2,1,0:T(1,128)} %param.18) | copy-start | bytes 3076
  57.2 27.7 %copy-start.10 = (f32[32]{0:T(128)S(1)}, f32[32]{0:T(128)}, u32[]{:S(2)}) copy-start(f32[32]{0:T(128)} %param.21) | copy-start | bytes 388
  57.3 55.5 %all-to-all-start = ((f32[24,32,512]{2,1,0:T(8,128)}), f32[24,32,512]{2,1,0:T(8,128)S(1)}, u32[]{:S(2)}, u32[]{:S(2)}) async-start(f32[24,32,512]{2,1,0:T(8,128)} %copy.110), calls=%async_computation | async-start | bytes 3145728 | tf_op jit(solution)/shard_map/all_to_all | solution.py:180
  112.8 4.2 %copy-start.2 = (f32[24,32,512]{2,1,0:T(8,128)}, f32[24,32,512]{2,1,0:T(8,128)S(1)}, u32[]{:S(2)}) copy-start(f32[24,32,512]{2,1,0:T(8,128)S(1)} %all-to-all-done) | copy-start | bytes 4718596
  169.8 1.3 copy-start.9
  277.0 46.8 %collective-permute-start.4 = (f32[32,2,32,128]{3,2,1,0:T(8,128)}, f32[32,2,32,128]{3,2,1,0:T(8,128)S(1)}, u32[]{:S(2)}, u32[]{:S(2)}) collective-permute-start(f32[32,2,32,128]{3,2,1,0:T(8,128)} %copy.120), channel_id=1, source_target_pairs={{0,1},{1,2},{2,3},{3,4},{4,5},{5,6},{6,7},{7,8},{8,9},{9,10},{10,1... | collective-permute-start | bytes 3145736 | tf_op jit(solution)/shard_map/ppermute | solution.py:41
  282.5 46.6 %collective-permute-start.5 = (f32[32,2,32,128]{3,2,1,0:T(8,128)}, f32[32,2,32,128]{3,2,1,0:T(8,128)}, u32[]{:S(2)}, u32[]{:S(2)}) collective-permute-start(f32[32,2,32,128]{3,2,1,0:T(8,128)} %copy.121), channel_id=1, source_target_pairs={{0,31},{1,0},{2,1},{3,2},{4,3},{5,4},{6,5},{7,6},{8,7},{9,8},{10,9... | collective-permute-start | bytes 3145736 | tf_op jit(solution)/shard_map/ppermute | solution.py:41
  329.1 3.8 %copy-start.1 = (f32[32,32]{1,0:T(8,128)S(1)}, f32[32,32]{1,0:T(8,128)}, u32[]{:S(2)}) copy-start(f32[32,32]{1,0:T(8,128)} %param.13) | copy-start | bytes 12292

commit v2 on v1

--- a/solution.py
+++ b/solution.py
@@ -49,11 +49,32 @@
     )
 
 
-def two_passes(field, courant_padded):
-    width = field.shape[1]
-    from_left = ring_shift(field[:, width - 2 :], "lon", 1)
-    from_right = ring_shift(field[:, :2], "lon", -1)
-    padded = jnp.concatenate([from_left, field, from_right], axis=1)
+def halo_padded(field, from_left, from_right):
+    return jnp.concatenate([from_left, field, from_right], axis=1)
+
+
+def exchange(field, wind=None):
+    mem_local, width, levels, lat_rows = field.shape
+    to_right = field[:, width - 2 :].reshape(mem_local * 2, levels, lat_rows)
+    to_left = field[:, :2].reshape(mem_local * 2, levels, lat_rows)
+    if wind is not None:
+        to_right = jnp.concatenate([to_right, wind[-1:]], axis=0)
+        to_left = jnp.concatenate([to_left, wind[:1]], axis=0)
+    got_left = ring_shift(to_right, "lon", 1)
+    got_right = ring_shift(to_left, "lon", -1)
+    count = mem_local * 2
+    padded = halo_padded(
+        field,
+        got_left[:count].reshape(mem_local, 2, levels, lat_rows),
+        got_right[:count].reshape(mem_local, 2, levels, lat_rows),
+    )
+    if wind is None:
+        return padded, None
+    return padded, jnp.concatenate([got_left[count:], wind, got_right[count:]], axis=0)
+
+
+def two_passes(padded, courant_padded):
+    width = padded.shape[1] - 4
     first = advect_step(
         padded[:, : width + 2], padded[:, 1 : width + 3], padded[:, 2 : width + 4], courant_padded
     )
@@ -70,33 +91,65 @@
     return result
 
 
-def network_kernel(x_ref, w_in_ref, offset_ref, w_out_ref, out_ref):
-    pre = jnp.dot(x_ref[...], w_in_ref[...], preferred_element_type=jnp.float32)
-    hidden = jnp.tanh(pre + offset_ref[...]).astype(jnp.bfloat16)
-    out_ref[...] = jnp.dot(hidden, w_out_ref[...], preferred_element_type=jnp.float32)
-
-
-def network(net_in, bias_in, bias_offset, bias_out, rows=512):
-    total, nin = net_in.shape
+def network_kernel(x_ref, pred_ref, w_prof_ref, w_pred_ref, offset_ref, w_out_ref, w_phys_ref, out_ref):
+    x = x_ref[...]
+    narrow = x.astype(jnp.bfloat16)
+    extra = pred_ref[...]
+    total = jnp.dot(x, w_phys_ref[...], precision=highest, preferred_element_type=jnp.float32)
+    for part in range(w_prof_ref.shape[0]):
+        pre = jnp.dot(narrow, w_prof_ref[part], preferred_element_type=jnp.float32)
+        pre = pre + jnp.dot(extra, w_pred_ref[part], preferred_element_type=jnp.float32)
+        hidden = jnp.tanh(pre + offset_ref[...]).astype(jnp.bfloat16)
+        total = total + jnp.dot(hidden, w_out_ref[part], preferred_element_type=jnp.float32)
+    out_ref[...] = total
+
+
+def block_diagonal(matrix, parts, dtype):
+    eye = jnp.eye(parts, dtype=dtype)
+    rows, cols = matrix.shape
+    return (eye[:, :, None, None] * matrix.astype(dtype)[None, None]).reshape(parts, parts * rows, cols)
+
+
+def network(packed, predictors, weighting, bias_in, bias_offset, bias_out, levels, rows=256):
+    total_rows, lanes = packed.shape
+    parts = lanes // levels
     hid = bias_in.shape[1]
     channels = bias_out.shape[1]
+    npred = predictors.shape[1]
+    w_prof = block_diagonal(bias_in[:levels], parts, jnp.bfloat16)
+    w_pred = block_diagonal(bias_in[levels:], parts, jnp.bfloat16)
+    out_parts = block_diagonal(bias_out.T, parts, jnp.bfloat16)
+    w_out = jnp.transpose(out_parts.reshape(parts, parts, channels, hid), (0, 3, 1, 2)).reshape(
+        parts, hid, parts * channels
+    )
+    phys_parts = block_diagonal(weighting.T, parts, jnp.float32)
+    w_phys = jnp.transpose(phys_parts, (1, 0, 2)).reshape(parts * levels, parts * channels)
+    column_groups = predictors.shape[0] // parts
+    pred_tiled = jnp.tile(
+        predictors.reshape(column_groups, parts * npred), (rows // column_groups, 1)
+    )
+    const = lambda i: (0, 0)
+    const3 = lambda i: (0, 0, 0)
     return pl.pallas_call(
         network_kernel,
-        out_shape=jax.ShapeDtypeStruct((total, channels), jnp.float32),
-        grid=(total // rows,),
+        out_shape=jax.ShapeDtypeStruct((total_rows, parts * channels), jnp.float32),
+        grid=(total_rows // rows,),
         in_specs=[
-            pl.BlockSpec((rows, nin), lambda i: (i, 0)),
-            pl.BlockSpec((nin, hid), lambda i: (0, 0)),
-            pl.BlockSpec((1, hid), lambda i: (0, 0)),
-            pl.BlockSpec((hid, channels), lambda i: (0, 0)),
+            pl.BlockSpec((rows, lanes), lambda i: (i, 0)),
+            pl.BlockSpec((rows, parts * npred), const),
+            pl.BlockSpec((parts, lanes, hid), const3),
+            pl.BlockSpec((parts, parts * npred, hid), const3),
+            pl.BlockSpec((1, hid), const),
+            pl.BlockSpec((parts, hid, parts * channels), const3),
+            pl.BlockSpec((lanes, parts * channels), const),
         ],
-        out_specs=pl.BlockSpec((rows, channels), lambda i: (i, 0)),
+        out_specs=pl.BlockSpec((rows, parts * channels), lambda i: (i, 0)),
         cost_estimate=pl.CostEstimate(
-            flops=2 * total * hid * (nin + channels),
-            transcendentals=total * hid,
-            bytes_accessed=total * (nin * 2 + channels * 4),
+            flops=2 * total_rows * parts * hid * (lanes + parts * npred + parts * channels),
+            transcendentals=total_rows * parts * hid,
+            bytes_accessed=total_rows * (lanes + parts * channels) * 4,
         ),
-    )(net_in, bias_in, bias_offset.reshape(1, hid), bias_out)
+    )(packed, pred_tiled, w_prof, w_pred, bias_offset.reshape(1, hid), w_out, w_phys)
 
 
 def analyse(
@@ -115,13 +168,8 @@
 ):
     members = flat.shape[0]
     channels = weighting.shape[0]
-    profile = jnp.transpose(flat.reshape(members, levels, columns), (0, 2, 1))
-    rows = profile.reshape(members * columns, levels)
-    phys = jnp.dot(rows, weighting.T, precision=highest)
-    extra = jnp.broadcast_to(predictors[None], (members, columns, predictors.shape[1]))
-    net_in = jnp.concatenate([profile.astype(jnp.bfloat16), extra], axis=2)
-    net_in = net_in.reshape(members * columns, net_in.shape[2])
-    evolved = phys + network(net_in, bias_in, bias_offset, bias_out)
+    packed = flat.reshape(members * columns * levels // 128, 128)
+    evolved = network(packed, predictors, weighting, bias_in, bias_offset, bias_out, levels)
     table = evolved.reshape(members, columns * channels)
     picks = obs_column * channels + obs_channel
     hx = jnp.take(table, picks, axis=1)
@@ -141,11 +189,14 @@
     def multiply(vectors):
         return jnp.dot(mtx, vectors, precision=highest)
 
+    def multiply_fast(vectors):
+        return jnp.dot(mtx, vectors, precision=lax.Precision.HIGH)
+
     drive = jnp.dot(spread_wide, innov, precision=highest)
     mean_weights = apply_root(multiply, apply_root(multiply, drive)) / (scale * root_count)
     xmean = jnp.mean(flat, axis=0)
     pert = flat - xmean
-    spread_part = apply_root(multiply, pert)
+    spread_part = apply_root(multiply_fast, pert)
     shift_part = jnp.dot(mean_weights, pert, precision=highest)
     return xmean + spread_part / jnp.sqrt(scale) + shift_part
 
@@ -169,16 +220,14 @@
     blocks = lat_rows // patch_cols
     field = jnp.transpose(state, (0, 2, 1, 3))
     wind = jnp.transpose(courant, (1, 0, 2))
-    wind_padded = jnp.concatenate(
-        [ring_shift(wind[-1:], "lon", 1), wind, ring_shift(wind[:1], "lon", -1)], axis=0
-    )
-    field = two_passes(field, wind_padded)
+    padded, wind_padded = exchange(field, wind)
+    field = two_passes(padded, wind_padded)
     outgoing = field.reshape(mem_local, lon_local, levels, blocks, patch_cols)
-    outgoing = jnp.transpose(outgoing, (1, 3, 0, 2, 4)).reshape(
-        groups, mem_local, levels * patch_cols
+    outgoing = jnp.transpose(outgoing, (1, 3, 0, 4, 2)).reshape(
+        groups, mem_local, patch_cols * levels
     )
     arrived = lax.all_to_all(outgoing, "mem", split_axis=0, concat_axis=0, tiled=True)
-    flat = arrived.reshape(groups * mem_local, levels * patch_cols)
+    flat = arrived.reshape(groups * mem_local, patch_cols * levels)
     analysed = analyse(
         flat,
         predictors[0, 0],
@@ -193,13 +242,14 @@
         levels,
         patch_cols,
     )
-    returning = analysed.reshape(groups, mem_local, levels * patch_cols)
+    returning = analysed.reshape(groups, mem_local, patch_cols * levels)
     restored = lax.all_to_all(returning, "mem", split_axis=0, concat_axis=0, tiled=True)
-    restored = restored.reshape(lon_local, blocks, mem_local, levels, patch_cols)
-    restored = jnp.transpose(restored, (2, 0, 3, 1, 4)).reshape(
+    restored = restored.reshape(lon_local, blocks, mem_local, patch_cols, levels)
+    restored = jnp.transpose(restored, (2, 0, 4, 1, 3)).reshape(
         mem_local, lon_local, levels, lat_rows
     )
-    field = two_passes(restored, wind_padded)
+    padded, _ = exchange(restored)
+    field = two_passes(padded, wind_padded)
     return jnp.transpose(field, (0, 2, 1, 3))
 
 

time: 338 us -> 295 us (0.87); the launches traced: 333 us -> 295 us
  local copies, waits for them, and re-layouts: 76.9 us -> 45.4 us
  matrix products: 35.8 us -> 20.3 us
  starting transfers between devices: 71.7 us -> 60.3 us
  waiting for transfers between devices: 62.9 us -> 73.2 us
  blocking collectives: 50.4 us -> 54.5 us
    transpose x3 -> x0, local copies, waits for them, and re-layouts: 21.7 us -> none  [the longest x1 8.44 us: shards(): jnp.transpose(restored, (2, 0, 3, 1, 4))]
    ppermute x6 -> x4, waiting for transfers between devices: 35.2 us -> 49.2 us  [ring_shift(): return lax.ppermute(block, axis, pairs)]
    ppermute x6 -> x4, starting transfers between devices: 44.9 us -> 31 us  [ring_shift(): return lax.ppermute(block, axis, pairs)]
    reshape x2 -> x6, local copies, waits for them, and re-layouts: 9.89 us -> 22.1 us  [the longest x2 6.72 us: shards(): jnp.transpose(outgoing, (1, 3, 0, 4, 2))]
    dot_general x9 -> x6, matrix products: 24.5 us -> 12.3 us  [multiply(): return jnp.dot(mtx, vectors, precision=highest)]
    slice x5 -> x11, local copies, waits for them, and re-layouts: 17.1 us -> 9.89 us  [the longest x2 9.72 us: exchange(): to_right = field[:, width - 2:].reshape(mem_local * 2, levels, lat_rows)]
    concatenate x1 -> x0, local copies, waits for them, and re-layouts: 4.41 us -> none  [analyse(): net_in = jnp.concatenate([profile.astype(jnp.bfloat16), extra], axis=2)]
    all_to_all x1 -> x0, local copies, waits for them, and re-layouts: 4.2 us -> none  [shards(): lax.all_to_all(outgoing, 'mem', split_axis=0, concat_axis=0, tiled=True)]
  transfers between devices with their start and end apart: 7 -> 5, of which waited for: 5 -> 5; matrix products, arithmetic and copies ran while one was open for 3% -> 4% of each run, Pallas kernels for 0% -> 0%
where the time goes in v2:
time: 295 us
  waiting for transfers between devices  73.2 us (25%)
  starting transfers between devices  60.3 us (20%)
  blocking collectives  54.5 us (18%)
  local copies, waits for them, and re-layouts  45.4 us (15%)
  Pallas kernels  26.2 us (9%)
  matrix products  20.3 us (7%)
  other arithmetic  13.3 us (5%)
    all_to_all x1, blocking collectives, shards(): lax.all_to_all(returning, 'mem', split_axis=0, concat_axis=0, tiled=True)  54.5 us
    ppermute x4, waiting for transfers between devices, ring_shift(): return lax.ppermute(block, axis, pairs)  49.2 us
    ppermute x4, starting transfers between devices, ring_shift(): return lax.ppermute(block, axis, pairs)  31 us
    all_to_all x1, starting transfers between devices, shards(): lax.all_to_all(outgoing, 'mem', split_axis=0, concat_axis=0, tiled=True)  29.4 us
    pallas_call x1, Pallas kernels, network(): pl.pallas_call(network_kernel, out_shape=jax.ShapeDtypeStruct((total_rows...  26.2 us
    all_to_all x1, waiting for transfers between devices, shards(): lax.all_to_all(outgoing, 'mem', split_axis=0, concat_axis=0, tiled=True)  24 us
    dot_general x6, matrix products, multiply(): return jnp.dot(mtx, vectors, precision=highest)  12.3 us
    slice x2, local copies, waits for them, and re-layouts, exchange(): to_right = field[:, width - 2:].reshape(mem_local * 2, levels, lat_rows)  9.72 us
  transfers between devices with their start and end apart: 5, of which 5 were waited for; matrix products, arithmetic and copies ran while one was open for 4% of the time, Pallas kernels for 0%

profile of v2, /device:TPU:128, one launch (start us, length us, event | category | flops | bytes accessed | tf_op | source)
XLA Modules:
  0.0 294.5 jit_solution(4113776537098702270)
XLA Ops:
  0.0 1.8 fusion.23
  1.9 1.9 collective-permute-start
  3.9 15.1 %collective-permute-start.1 = (f32[65,32,128]{2,1,0:T(8,128)S(1)}, f32[65,32,128]{2,1,0:T(8,128)S(1)}, u32[]{:S(2)}, u32[]{:S(2)}) collective-permute-start(f32[65,32,128]{2,1,0:T(8,128)S(1)} %pad_maximum_fusion.9), channel_id=1, source_target_pairs={{0,31},{1,0},{2,1},{3,2},{4,3},{5,4},{6,5},{7,6},{8,7},{9,8},{10,9... | collective-permute-start | bytes 3194888 | tf_op jit(solution)/shard_map/ppermute | solution.py:41
  19.0 17.4 %collective-permute-done = f32[65,32,128]{2,1,0:T(8,128)S(1)} collective-permute-done((f32[65,32,128]{2,1,0:T(8,128)S(1)}, f32[65,32,128]{2,1,0:T(8,128)S(1)}, u32[]{:S(2)}, u32[]{:S(2)}) %collective-permute-start) | collective-permute-done | bytes 1064992 | tf_op jit(solution)/shard_map/ppermute | solution.py:41
  36.4 1.6 collective-permute-done.1
  38.3 1.3 copy-done.1
  39.6 1.0 multiply_add_fusion.1
  41.1 4.0 %copy.77 = f32[32,3,32,128]{2,3,1,0:T(8,128)} copy(f32[32,3,32,128]{3,2,1,0:T(8,128)S(1)} %multiply_add_fusion.2) | data formatting | bytes 3145728 | tf_op jit(solution)/shard_map/add | solution.py:46
  45.1 4.7 %reshape.199 = f32[24,32,512]{2,0,1:T(8,128)S(1)} reshape(f32[3,8,32,16,32]{4,3,1,0,2:T(8,128)} %bitcast.75) | data formatting | bytes 3145728 | tf_op jit(solution)/shard_map/reshape | solution.py:226
  49.7 2.1 copy.78
  51.8 29.4 %all-to-all-start = ((f32[24,32,512]{2,1,0:T(8,128)}), f32[24,32,512]{2,1,0:T(8,128)S(1)}, u32[]{:S(2)}, u32[]{:S(2)}) async-start(f32[24,32,512]{2,1,0:T(8,128)} %copy.78), calls=%async_computation | async-start | bytes 3145728 | tf_op jit(solution)/shard_map/all_to_all | solution.py:229
  82.1 0.7 copy.80.w_phys_ref
  83.1 0.9 broadcast_multiply_fusion.2.w_pred_ref
  84.0 1.1 broadcast_multiply_fusion.w_out_ref
  85.1 1.1 broadcast_multiply_fusion.1.w_prof_ref
  86.2 24.0 %all-to-all-done = f32[24,32,512]{2,1,0:T(8,128)S(1)} async-done(((f32[24,32,512]{2,1,0:T(8,128)}), f32[24,32,512]{2,1,0:T(8,128)S(1)}, u32[]{:S(2)}, u32[]{:S(2)}) %all-to-all-start) | async-done | bytes 1572896 | tf_op jit(solution)/shard_map/all_to_all | solution.py:229
  110.2 1.3 reshape_reshape.3.x_ref
  111.8 0.6 tile.11
  112.5 26.2 %shard_map.109 = f32[3072,128]{1,0:T(8,128)} custom-call(f32[3072,128]{1,0:T(8,128)} %reshape_reshape.3.x_ref, bf16[256,64]{1,0:T(8,128)(2,1)} %bitcast.92, bf16[4,128,1024]{2,1,0:T(8,128)(2,1)} %broadcast_multiply_fusion.1.w_prof_ref, bf16[4,64,1024]{2,1,0:T(8,128)(2,1)} %broadcast_multiply_fusion.2.w_pred_ref, f32[1,1024]{1,0:T(1,128)} %bitcast.102, ...), custom_call_target="tpu_custom_call" | custom-call | flops 8053063680 | bytes 3145728 | tf_op jit(solution)/shard_map/pallas_call | solution.py:133
  138.6 1.7 reshape.201
  140.8 1.1 gather_fusion
  142.2 1.0 multiply_reduce_fusion
  143.9 0.5 add_divide_fusion
  144.8 2.1 convolution_reduce_fusion.5
  146.9 2.1 convolution_reduce_fusion.4
  148.9 2.1 convolution_reduce_fusion.3
  151.0 2.1 convolution_reduce_fusion.2
  153.1 2.1 convolution_reduce_fusion.1
  155.2 2.1 convolution_reduce_fusion
  157.3 1.8 reduce_sum.36
  159.1 1.6 bitcast_subtract_fusion
  160.6 2.1 fusion.6
  162.7 0.9 fusion.25
  163.6 2.1 fusion.3
  165.7 2.2 add_add_fusion
  167.9 54.5 %all_to_all.10 = f32[24,32,512]{2,1,0:T(8,128)S(1)} all-to-all(f32[24,32,512]{2,1,0:T(8,128)S(1)} %bitcast.84), channel_id=1, replica_groups=mesh['mem'=24,'lon'=32] {'mem'}, dimensions={0} | all-to-all | bytes 3145728 | tf_op jit(solution)/shard_map/all_to_all | solution.py:246
  222.4 0.9 copy.82
  223.3 3.8 %reshape.204 = f32[3,8,32,16,32]{4,3,1,0,2:T(8,128)} reshape(f32[24,32,512]{2,0,1:T(8,128)S(1)} %copy.82) | data formatting | bytes 3145728 | tf_op jit(solution)/shard_map/reshape | solution.py:247
  227.1 7.9 %fusion.22 = (f32[32,2,32,128]{2,3,1,0:T(8,128)}, f32[32,2,32,128]{2,3,1,0:T(8,128)}) fusion(f32[32,3,32,128]{2,3,1,0:T(8,128)} %bitcast.73), kind=kLoop, calls=%fused_computation.75 | loop fusion | bytes 4194304 | tf_op jit(solution)/shard_map/slice | solution.py:58
  235.0 3.6 %copy.83 = f32[64,32,128]{2,1,0:T(8,128)} copy(f32[64,32,128]{1,2,0:T(8,128)} %bitcast.77) | data formatting | bytes 2097152 | tf_op jit(solution)/shard_map/reshape | solution.py:58
  238.6 1.9 collective-permute-start.2
  240.5 3.6 %copy.84 = f32[64,32,128]{2,1,0:T(8,128)} copy(f32[64,32,128]{1,2,0:T(8,128)} %bitcast.76) | data formatting | bytes 2097152 | tf_op jit(solution)/shard_map/reshape | solution.py:59
  244.1 12.1 %collective-permute-start.3 = (f32[64,32,128]{2,1,0:T(8,128)}, f32[64,32,128]{2,1,0:T(8,128)}, u32[]{:S(2)}, u32[]{:S(2)}) collective-permute-start(f32[64,32,128]{2,1,0:T(8,128)} %copy.84), channel_id=1, source_target_pairs={{0,31},{1,0},{2,1},{3,2},{4,3},{5,4},{6,5},{7,6},{8,7},{9,8},{10,9... | collective-permute-start | bytes 3145736 | tf_op jit(solution)/shard_map/ppermute | solution.py:41
  256.2 4.4 %copy.85 = f32[32,3,32,128]{3,2,1,0:T(8,128)S(1)} copy(f32[32,3,32,128]{2,3,1,0:T(8,128)} %bitcast.74) | data formatting | bytes 3145728 | tf_op jit(solution)/shard_map/reshape | solution.py:248
  260.6 24.8 %collective-permute-done.2 = f32[64,32,128]{2,1,0:T(8,128)S(1)} collective-permute-done((f32[64,32,128]{2,1,0:T(8,128)}, f32[64,32,128]{2,1,0:T(8,128)S(1)}, u32[]{:S(2)}, u32[]{:S(2)}) %collective-permute-start.2) | collective-permute-done | bytes 1048608 | tf_op jit(solution)/shard_map/ppermute | solution.py:41
  285.4 5.4 %collective-permute-done.3 = f32[64,32,128]{2,1,0:T(8,128)} collective-permute-done((f32[64,32,128]{2,1,0:T(8,128)}, f32[64,32,128]{2,1,0:T(8,128)}, u32[]{:S(2)}, u32[]{:S(2)}) %collective-permute-start.3) | collective-permute-done | bytes 1048608 | tf_op jit(solution)/shard_map/ppermute | solution.py:41
  290.8 2.1 multiply_add_fusion
  292.9 1.6 add_bitcast_fusion
  (73 shorter events, 3.2 us)
Async XLA Ops:
  0.0 1.8 copy-start.2
  1.9 34.5 %collective-permute-start = (f32[65,32,128]{2,1,0:T(8,128)S(1)}, f32[65,32,128]{2,1,0:T(8,128)S(1)}, u32[]{:S(2)}, u32[]{:S(2)}) collective-permute-start(f32[65,32,128]{2,1,0:T(8,128)S(1)} %pad_maximum_fusion.8), channel_id=1, source_target_pairs={{0,1},{1,2},{2,3},{3,4},{4,5},{5,6},{6,7},{7,8},{8,9},{9,10},{10,1... | collective-permute-start | bytes 3194888 | tf_op jit(solution)/shard_map/ppermute | solution.py:41
  3.9 34.1 %collective-permute-start.1 = (f32[65,32,128]{2,1,0:T(8,128)S(1)}, f32[65,32,128]{2,1,0:T(8,128)S(1)}, u32[]{:S(2)}, u32[]{:S(2)}) collective-permute-start(f32[65,32,128]{2,1,0:T(8,128)S(1)} %pad_maximum_fusion.9), channel_id=1, source_target_pairs={{0,31},{1,0},{2,1},{3,2},{4,3},{5,4},{6,5},{7,6},{8,7},{9,8},{10,9... | collective-permute-start | bytes 3194888 | tf_op jit(solution)/shard_map/ppermute | solution.py:41
  38.2 1.4 copy-start.1
  51.8 29.6 %copy-start.3 = (bf16[1024,32]{0,1:T(8,128)(2,1)S(1)}, bf16[1024,32]{0,1:T(8,128)(2,1)}, u32[]{:S(2)}) copy-start(bf16[1024,32]{0,1:T(8,128)(2,1)} %param.16) | copy-start | bytes 196612
  51.8 30.0 %copy-start.4 = (f32[32,32]{1,0:T(8,128)S(1)}, f32[32,32]{1,0:T(8,128)}, u32[]{:S(2)}) copy-start(f32[32,32]{1,0:T(8,128)} %param.13) | copy-start | bytes 12292
  51.8 31.0 %copy-start.6 = (bf16[1,1,16,16]{3,2,1,0:T(8,128)(2,1)S(1)}, bf16[1,1,16,16]{3,2,1,0:T(8,128)(2,1)}, u32[]{:S(2)}) copy-start(bf16[1,1,16,16]{3,2,1,0:T(8,128)(2,1)} %param.17) | copy-start | bytes 1540
  51.8 31.1 %copy-start.5 = (s32[1,1,256]{2,1,0:T(1,128)S(1)}, s32[1,1,256]{2,1,0:T(1,128)}, u32[]{:S(2)}) copy-start(s32[1,1,256]{2,1,0:T(1,128)} %param.19) | copy-start | bytes 3076
  51.8 31.1 %copy-start.7 = (s32[1,1,256]{2,1,0:T(1,128)S(1)}, s32[1,1,256]{2,1,0:T(1,128)}, u32[]{:S(2)}) copy-start(s32[1,1,256]{2,1,0:T(1,128)} %param.18) | copy-start | bytes 3076
  51.8 31.1 %copy-start.9 = (f32[32]{0:T(128)S(1)}, f32[32]{0:T(128)}, u32[]{:S(2)}) copy-start(f32[32]{0:T(128)} %param.21) | copy-start | bytes 388
  51.8 31.2 %slice-start.1 = ((bf16[48,1024]{1,0:T(8,128)(2,1)}), bf16[16,1024]{1,0:T(8,128)(2,1)S(1)}, s32[]{:S(2)}) async-start(bf16[48,1024]{1,0:T(8,128)(2,1)} %param.14), calls=%async_computation.3 | async-start | bytes 65536 | tf_op jit(solution)/shard_map/slice | solution.py:120
  51.8 58.3 %all-to-all-start = ((f32[24,32,512]{2,1,0:T(8,128)}), f32[24,32,512]{2,1,0:T(8,128)S(1)}, u32[]{:S(2)}, u32[]{:S(2)}) async-start(f32[24,32,512]{2,1,0:T(8,128)} %copy.78), calls=%async_computation | async-start | bytes 3145728 | tf_op jit(solution)/shard_map/all_to_all | solution.py:229
  81.4 3.6 %slice-start = ((bf16[48,1024]{1,0:T(8,128)(2,1)}), bf16[32,1024]{1,0:T(8,128)(2,1)S(1)}, s32[]{:S(2)}) async-start(bf16[48,1024]{1,0:T(8,128)(2,1)} %param.14), calls=%async_computation.2 | async-start | bytes 131072 | tf_op jit(solution)/shard_map/slice | solution.py:119
  110.2 1.7 copy-start
  140.8 1.3 copy-start.8
  238.6 46.8 %collective-permute-start.2 = (f32[64,32,128]{2,1,0:T(8,128)}, f32[64,32,128]{2,1,0:T(8,128)S(1)}, u32[]{:S(2)}, u32[]{:S(2)}) collective-permute-start(f32[64,32,128]{2,1,0:T(8,128)} %copy.83), channel_id=1, source_target_pairs={{0,1},{1,2},{2,3},{3,4},{4,5},{5,6},{6,7},{7,8},{8,9},{9,10},{10,1... | collective-permute-start | bytes 3145736 | tf_op jit(solution)/shard_map/ppermute | solution.py:41
  244.1 46.6 %collective-permute-start.3 = (f32[64,32,128]{2,1,0:T(8,128)}, f32[64,32,128]{2,1,0:T(8,128)}, u32[]{:S(2)}, u32[]{:S(2)}) collective-permute-start(f32[64,32,128]{2,1,0:T(8,128)} %copy.84), channel_id=1, source_target_pairs={{0,31},{1,0},{2,1},{3,2},{4,3},{5,4},{6,5},{7,6},{8,7},{9,8},{10,9... | collective-permute-start | bytes 3145736 | tf_op jit(solution)/shard_map/ppermute | solution.py:41

commit v3 on v2

--- a/solution.py
+++ b/solution.py
@@ -112,6 +112,7 @@
 
 def network(packed, predictors, weighting, bias_in, bias_offset, bias_out, levels, rows=256):
     total_rows, lanes = packed.shape
+    assert total_rows % rows == 0
     parts = lanes // levels
     hid = bias_in.shape[1]
     channels = bias_out.shape[1]
@@ -153,7 +154,7 @@
 
 
 def analyse(
-    flat,
+    flats,
     predictors,
     obs_column,
     obs_channel,
@@ -166,11 +167,15 @@
     levels,
     columns,
 ):
+    channels = weighting.shape[0]
+    tables = []
+    for part in flats:
+        packed = part.reshape(part.shape[0] * columns * levels // 128, 128)
+        evolved = network(packed, predictors, weighting, bias_in, bias_offset, bias_out, levels)
+        tables.append(evolved.reshape(part.shape[0], columns * channels))
+    table = jnp.concatenate(tables, axis=0)
+    flat = jnp.concatenate(flats, axis=0)
     members = flat.shape[0]
-    channels = weighting.shape[0]
-    packed = flat.reshape(members * columns * levels // 128, 128)
-    evolved = network(packed, predictors, weighting, bias_in, bias_offset, bias_out, levels)
-    table = evolved.reshape(members, columns * channels)
     picks = obs_column * channels + obs_channel
     hx = jnp.take(table, picks, axis=1)
     onehot = (obs_channel[:, None] == jnp.arange(channels, dtype=jnp.int32)[None, :]).astype(
@@ -186,19 +191,36 @@
     gram = jnp.dot(spread, spread.T, preferred_element_type=jnp.float32)
     mtx = (jnp.eye(members, dtype=jnp.float32) + gram) / scale
 
-    def multiply(vectors):
-        return jnp.dot(mtx, vectors, precision=highest)
+    def multiply_vector(vector):
+        inner = jnp.sum(spread_wide * vector[:, None], axis=0)
+        return (vector + jnp.sum(spread_wide * inner[None, :], axis=1)) / scale
 
     def multiply_fast(vectors):
         return jnp.dot(mtx, vectors, precision=lax.Precision.HIGH)
 
-    drive = jnp.dot(spread_wide, innov, precision=highest)
-    mean_weights = apply_root(multiply, apply_root(multiply, drive)) / (scale * root_count)
+    drive = jnp.sum(spread_wide * innov[None, :], axis=1)
+    mean_weights = apply_root(multiply_vector, apply_root(multiply_vector, drive)) / (
+        scale * root_count
+    )
     xmean = jnp.mean(flat, axis=0)
     pert = flat - xmean
-    spread_part = apply_root(multiply_fast, pert)
+    root_coefs = chebyshev_root(0.5, 12.0)
+    result = root_coefs[3] * pert
+    for degree in (2, 1):
+        result = multiply_fast(result) + root_coefs[degree] * pert
     shift_part = jnp.dot(mean_weights, pert, precision=highest)
-    return xmean + spread_part / jnp.sqrt(scale) + shift_part
+    root_scale = jnp.sqrt(scale)
+    outs = []
+    start = 0
+    for part in flats:
+        stop = start + part.shape[0]
+        spread_part = (
+            jnp.dot(mtx[start:stop], result, precision=lax.Precision.HIGH)
+            + root_coefs[0] * pert[start:stop]
+        )
+        outs.append(xmean + spread_part / root_scale + shift_part)
+        start = stop
+    return outs
 
 
 def shards(
@@ -218,18 +240,24 @@
     groups = lax.axis_size("mem")
     patch_cols = lon_local * lat_rows // groups
     blocks = lat_rows // patch_cols
+    halves = 2
+    size = mem_local // halves
     field = jnp.transpose(state, (0, 2, 1, 3))
     wind = jnp.transpose(courant, (1, 0, 2))
-    padded, wind_padded = exchange(field, wind)
-    field = two_passes(padded, wind_padded)
-    outgoing = field.reshape(mem_local, lon_local, levels, blocks, patch_cols)
-    outgoing = jnp.transpose(outgoing, (1, 3, 0, 4, 2)).reshape(
-        groups, mem_local, patch_cols * levels
-    )
-    arrived = lax.all_to_all(outgoing, "mem", split_axis=0, concat_axis=0, tiled=True)
-    flat = arrived.reshape(groups * mem_local, patch_cols * levels)
+    chunks = [field[h * size : (h + 1) * size] for h in range(halves)]
+    first_padded, wind_padded = exchange(chunks[0], wind)
+    paddeds = [first_padded] + [exchange(chunk)[0] for chunk in chunks[1:]]
+    flats = []
+    for padded in paddeds:
+        forecast = two_passes(padded, wind_padded)
+        outgoing = forecast.reshape(size, lon_local, levels, blocks, patch_cols)
+        outgoing = jnp.transpose(outgoing, (1, 3, 0, 4, 2)).reshape(
+            groups, size, patch_cols * levels
+        )
+        arrived = lax.all_to_all(outgoing, "mem", split_axis=0, concat_axis=0, tiled=True)
+        flats.append(arrived.reshape(groups * size, patch_cols * levels))
     analysed = analyse(
-        flat,
+        flats,
         predictors[0, 0],
         obs_column[0, 0],
         obs_channel[0, 0],
@@ -242,15 +270,17 @@
         levels,
         patch_cols,
     )
-    returning = analysed.reshape(groups, mem_local, patch_cols * levels)
-    restored = lax.all_to_all(returning, "mem", split_axis=0, concat_axis=0, tiled=True)
-    restored = restored.reshape(lon_local, blocks, mem_local, patch_cols, levels)
-    restored = jnp.transpose(restored, (2, 0, 4, 1, 3)).reshape(
-        mem_local, lon_local, levels, lat_rows
-    )
-    padded, _ = exchange(restored)
-    field = two_passes(padded, wind_padded)
-    return jnp.transpose(field, (0, 2, 1, 3))
+    outs = []
+    for part in analysed:
+        returning = part.reshape(groups, size, patch_cols * levels)
+        restored = lax.all_to_all(returning, "mem", split_axis=0, concat_axis=0, tiled=True)
+        restored = restored.reshape(lon_local, blocks, size, patch_cols, levels)
+        restored = jnp.transpose(restored, (2, 0, 4, 1, 3)).reshape(
+            size, lon_local, levels, lat_rows
+        )
+        padded, _ = exchange(restored)
+        outs.append(two_passes(padded, wind_padded))
+    return jnp.transpose(jnp.concatenate(outs, axis=0), (0, 2, 1, 3))
 
 
 def solution(mesh):

time: 295 us -> 310 us (1.051)
  the two profiles are of different devices: /device:TPU:128 before, /device:TPU:2 now
where the time goes in v3:
time: 310 us; the launch traced here: 309 us
  starting transfers between devices  106 us (34%)
  waiting for transfers between devices  84.7 us (27%)
  local copies, waits for them, and re-layouts  59.3 us (19%)
  Pallas kernels  28.6 us (9%)
  other arithmetic  16.2 us (5%)
  matrix products  13 us (4%)
    ppermute x8, starting transfers between devices, ring_shift(): return lax.ppermute(block, axis, pairs)  64 us
    ppermute x8, waiting for transfers between devices, ring_shift(): return lax.ppermute(block, axis, pairs)  61.8 us
    pallas_call x2, Pallas kernels, network(): pl.pallas_call(network_kernel, out_shape=jax.ShapeDtypeStruct((total_rows...  28.6 us
    all_to_all x2, starting transfers between devices, shards(): lax.all_to_all(outgoing, 'mem', split_axis=0, concat_axis=0, tiled=True)  22.2 us
    all_to_all x2, starting transfers between devices, shards(): lax.all_to_all(returning, 'mem', split_axis=0, concat_axis=0, tiled=True)  19.6 us
    all_to_all x2, waiting for transfers between devices, shards(): lax.all_to_all(returning, 'mem', split_axis=0, concat_axis=0, tiled=True)  12.7 us
    all_to_all x2, waiting for transfers between devices, shards(): lax.all_to_all(outgoing, 'mem', split_axis=0, concat_axis=0, tiled=True)  10.2 us
    slice x3, local copies, waits for them, and re-layouts, exchange(): to_right = field[:, width - 2:].reshape(mem_local * 2, levels, lat_rows)  8.9 us
  transfers between devices with their start and end apart: 12, of which 7 were waited for; matrix products, arithmetic and copies ran while one was open for 17% of the time, Pallas kernels for 5%

profile of v3, /device:TPU:2, one launch (start us, length us, event | category | flops | bytes accessed | tf_op | source)
XLA Modules:
  0.0 308.9 jit_solution(14072470491051614790)
XLA Ops:
  0.7 1.7 fusion.41
  2.5 17.6 %collective-permute-start.1 = (f32[33,32,128]{2,1,0:T(8,128)S(1)}, f32[33,32,128]{2,1,0:T(8,128)S(1)}, u32[]{:S(2)}, u32[]{:S(2)}) collective-permute-start(f32[33,32,128]{2,1,0:T(8,128)S(1)} %pad_maximum_fusion.18), channel_id=1, source_target_pairs={{0,31},{1,0},{2,1},{3,2},{4,3},{5,4},{6,5},{7,6},{8,7},{9,8},{10,9... | collective-permute-start | bytes 1622024 | tf_op jit(solution)/shard_map/ppermute | solution.py:41
  20.2 1.9 collective-permute-start
  22.1 12.1 %collective-permute-start.3 = (f32[32,32,128]{2,1,0:T(8,128)S(1)}, f32[32,32,128]{2,1,0:T(8,128)S(1)}, u32[]{:S(2)}, u32[]{:S(2)}) collective-permute-start(f32[32,32,128]{2,1,0:T(8,128)S(1)} %bitcast.101), channel_id=1, source_target_pairs={{0,31},{1,0},{2,1},{3,2},{4,3},{5,4},{6,5},{7,6},{8,7},{9,8},{10,9... | collective-permute-start | bytes 1572872 | tf_op jit(solution)/shard_map/ppermute | solution.py:41
  34.2 1.9 collective-permute-start.2
  36.3 12.7 %collective-permute-done.1 = f32[33,32,128]{2,1,0:T(8,128)S(1)} collective-permute-done((f32[33,32,128]{2,1,0:T(8,128)S(1)}, f32[33,32,128]{2,1,0:T(8,128)S(1)}, u32[]{:S(2)}, u32[]{:S(2)}) %collective-permute-start.1) | collective-permute-done | bytes 540704 | tf_op jit(solution)/shard_map/ppermute | solution.py:41
  49.1 14.5 %collective-permute-done = f32[33,32,128]{2,1,0:T(8,128)S(1)} collective-permute-done((f32[33,32,128]{2,1,0:T(8,128)S(1)}, f32[33,32,128]{2,1,0:T(8,128)S(1)}, u32[]{:S(2)}, u32[]{:S(2)}) %collective-permute-start) | collective-permute-done | bytes 540704 | tf_op jit(solution)/shard_map/ppermute | solution.py:41
  63.7 10.3 %collective-permute-done.2 = f32[32,32,128]{2,1,0:T(8,128)S(1)} collective-permute-done((f32[32,32,128]{2,1,0:T(8,128)S(1)}, f32[32,32,128]{2,1,0:T(8,128)S(1)}, u32[]{:S(2)}, u32[]{:S(2)}) %collective-permute-start.2) | collective-permute-done | bytes 524320 | tf_op jit(solution)/shard_map/ppermute | solution.py:41
  75.1 1.6 multiply_add_fusion.8
  76.7 2.0 copy.118
  78.6 2.1 reshape.333
  80.7 2.5 copy.119
  83.3 13.2 %all-to-all-start = ((f32[24,16,512]{2,1,0:T(8,128)}), f32[24,16,512]{2,1,0:T(8,128)S(1)}, u32[]{:S(2)}, u32[]{:S(2)}) async-start(f32[24,16,512]{2,1,0:T(8,128)} %copy.119), calls=%async_computation | async-start | bytes 1572864 | tf_op jit(solution)/shard_map/all_to_all | solution.py:257
  96.5 2.2 copy.120
  98.8 2.7 reshape.339
  102.8 10.2 %all-to-all-done = f32[24,16,512]{2,1,0:T(8,128)S(1)} async-done(((f32[24,16,512]{2,1,0:T(8,128)}), f32[24,16,512]{2,1,0:T(8,128)S(1)}, u32[]{:S(2)}, u32[]{:S(2)}) %all-to-all-start) | async-done | bytes 786464 | tf_op jit(solution)/shard_map/all_to_all | solution.py:257
  113.1 8.9 %all-to-all-start.1 = ((f32[24,16,512]{2,1,0:T(8,128)}), f32[24,16,512]{2,1,0:T(8,128)S(1)}, u32[]{:S(2)}, u32[]{:S(2)}) async-start(f32[24,16,512]{2,1,0:T(8,128)} %copy.121), calls=%async_computation.1 | async-start | bytes 1572864 | tf_op jit(solution)/shard_map/all_to_all | solution.py:257
  128.5 14.3 %shard_map.109 = f32[1536,128]{1,0:T(8,128)} custom-call(f32[1536,128]{1,0:T(8,128)} %reshape_reshape.6.x_ref, bf16[256,64]{1,0:T(8,128)(2,1)} %bitcast.105, bf16[4,128,1024]{2,1,0:T(8,128)(2,1)} %broadcast_multiply_fusion.1.w_prof_ref, bf16[4,64,1024]{2,1,0:T(8,128)(2,1)} %broadcast_multiply_fusion.2.w_pred_ref, f32[1,1024]{1,0:T(1,128)} %bitcast.116, ...), custom_call_target="tpu_custom_call" | custom-call | flops 4026531840 | bytes 1572864 | tf_op jit(solution)/shard_map/pallas_call | solution.py:134
  146.3 14.3 %shard_map.110 = f32[1536,128]{1,0:T(8,128)} custom-call(f32[1536,128]{1,0:T(8,128)} %reshape_reshape.7.x_ref, bf16[256,64]{1,0:T(8,128)(2,1)} %bitcast.106, bf16[4,128,1024]{2,1,0:T(8,128)(2,1)} %broadcast_multiply_fusion.1.w_prof_ref, bf16[4,64,1024]{2,1,0:T(8,128)(2,1)} %broadcast_multiply_fusion.2.w_pred_ref, f32[1,1024]{1,0:T(1,128)} %bitcast.117, ...), custom_call_target="tpu_custom_call" | custom-call | flops 4026531840 | bytes 1572864 | tf_op jit(solution)/shard_map/pallas_call | solution.py:134
  163.0 1.5 pad_maximum_fusion
  164.5 2.0 gather_fusion
  166.5 1.4 select_reduce_fusion
  169.8 1.9 add_divide_fusion
  175.3 2.1 fusion.5
  177.4 2.1 multiply_add_fusion
  179.5 2.2 fusion.9
  181.7 10.6 %all-to-all-start.2 = ((f32[24,16,512]{2,1,0:T(8,128)}), f32[24,16,512]{2,1,0:T(8,128)S(1)}, u32[]{:S(2)}, u32[]{:S(2)}) async-start(f32[24,16,512]{2,1,0:T(8,128)} %bitcast.30), calls=%async_computation.2 | async-start | bytes 1572864 | tf_op jit(solution)/shard_map/all_to_all | solution.py:276
  192.3 3.8 %fusion.12 = f32[384,512]{1,0:T(8,128)} fusion(f32[768,512]{1,0:T(8,128)} %copy-done.5, f32[768,768]{1,0:T(8,128)} %add_divide_fusion, f32[768,512]{1,0:T(8,128)S(1)} %maximum_subtract_fusion, f32[512]{0:T(512)S(1)} %bitcast.114, f32[]{:T(128)S(6)} %sqrt.3, f32[512]{0:T(512)S(1)} %add_multiply_fusion), kind=kOutput, calls=%fused_computation.53 | convolution fusion | flops 906952704 | bytes 4329476 | tf_op jit(solution)/shard_map/dot_general | solution.py:218
  196.2 12.7 %all-to-all-done.2 = f32[24,16,512]{2,1,0:T(8,128)S(1)} async-done(((f32[24,16,512]{2,1,0:T(8,128)}), f32[24,16,512]{2,1,0:T(8,128)S(1)}, u32[]{:S(2)}, u32[]{:S(2)}) %all-to-all-start.2) | async-done | bytes 786464 | tf_op jit(solution)/shard_map/all_to_all | solution.py:276
  208.9 9.0 %all-to-all-start.3 = ((f32[24,16,512]{2,1,0:T(8,128)}), f32[24,16,512]{2,1,0:T(8,128)}, u32[]{:S(2)}, u32[]{:S(2)}) async-start(f32[24,16,512]{2,1,0:T(8,128)} %bitcast.38), calls=%async_computation.3 | async-start | bytes 1572864 | tf_op jit(solution)/shard_map/all_to_all | solution.py:276
  219.2 1.9 reshape.346
  221.0 2.4 fusion.38
  223.5 3.0 copy.128
  226.4 3.0 copy.129
  229.5 14.5 %collective-permute-start.5 = (f32[32,32,128]{2,1,0:T(8,128)}, f32[32,32,128]{2,1,0:T(8,128)}, u32[]{:S(2)}, u32[]{:S(2)}) collective-permute-start(f32[32,32,128]{2,1,0:T(8,128)} %copy.129), channel_id=1, source_target_pairs={{0,31},{1,0},{2,1},{3,2},{4,3},{5,4},{6,5},{7,6},{8,7},{9,8},{10,9... | collective-permute-start | bytes 1572872 | tf_op jit(solution)/shard_map/ppermute | solution.py:41
  244.0 1.9 collective-permute-start.4
  245.9 2.5 copy.133
  248.4 3.1 %reshape.353 = f32[3,8,16,16,32]{4,3,1,0,2:T(8,128)} reshape(f32[24,16,512]{2,0,1:T(8,128)} %copy.133) | data formatting | bytes 1572864 | tf_op jit(solution)/shard_map/reshape | solution.py:277
  251.5 4.8 %fusion.39 = (f32[16,2,32,128]{2,3,1,0:T(8,128)}, f32[16,2,32,128]{2,3,1,0:T(8,128)}) fusion(f32[16,3,32,128]{2,3,1,0:T(8,128)} %bitcast.79), kind=kLoop, calls=%fused_computation.116 | loop fusion | bytes 2097152 | tf_op jit(solution)/shard_map/slice | solution.py:58
  256.3 3.0 copy.134
  259.3 3.0 copy.135
  262.2 12.1 %collective-permute-start.7 = (f32[32,32,128]{2,1,0:T(8,128)}, f32[32,32,128]{2,1,0:T(8,128)}, u32[]{:S(2)}, u32[]{:S(2)}) collective-permute-start(f32[32,32,128]{2,1,0:T(8,128)} %copy.135), channel_id=1, source_target_pairs={{0,31},{1,0},{2,1},{3,2},{4,3},{5,4},{6,5},{7,6},{8,7},{9,8},{10,9... | collective-permute-start | bytes 1572872 | tf_op jit(solution)/shard_map/ppermute | solution.py:41
  274.3 1.9 collective-permute-start.6
  276.2 1.9 copy.130
  278.1 2.4 copy.136
  280.5 11.8 %collective-permute-done.7 = f32[32,32,128]{2,1,0:T(8,128)} collective-permute-done((f32[32,32,128]{2,1,0:T(8,128)}, f32[32,32,128]{2,1,0:T(8,128)}, u32[]{:S(2)}, u32[]{:S(2)}) %collective-permute-start.7) | collective-permute-done | bytes 524320 | tf_op jit(solution)/shard_map/ppermute | solution.py:41
  292.3 12.4 %collective-permute-done.6 = f32[32,32,128]{2,1,0:T(8,128)} collective-permute-done((f32[32,32,128]{2,1,0:T(8,128)}, f32[32,32,128]{2,1,0:T(8,128)}, u32[]{:S(2)}, u32[]{:S(2)}) %collective-permute-start.6) | collective-permute-done | bytes 524320 | tf_op jit(solution)/shard_map/ppermute | solution.py:41
  304.8 2.4 multiply_add_fusion.2
  (111 shorter events, 23.5 us)
Async XLA Ops:
  2.5 33.7 %copy-start.6 = (f32[32,3,128]{2,0,1:T(8,128)S(1)}, f32[32,3,128]{2,0,1:T(8,128)}, u32[]{:S(2)}) copy-start(f32[32,3,128]{2,0,1:T(8,128)} %param.12) | copy-start | bytes 147460
  2.5 33.7 %copy-start.1 = (f32[32,32,3,128]{3,1,2,0:T(8,128)S(1)}, f32[32,32,3,128]{3,1,2,0:T(8,128)}, u32[]{:S(2)}) copy-start(f32[32,32,3,128]{3,1,2,0:T(8,128)} %param.11) | copy-start | bytes 4718596
  2.5 46.5 %collective-permute-start.1 = (f32[33,32,128]{2,1,0:T(8,128)S(1)}, f32[33,32,128]{2,1,0:T(8,128)S(1)}, u32[]{:S(2)}, u32[]{:S(2)}) collective-permute-start(f32[33,32,128]{2,1,0:T(8,128)S(1)} %pad_maximum_fusion.18), channel_id=1, source_target_pairs={{0,31},{1,0},{2,1},{3,2},{4,3},{5,4},{6,5},{7,6},{8,7},{9,8},{10,9... | collective-permute-start | bytes 1622024 | tf_op jit(solution)/shard_map/ppermute | solution.py:41
  20.2 43.4 %collective-permute-start = (f32[33,32,128]{2,1,0:T(8,128)S(1)}, f32[33,32,128]{2,1,0:T(8,128)S(1)}, u32[]{:S(2)}, u32[]{:S(2)}) collective-permute-start(f32[33,32,128]{2,1,0:T(8,128)S(1)} %pad_maximum_fusion.17), channel_id=1, source_target_pairs={{0,1},{1,2},{2,3},{3,4},{4,5},{5,6},{6,7},{7,8},{8,9},{9,10},{10,1... | collective-permute-start | bytes 1622024 | tf_op jit(solution)/shard_map/ppermute | solution.py:41
  22.1 41.5 %collective-permute-start.3 = (f32[32,32,128]{2,1,0:T(8,128)S(1)}, f32[32,32,128]{2,1,0:T(8,128)S(1)}, u32[]{:S(2)}, u32[]{:S(2)}) collective-permute-start(f32[32,32,128]{2,1,0:T(8,128)S(1)} %bitcast.101), channel_id=1, source_target_pairs={{0,31},{1,0},{2,1},{3,2},{4,3},{5,4},{6,5},{7,6},{8,7},{9,8},{10,9... | collective-permute-start | bytes 1572872 | tf_op jit(solution)/shard_map/ppermute | solution.py:41
  34.2 39.8 %collective-permute-start.2 = (f32[32,32,128]{2,1,0:T(8,128)S(1)}, f32[32,32,128]{2,1,0:T(8,128)S(1)}, u32[]{:S(2)}, u32[]{:S(2)}) collective-permute-start(f32[32,32,128]{2,1,0:T(8,128)S(1)} %bitcast.100), channel_id=1, source_target_pairs={{0,1},{1,2},{2,3},{3,4},{4,5},{5,6},{6,7},{7,8},{8,9},{9,10},{10,1... | collective-permute-start | bytes 1572872 | tf_op jit(solution)/shard_map/ppermute | solution.py:41
  80.7 15.8 %copy-start.4 = (f32[16,3,32,128]{3,2,1,0:T(8,128)S(1)}, f32[16,3,32,128]{3,2,1,0:T(8,128)}, u32[]{:S(2)}) copy-start(f32[16,3,32,128]{3,2,1,0:T(8,128)} %get-tuple-element.28) | copy-start | bytes 2359300
  83.3 29.8 %all-to-all-start = ((f32[24,16,512]{2,1,0:T(8,128)}), f32[24,16,512]{2,1,0:T(8,128)S(1)}, u32[]{:S(2)}, u32[]{:S(2)}) async-start(f32[24,16,512]{2,1,0:T(8,128)} %copy.119), calls=%async_computation | async-start | bytes 1572864 | tf_op jit(solution)/shard_map/all_to_all | solution.py:257
  101.4 20.6 %copy-start.10 = (bf16[1,1,16,16]{3,2,1,0:T(8,128)(2,1)S(1)}, bf16[1,1,16,16]{3,2,1,0:T(8,128)(2,1)}, u32[]{:S(2)}) copy-start(bf16[1,1,16,16]{3,2,1,0:T(8,128)(2,1)} %param.17) | copy-start | bytes 1540
  101.4 21.2 %copy-start.8 = (f32[32,32]{1,0:T(8,128)S(1)}, f32[32,32]{1,0:T(8,128)}, u32[]{:S(2)}) copy-start(f32[32,32]{1,0:T(8,128)} %param.13) | copy-start | bytes 12292
  102.8 20.6 %copy-start.7 = (bf16[1024,32]{0,1:T(8,128)(2,1)S(1)}, bf16[1024,32]{0,1:T(8,128)(2,1)}, u32[]{:S(2)}) copy-start(bf16[1024,32]{0,1:T(8,128)(2,1)} %param.16) | copy-start | bytes 196612
  102.8 20.8 %copy-start.9 = (s32[1,1,256]{2,1,0:T(1,128)S(1)}, s32[1,1,256]{2,1,0:T(1,128)}, u32[]{:S(2)}) copy-start(s32[1,1,256]{2,1,0:T(1,128)} %param.19) | copy-start | bytes 3076
  102.8 20.8 %copy-start.11 = (s32[1,1,256]{2,1,0:T(1,128)S(1)}, s32[1,1,256]{2,1,0:T(1,128)}, u32[]{:S(2)}) copy-start(s32[1,1,256]{2,1,0:T(1,128)} %param.18) | copy-start | bytes 3076
  102.8 20.9 %copy-start.13 = (f32[32]{0:T(128)S(1)}, f32[32]{0:T(128)}, u32[]{:S(2)}) copy-start(f32[32]{0:T(128)} %param.21) | copy-start | bytes 388
  102.8 21.0 %slice-start = ((bf16[48,1024]{1,0:T(8,128)(2,1)}), bf16[16,1024]{1,0:T(8,128)(2,1)S(1)}, s32[]{:S(2)}) async-start(bf16[48,1024]{1,0:T(8,128)(2,1)} %param.14), calls=%async_computation.4 | async-start | bytes 65536 | tf_op jit(solution)/shard_map/slice | solution.py:121
  113.1 32.2 %all-to-all-start.1 = ((f32[24,16,512]{2,1,0:T(8,128)}), f32[24,16,512]{2,1,0:T(8,128)S(1)}, u32[]{:S(2)}, u32[]{:S(2)}) async-start(f32[24,16,512]{2,1,0:T(8,128)} %copy.121), calls=%async_computation.1 | async-start | bytes 1572864 | tf_op jit(solution)/shard_map/all_to_all | solution.py:257
  123.5 2.4 slice-start.1
  164.5 3.4 %copy-start.12 = (f32[1,1,256]{2,1,0:T(1,128)S(1)}, f32[1,1,256]{2,1,0:T(1,128)}, u32[]{:S(2)}) copy-start(f32[1,1,256]{2,1,0:T(1,128)} %param.20) | copy-start | bytes 3076
  166.4 1.4 copy-start.2
  173.6 1.7 copy-start
  179.5 2.2 copy-start.5
  181.7 27.2 %all-to-all-start.2 = ((f32[24,16,512]{2,1,0:T(8,128)}), f32[24,16,512]{2,1,0:T(8,128)S(1)}, u32[]{:S(2)}, u32[]{:S(2)}) async-start(f32[24,16,512]{2,1,0:T(8,128)} %bitcast.30), calls=%async_computation.2 | async-start | bytes 1572864 | tf_op jit(solution)/shard_map/all_to_all | solution.py:276
  208.9 37.1 %all-to-all-start.3 = ((f32[24,16,512]{2,1,0:T(8,128)}), f32[24,16,512]{2,1,0:T(8,128)}, u32[]{:S(2)}, u32[]{:S(2)}) async-start(f32[24,16,512]{2,1,0:T(8,128)} %bitcast.38), calls=%async_computation.3 | async-start | bytes 1572864 | tf_op jit(solution)/shard_map/all_to_all | solution.py:276
  229.5 51.0 %collective-permute-start.5 = (f32[32,32,128]{2,1,0:T(8,128)}, f32[32,32,128]{2,1,0:T(8,128)}, u32[]{:S(2)}, u32[]{:S(2)}) collective-permute-start(f32[32,32,128]{2,1,0:T(8,128)} %copy.129), channel_id=1, source_target_pairs={{0,31},{1,0},{2,1},{3,2},{4,3},{5,4},{6,5},{7,6},{8,7},{9,8},{10,9... | collective-permute-start | bytes 1572872 | tf_op jit(solution)/shard_map/ppermute | solution.py:41
  244.0 36.5 %collective-permute-start.4 = (f32[32,32,128]{2,1,0:T(8,128)}, f32[32,32,128]{2,1,0:T(8,128)}, u32[]{:S(2)}, u32[]{:S(2)}) collective-permute-start(f32[32,32,128]{2,1,0:T(8,128)} %copy.128), channel_id=1, source_target_pairs={{0,1},{1,2},{2,3},{3,4},{4,5},{5,6},{6,7},{7,8},{8,9},{9,10},{10,1... | collective-permute-start | bytes 1572872 | tf_op jit(solution)/shard_map/ppermute | solution.py:41
  262.2 30.1 %collective-permute-start.7 = (f32[32,32,128]{2,1,0:T(8,128)}, f32[32,32,128]{2,1,0:T(8,128)}, u32[]{:S(2)}, u32[]{:S(2)}) collective-permute-start(f32[32,32,128]{2,1,0:T(8,128)} %copy.135), channel_id=1, source_target_pairs={{0,31},{1,0},{2,1},{3,2},{4,3},{5,4},{6,5},{7,6},{8,7},{9,8},{10,9... | collective-permute-start | bytes 1572872 | tf_op jit(solution)/shard_map/ppermute | solution.py:41
  274.3 30.5 %collective-permute-start.6 = (f32[32,32,128]{2,1,0:T(8,128)}, f32[32,32,128]{2,1,0:T(8,128)}, u32[]{:S(2)}, u32[]{:S(2)}) collective-permute-start(f32[32,32,128]{2,1,0:T(8,128)} %copy.134), channel_id=1, source_target_pairs={{0,1},{1,2},{2,3},{3,4},{4,5},{5,6},{6,7},{7,8},{8,9},{9,10},{10,1... | collective-permute-start | bytes 1572872 | tf_op jit(solution)/shard_map/ppermute | solution.py:41
  278.1 26.7 %copy-start.3 = (f32[16,3,32,128]{3,2,1,0:T(8,128)S(1)}, f32[16,3,32,128]{3,2,1,0:T(8,128)}, u32[]{:S(2)}) copy-start(f32[16,3,32,128]{3,2,1,0:T(8,128)} %copy.130) | copy-start | bytes 2359300

commit v4 on v2

--- a/solution.py
+++ b/solution.py
@@ -5,6 +5,7 @@
 import jax.numpy as jnp
 from jax import lax
 from jax.experimental import pallas as pl
+from jax.experimental.layout import Layout, with_layout_constraint
 from jax.experimental.pallas import tpu as pltpu
 from jax.sharding import PartitionSpec as P
 
@@ -112,6 +113,7 @@
 
 def network(packed, predictors, weighting, bias_in, bias_offset, bias_out, levels, rows=256):
     total_rows, lanes = packed.shape
+    assert total_rows % rows == 0
     parts = lanes // levels
     hid = bias_in.shape[1]
     channels = bias_out.shape[1]
@@ -186,14 +188,17 @@
     gram = jnp.dot(spread, spread.T, preferred_element_type=jnp.float32)
     mtx = (jnp.eye(members, dtype=jnp.float32) + gram) / scale
 
-    def multiply(vectors):
-        return jnp.dot(mtx, vectors, precision=highest)
+    def multiply_vector(vector):
+        inner = jnp.sum(spread_wide * vector[:, None], axis=0)
+        return (vector + jnp.sum(spread_wide * inner[None, :], axis=1)) / scale
 
     def multiply_fast(vectors):
         return jnp.dot(mtx, vectors, precision=lax.Precision.HIGH)
 
     drive = jnp.dot(spread_wide, innov, precision=highest)
-    mean_weights = apply_root(multiply, apply_root(multiply, drive)) / (scale * root_count)
+    mean_weights = apply_root(multiply_vector, apply_root(multiply_vector, drive)) / (
+        scale * root_count
+    )
     xmean = jnp.mean(flat, axis=0)
     pert = flat - xmean
     spread_part = apply_root(multiply_fast, pert)
@@ -248,6 +253,7 @@
     restored = jnp.transpose(restored, (2, 0, 4, 1, 3)).reshape(
         mem_local, lon_local, levels, lat_rows
     )
+    restored = with_layout_constraint(restored, Layout((0, 1, 2, 3)))
     padded, _ = exchange(restored)
     field = two_passes(padded, wind_padded)
     return jnp.transpose(field, (0, 2, 1, 3))

time: 295 us -> 287 us (0.973)
  the two profiles are of different devices: /device:TPU:128 before, /device:TPU:512 now
where the time goes in v4:
time: 287 us
  waiting for transfers between devices  102 us (36%)
  starting transfers between devices  56.9 us (20%)
  local copies, waits for them, and re-layouts  39.5 us (14%)
  blocking collectives  38.8 us (14%)
  Pallas kernels  26.2 us (9%)
  other arithmetic  12.3 us (4%)
  matrix products  9.41 us (3%)
    ppermute x4, waiting for transfers between devices, ring_shift(): return lax.ppermute(block, axis, pairs)  78.5 us
    all_to_all x1, blocking collectives, shards(): lax.all_to_all(returning, 'mem', split_axis=0, concat_axis=0, tiled=True)  38.8 us
    ppermute x4, starting transfers between devices, ring_shift(): return lax.ppermute(block, axis, pairs)  34.6 us
    pallas_call x1, Pallas kernels, network(): pl.pallas_call(network_kernel, out_shape=jax.ShapeDtypeStruct((total_rows...  26.2 us
    all_to_all x1, waiting for transfers between devices, shards(): lax.all_to_all(outgoing, 'mem', split_axis=0, concat_axis=0, tiled=True)  23.7 us
    all_to_all x1, starting transfers between devices, shards(): lax.all_to_all(outgoing, 'mem', split_axis=0, concat_axis=0, tiled=True)  22.3 us
    reshape x2, local copies, waits for them, and re-layouts, shards(): jnp.transpose(outgoing, (1, 3, 0, 4, 2))  6.72 us
    transpose x1, local copies, waits for them, and re-layouts, shards(): jnp.transpose(restored, (2, 0, 4, 1, 3))  6.39 us
  transfers between devices with their start and end apart: 5, of which 5 were waited for; matrix products, arithmetic and copies ran while one was open for 2% of the time, Pallas kernels for 0%

profile of v4, /device:TPU:512, one launch (start us, length us, event | category | flops | bytes accessed | tf_op | source)
XLA Modules:
  0.0 286.7 jit_solution(14174901725646423445)
XLA Ops:
  0.0 0.7 fusion.37
  0.7 1.8 fusion.36
  2.6 2.1 collective-permute-start.1
  4.8 2.4 collective-permute-start
  7.2 21.5 %collective-permute-done.1 = f32[65,32,128]{2,1,0:T(8,128)S(1)} collective-permute-done((f32[65,32,128]{2,1,0:T(8,128)S(1)}, f32[65,32,128]{2,1,0:T(8,128)S(1)}, u32[]{:S(2)}, u32[]{:S(2)}) %collective-permute-start.1) | collective-permute-done | bytes 1064992 | tf_op jit(solution)/shard_map/ppermute | solution.py:42
  28.7 12.5 %collective-permute-done = f32[65,32,128]{2,1,0:T(8,128)S(1)} collective-permute-done((f32[65,32,128]{2,1,0:T(8,128)S(1)}, f32[65,32,128]{2,1,0:T(8,128)S(1)}, u32[]{:S(2)}, u32[]{:S(2)}) %collective-permute-start) | collective-permute-done | bytes 1064992 | tf_op jit(solution)/shard_map/ppermute | solution.py:42
  41.4 1.3 copy-done.3
  42.7 1.0 multiply_add_fusion.1
  43.8 0.5 multiply_add_fusion.2
  44.2 4.0 %copy.23 = f32[32,3,32,128]{2,3,1,0:T(8,128)} copy(f32[32,3,32,128]{3,2,1,0:T(8,128)S(1)} %multiply_add_fusion.2) | data formatting | bytes 3145728 | tf_op jit(solution)/shard_map/add | solution.py:47
  48.2 4.7 %reshape.234 = f32[24,32,512]{2,0,1:T(8,128)S(1)} reshape(f32[3,8,32,16,32]{4,3,1,0,2:T(8,128)} %bitcast.72) | data formatting | bytes 3145728 | tf_op jit(solution)/shard_map/reshape | solution.py:231
  52.9 2.1 copy.30
  55.0 22.3 %all-to-all-start = ((f32[24,32,512]{2,1,0:T(8,128)}), f32[24,32,512]{2,1,0:T(8,128)S(1)}, u32[]{:S(2)}, u32[]{:S(2)}) async-start(f32[24,32,512]{2,1,0:T(8,128)} %copy.30), calls=%async_computation | async-start | bytes 3145728 | tf_op jit(solution)/shard_map/all_to_all | solution.py:234
  78.0 0.7 copy.26.w_phys_ref
  79.1 0.9 broadcast_multiply_fusion.2.w_pred_ref
  80.0 1.1 broadcast_multiply_fusion.w_out_ref
  81.1 1.1 broadcast_multiply_fusion.1.w_prof_ref
  82.2 23.7 %all-to-all-done = f32[24,32,512]{2,1,0:T(8,128)S(1)} async-done(((f32[24,32,512]{2,1,0:T(8,128)}), f32[24,32,512]{2,1,0:T(8,128)S(1)}, u32[]{:S(2)}, u32[]{:S(2)}) %all-to-all-start) | async-done | bytes 1572896 | tf_op jit(solution)/shard_map/all_to_all | solution.py:234
  106.0 1.3 reshape_reshape.3.x_ref
  107.3 0.3 copy-done
  107.6 0.6 tile.11
  108.3 26.2 %shard_map.109 = f32[3072,128]{1,0:T(8,128)} custom-call(f32[3072,128]{1,0:T(8,128)} %reshape_reshape.3.x_ref, bf16[256,64]{1,0:T(8,128)(2,1)} %bitcast.90, bf16[4,128,1024]{2,1,0:T(8,128)(2,1)} %broadcast_multiply_fusion.1.w_prof_ref, bf16[4,64,1024]{2,1,0:T(8,128)(2,1)} %broadcast_multiply_fusion.2.w_pred_ref, f32[1,1024]{1,0:T(1,128)} %bitcast.100, ...), custom_call_target="tpu_custom_call" | custom-call | flops 8053063680 | bytes 3145728 | tf_op jit(solution)/shard_map/pallas_call | solution.py:135
  134.5 2.6 reshape.213
  137.0 1.9 copy.27
  138.9 1.1 gather_fusion
  140.4 0.3 convolution_reduce_fusion
  141.0 1.1 fusion.12
  142.8 1.9 add_divide_fusion
  144.9 0.3 fusion.13
  145.5 0.3 fusion.15
  146.0 0.3 fusion.17
  146.5 0.3 fusion.19
  147.1 0.3 fusion.21
  147.8 0.9 fusion.38
  148.7 0.6 copy-done.2
  149.3 2.1 fusion.6
  151.3 2.1 fusion.3
  153.4 2.2 add_add_fusion
  155.6 38.8 %all_to_all.10 = f32[24,32,512]{2,1,0:T(8,128)S(1)} all-to-all(f32[24,32,512]{2,1,0:T(8,128)S(1)} %bitcast.79), channel_id=1, replica_groups=mesh['mem'=24,'lon'=32] {'mem'}, dimensions={0} | all-to-all | bytes 3145728 | tf_op jit(solution)/shard_map/all_to_all | solution.py:251
  194.4 3.8 %reshape.216 = f32[3,8,32,16,32]{4,3,2,1,0:T(8,128)} reshape(f32[24,32,512]{2,1,0:T(8,128)S(1)} %all_to_all.10) | data formatting | bytes 3145728 | tf_op jit(solution)/shard_map/reshape | solution.py:252
  198.2 6.4 %copy.28 = f32[32,3,32,8,16]{2,4,3,1,0:T(8,128)} copy(f32[32,3,32,8,16]{2,4,0,3,1:T(8,128)} %bitcast.70) | data formatting | bytes 3145728 | tf_op jit(solution)/shard_map/transpose | solution.py:253
  204.6 4.4 %copy.29 = f32[32,3,32,128]{3,2,1,0:T(8,128)S(1)} copy(f32[32,3,32,128]{2,3,1,0:T(8,128)} %bitcast.71) | data formatting | bytes 3145728 | tf_op jit(solution)/shard_map/reshape | solution.py:253
  209.2 28.3 %collective-permute-start.3 = (f32[64,32,128]{2,1,0:T(8,128)S(1)}, f32[64,32,128]{2,1,0:T(8,128)S(1)}, u32[]{:S(2)}, u32[]{:S(2)}) collective-permute-start(f32[64,32,128]{2,1,0:T(8,128)S(1)} %bitcast.85), channel_id=1, source_target_pairs={{0,31},{1,0},{2,1},{3,2},{4,3},{5,4},{6,5},{7,6},{8,7},{9,8},{10,9... | collective-permute-start | bytes 3145736 | tf_op jit(solution)/shard_map/ppermute | solution.py:42
  237.5 1.9 collective-permute-start.2
  239.4 32.3 %collective-permute-done.3 = f32[64,32,128]{2,1,0:T(8,128)S(1)} collective-permute-done((f32[64,32,128]{2,1,0:T(8,128)S(1)}, f32[64,32,128]{2,1,0:T(8,128)S(1)}, u32[]{:S(2)}, u32[]{:S(2)}) %collective-permute-start.3) | collective-permute-done | bytes 1048608 | tf_op jit(solution)/shard_map/ppermute | solution.py:42
  271.7 12.3 %collective-permute-done.2 = f32[64,32,128]{2,1,0:T(8,128)S(1)} collective-permute-done((f32[64,32,128]{2,1,0:T(8,128)S(1)}, f32[64,32,128]{2,1,0:T(8,128)S(1)}, u32[]{:S(2)}, u32[]{:S(2)}) %collective-permute-start.2) | collective-permute-done | bytes 1048608 | tf_op jit(solution)/shard_map/ppermute | solution.py:42
  284.0 1.0 multiply_add_fusion
  285.0 1.6 add_bitcast_fusion
  (75 shorter events, 3.9 us)
Async XLA Ops:
  2.6 4.6 %copy-start.4 = (f32[32,3,128]{2,0,1:T(8,128)S(1)}, f32[32,3,128]{2,0,1:T(8,128)}, u32[]{:S(2)}) copy-start(f32[32,3,128]{2,0,1:T(8,128)} %param.12) | copy-start | bytes 147460
  2.6 26.0 %collective-permute-start.1 = (f32[65,32,128]{2,1,0:T(8,128)S(1)}, f32[65,32,128]{2,1,0:T(8,128)S(1)}, u32[]{:S(2)}, u32[]{:S(2)}) collective-permute-start(f32[65,32,128]{2,1,0:T(8,128)S(1)} %pad_maximum_fusion.9), channel_id=1, source_target_pairs={{0,31},{1,0},{2,1},{3,2},{4,3},{5,4},{6,5},{7,6},{8,7},{9,8},{10,9... | collective-permute-start | bytes 3194888 | tf_op jit(solution)/shard_map/ppermute | solution.py:42
  4.8 36.4 %collective-permute-start = (f32[65,32,128]{2,1,0:T(8,128)S(1)}, f32[65,32,128]{2,1,0:T(8,128)S(1)}, u32[]{:S(2)}, u32[]{:S(2)}) collective-permute-start(f32[65,32,128]{2,1,0:T(8,128)S(1)} %pad_maximum_fusion.8), channel_id=1, source_target_pairs={{0,1},{1,2},{2,3},{3,4},{4,5},{5,6},{6,7},{7,8},{8,9},{9,10},{10,1... | collective-permute-start | bytes 3194888 | tf_op jit(solution)/shard_map/ppermute | solution.py:42
  41.3 1.4 copy-start.3
  54.9 22.4 %copy-start.8 = (bf16[1,1,16,16]{3,2,1,0:T(8,128)(2,1)S(1)}, bf16[1,1,16,16]{3,2,1,0:T(8,128)(2,1)}, u32[]{:S(2)}) copy-start(bf16[1,1,16,16]{3,2,1,0:T(8,128)(2,1)} %param.17) | copy-start | bytes 1540
  54.9 23.0 %copy-start.6 = (f32[32,32]{1,0:T(8,128)S(1)}, f32[32,32]{1,0:T(8,128)}, u32[]{:S(2)}) copy-start(f32[32,32]{1,0:T(8,128)} %param.13) | copy-start | bytes 12292
  54.9 23.8 %copy-start.5 = (bf16[1024,32]{0,1:T(8,128)(2,1)S(1)}, bf16[1024,32]{0,1:T(8,128)(2,1)}, u32[]{:S(2)}) copy-start(bf16[1024,32]{0,1:T(8,128)(2,1)} %param.16) | copy-start | bytes 196612
  54.9 24.0 %copy-start.7 = (s32[1,1,256]{2,1,0:T(1,128)S(1)}, s32[1,1,256]{2,1,0:T(1,128)}, u32[]{:S(2)}) copy-start(s32[1,1,256]{2,1,0:T(1,128)} %param.19) | copy-start | bytes 3076
  54.9 24.0 %copy-start.9 = (s32[1,1,256]{2,1,0:T(1,128)S(1)}, s32[1,1,256]{2,1,0:T(1,128)}, u32[]{:S(2)}) copy-start(s32[1,1,256]{2,1,0:T(1,128)} %param.18) | copy-start | bytes 3076
  54.9 24.1 %copy-start.11 = (f32[32]{0:T(128)S(1)}, f32[32]{0:T(128)}, u32[]{:S(2)}) copy-start(f32[32]{0:T(128)} %param.21) | copy-start | bytes 388
  54.9 24.2 %slice-start = ((bf16[48,1024]{1,0:T(8,128)(2,1)}), bf16[16,1024]{1,0:T(8,128)(2,1)S(1)}, s32[]{:S(2)}) async-start(bf16[48,1024]{1,0:T(8,128)(2,1)} %param.14), calls=%async_computation.2 | async-start | bytes 65536 | tf_op jit(solution)/shard_map/slice | solution.py:122
  55.0 51.0 %all-to-all-start = ((f32[24,32,512]{2,1,0:T(8,128)}), f32[24,32,512]{2,1,0:T(8,128)S(1)}, u32[]{:S(2)}, u32[]{:S(2)}) async-start(f32[24,32,512]{2,1,0:T(8,128)} %copy.30), calls=%async_computation | async-start | bytes 3145728 | tf_op jit(solution)/shard_map/all_to_all | solution.py:234
  78.0 3.1 %slice-start.1 = ((bf16[48,1024]{1,0:T(8,128)(2,1)}), bf16[32,1024]{1,0:T(8,128)(2,1)S(1)}, s32[]{:S(2)}) async-start(bf16[48,1024]{1,0:T(8,128)(2,1)} %param.14), calls=%async_computation.3 | async-start | bytes 131072 | tf_op jit(solution)/shard_map/slice | solution.py:121
  106.0 1.7 copy-start
  138.9 1.3 copy-start.10
  142.8 1.9 copy-start.1
  147.6 1.7 copy-start.2
  209.2 62.5 %collective-permute-start.3 = (f32[64,32,128]{2,1,0:T(8,128)S(1)}, f32[64,32,128]{2,1,0:T(8,128)S(1)}, u32[]{:S(2)}, u32[]{:S(2)}) collective-permute-start(f32[64,32,128]{2,1,0:T(8,128)S(1)} %bitcast.85), channel_id=1, source_target_pairs={{0,31},{1,0},{2,1},{3,2},{4,3},{5,4},{6,5},{7,6},{8,7},{9,8},{10,9... | collective-permute-start | bytes 3145736 | tf_op jit(solution)/shard_map/ppermute | solution.py:42
  237.5 46.5 %collective-permute-start.2 = (f32[64,32,128]{2,1,0:T(8,128)S(1)}, f32[64,32,128]{2,1,0:T(8,128)S(1)}, u32[]{:S(2)}, u32[]{:S(2)}) collective-permute-start(f32[64,32,128]{2,1,0:T(8,128)S(1)} %bitcast.84), channel_id=1, source_target_pairs={{0,1},{1,2},{2,3},{3,4},{4,5},{5,6},{6,7},{7,8},{8,9},{9,10},{10,1... | collective-permute-start | bytes 3145736 | tf_op jit(solution)/shard_map/ppermute | solution.py:42

commit v5 on v4

--- a/solution.py
+++ b/solution.py
@@ -152,6 +152,29 @@
             bytes_accessed=total_rows * (lanes + parts * channels) * 4,
         ),
     )(packed, pred_tiled, w_prof, w_pred, bias_offset.reshape(1, hid), w_out, w_phys)
+
+
+def mean_weight_kernel(root_count, spread_ref, drive_ref, scale_ref, out_ref):
+    spread = spread_ref[...]
+    scale = scale_ref[...]
+
+    def multiply(vector):
+        inner = jnp.sum(spread * vector, axis=0, keepdims=True)
+        return (vector + jnp.sum(spread * inner, axis=1, keepdims=True)) / scale
+
+    out_ref[...] = apply_root(multiply, apply_root(multiply, drive_ref[...])) / (scale * root_count)
+
+
+def mean_weight_chain(spread_wide, drive, scale, root_count):
+    members, obs = spread_wide.shape
+    out = pl.pallas_call(
+        functools.partial(mean_weight_kernel, root_count),
+        out_shape=jax.ShapeDtypeStruct((members, 1), jnp.float32),
+        cost_estimate=pl.CostEstimate(
+            flops=24 * members * obs, transcendentals=0, bytes_accessed=members * obs * 4
+        ),
+    )(spread_wide, drive.reshape(members, 1), scale.reshape(1, 1))
+    return out[:, 0]
 
 
 def analyse(
@@ -188,17 +211,11 @@
     gram = jnp.dot(spread, spread.T, preferred_element_type=jnp.float32)
     mtx = (jnp.eye(members, dtype=jnp.float32) + gram) / scale
 
-    def multiply_vector(vector):
-        inner = jnp.sum(spread_wide * vector[:, None], axis=0)
-        return (vector + jnp.sum(spread_wide * inner[None, :], axis=1)) / scale
-
     def multiply_fast(vectors):
         return jnp.dot(mtx, vectors, precision=lax.Precision.HIGH)
 
     drive = jnp.dot(spread_wide, innov, precision=highest)
-    mean_weights = apply_root(multiply_vector, apply_root(multiply_vector, drive)) / (
-        scale * root_count
-    )
+    mean_weights = mean_weight_chain(spread_wide, drive, scale, root_count)
     xmean = jnp.mean(flat, axis=0)
     pert = flat - xmean
     spread_part = apply_root(multiply_fast, pert)

time: 287 us -> 294 us (1.024)
  Pallas kernels: 26.2 us -> 30 us
  local copies, waits for them, and re-layouts: 39.5 us -> 43.2 us
    pallas_call x0 -> x1, Pallas kernels: none -> 3.81 us  [mean_weight_chain(): pl.pallas_call(functools.partial(mean_weight_kernel, root_count), out_sha...]
    reduce_sum x12 -> x1, other arithmetic: 3.88 us -> 0.85 us  [analyse(): scale = 1.0 + jnp.sum(spread_wide * spread_wide) / members]
where the time goes in v5:
time: 294 us; the launch traced here: 293 us
  waiting for transfers between devices  102 us (35%)
  starting transfers between devices  56.9 us (19%)
  local copies, waits for them, and re-layouts  43.2 us (15%)
  blocking collectives  38.8 us (13%)
  Pallas kernels  30 us (10%)
  other arithmetic  11.3 us (4%)
  matrix products  9.55 us (3%)
    ppermute x4, waiting for transfers between devices, ring_shift(): return lax.ppermute(block, axis, pairs)  78.5 us
    all_to_all x1, blocking collectives, shards(): lax.all_to_all(returning, 'mem', split_axis=0, concat_axis=0, tiled=True)  38.8 us
    ppermute x4, starting transfers between devices, ring_shift(): return lax.ppermute(block, axis, pairs)  34.7 us
    pallas_call x1, Pallas kernels, network(): pl.pallas_call(network_kernel, out_shape=jax.ShapeDtypeStruct((total_rows...  26.2 us
    all_to_all x1, waiting for transfers between devices, shards(): lax.all_to_all(outgoing, 'mem', split_axis=0, concat_axis=0, tiled=True)  23.7 us
    all_to_all x1, starting transfers between devices, shards(): lax.all_to_all(outgoing, 'mem', split_axis=0, concat_axis=0, tiled=True)  22.2 us
    reshape x2, local copies, waits for them, and re-layouts, shards(): jnp.transpose(outgoing, (1, 3, 0, 4, 2))  6.72 us
    transpose x1, local copies, waits for them, and re-layouts, shards(): jnp.transpose(restored, (2, 0, 4, 1, 3))  6.38 us
  transfers between devices with their start and end apart: 5, of which 5 were waited for; matrix products, arithmetic and copies ran while one was open for 2% of the time, Pallas kernels for 0%

profile of v5, /device:TPU:512, one launch (start us, length us, event | category | flops | bytes accessed | tf_op | source)
XLA Modules:
  0.0 293.2 jit_solution(10552488378435051465)
XLA Ops:
  0.0 0.7 fusion.24
  0.7 1.8 fusion.23
  2.6 2.1 collective-permute-start.1
  4.8 2.4 collective-permute-start
  7.2 21.5 %collective-permute-done.1 = f32[65,32,128]{2,1,0:T(8,128)S(1)} collective-permute-done((f32[65,32,128]{2,1,0:T(8,128)S(1)}, f32[65,32,128]{2,1,0:T(8,128)S(1)}, u32[]{:S(2)}, u32[]{:S(2)}) %collective-permute-start.1) | collective-permute-done | bytes 1064992 | tf_op jit(solution)/shard_map/ppermute | solution.py:42
  28.7 12.5 %collective-permute-done = f32[65,32,128]{2,1,0:T(8,128)S(1)} collective-permute-done((f32[65,32,128]{2,1,0:T(8,128)S(1)}, f32[65,32,128]{2,1,0:T(8,128)S(1)}, u32[]{:S(2)}, u32[]{:S(2)}) %collective-permute-start) | collective-permute-done | bytes 1064992 | tf_op jit(solution)/shard_map/ppermute | solution.py:42
  41.4 1.3 copy-done.1
  42.7 1.0 multiply_add_fusion.1
  43.8 0.5 multiply_add_fusion.2
  44.2 4.1 %copy.26 = f32[32,3,32,128]{2,3,1,0:T(8,128)} copy(f32[32,3,32,128]{3,2,1,0:T(8,128)S(1)} %multiply_add_fusion.2) | data formatting | bytes 3145728 | tf_op jit(solution)/shard_map/add | solution.py:47
  48.3 4.7 %reshape.236 = f32[24,32,512]{2,0,1:T(8,128)S(1)} reshape(f32[3,8,32,16,32]{4,3,1,0,2:T(8,128)} %bitcast.64) | data formatting | bytes 3145728 | tf_op jit(solution)/shard_map/reshape | solution.py:248
  53.0 2.1 copy.35
  55.1 22.2 %all-to-all-start = ((f32[24,32,512]{2,1,0:T(8,128)}), f32[24,32,512]{2,1,0:T(8,128)S(1)}, u32[]{:S(2)}, u32[]{:S(2)}) async-start(f32[24,32,512]{2,1,0:T(8,128)} %copy.35), calls=%async_computation | async-start | bytes 3145728 | tf_op jit(solution)/shard_map/all_to_all | solution.py:251
  78.0 0.7 copy.29.w_phys_ref
  79.1 0.9 broadcast_multiply_fusion.2.w_pred_ref
  80.0 1.1 broadcast_multiply_fusion.w_out_ref
  81.1 1.1 broadcast_multiply_fusion.1.w_prof_ref
  82.2 23.7 %all-to-all-done = f32[24,32,512]{2,1,0:T(8,128)S(1)} async-done(((f32[24,32,512]{2,1,0:T(8,128)}), f32[24,32,512]{2,1,0:T(8,128)S(1)}, u32[]{:S(2)}, u32[]{:S(2)}) %all-to-all-start) | async-done | bytes 1572896 | tf_op jit(solution)/shard_map/all_to_all | solution.py:251
  106.0 1.2 reshape_reshape.3.x_ref
  107.2 0.6 tile.11
  107.8 26.2 %shard_map.109 = f32[3072,128]{1,0:T(8,128)} custom-call(f32[3072,128]{1,0:T(8,128)} %reshape_reshape.3.x_ref, bf16[256,64]{1,0:T(8,128)(2,1)} %bitcast.83, bf16[4,128,1024]{2,1,0:T(8,128)(2,1)} %broadcast_multiply_fusion.1.w_prof_ref, bf16[4,64,1024]{2,1,0:T(8,128)(2,1)} %broadcast_multiply_fusion.2.w_pred_ref, f32[1,1024]{1,0:T(1,128)} %bitcast.93, ...), custom_call_target="tpu_custom_call" | custom-call | flops 8053063680 | bytes 3145728 | tf_op jit(solution)/shard_map/pallas_call | solution.py:135
  134.0 2.5 reshape.213
  136.6 1.9 copy.30
  138.5 2.0 gather_fusion
  140.4 1.4 copy.31
  142.0 1.0 bitcast_convert_fusion
  143.0 0.9 multiply_reduce_fusion
  144.5 1.9 add_divide_fusion
  146.6 0.5 convolution_reduce_fusion
  147.0 0.9 reshape.238.drive_ref
  148.0 3.8 %shard_map.110 = f32[768,1]{1,0:T(8,128)} custom-call(f32[768,256]{1,0:T(8,128)} %get-tuple-element.5.spread_ref, f32[768,1]{1,0:T(8,128)} %reshape.238.drive_ref, f32[1,1]{1,0:T(1,128)} %bitcast.24.scale_ref), custom_call_target="tpu_custom_call" | custom-call | flops 4718592 | bytes 786432 | tf_op jit(solution)/shard_map/pallas_call | solution.py:170
  151.8 1.2 reduce.3
  153.2 1.5 copy-done
  154.6 2.1 fusion.6
  156.7 2.1 fusion.3
  158.8 0.2 broadcast_subtract_fusion
  159.0 0.9 fusion.25
  159.9 2.2 add_add_fusion
  162.1 38.8 %all_to_all.10 = f32[24,32,512]{2,1,0:T(8,128)S(1)} all-to-all(f32[24,32,512]{2,1,0:T(8,128)S(1)} %bitcast.72), channel_id=1, replica_groups=mesh['mem'=24,'lon'=32] {'mem'}, dimensions={0} | all-to-all | bytes 3145728 | tf_op jit(solution)/shard_map/all_to_all | solution.py:268
  200.9 3.8 %reshape.218 = f32[3,8,32,16,32]{4,3,2,1,0:T(8,128)} reshape(f32[24,32,512]{2,1,0:T(8,128)S(1)} %all_to_all.10) | data formatting | bytes 3145728 | tf_op jit(solution)/shard_map/reshape | solution.py:269
  204.6 6.4 %copy.33 = f32[32,3,32,8,16]{2,4,3,1,0:T(8,128)} copy(f32[32,3,32,8,16]{2,4,0,3,1:T(8,128)} %bitcast.62) | data formatting | bytes 3145728 | tf_op jit(solution)/shard_map/transpose | solution.py:270
  211.0 4.4 %copy.34 = f32[32,3,32,128]{3,2,1,0:T(8,128)S(1)} copy(f32[32,3,32,128]{2,3,1,0:T(8,128)} %bitcast.63) | data formatting | bytes 3145728 | tf_op jit(solution)/shard_map/reshape | solution.py:270
  215.6 28.3 %collective-permute-start.3 = (f32[64,32,128]{2,1,0:T(8,128)S(1)}, f32[64,32,128]{2,1,0:T(8,128)S(1)}, u32[]{:S(2)}, u32[]{:S(2)}) collective-permute-start(f32[64,32,128]{2,1,0:T(8,128)S(1)} %bitcast.78), channel_id=1, source_target_pairs={{0,31},{1,0},{2,1},{3,2},{4,3},{5,4},{6,5},{7,6},{8,7},{9,8},{10,9... | collective-permute-start | bytes 3145736 | tf_op jit(solution)/shard_map/ppermute | solution.py:42
  244.0 1.9 collective-permute-start.2
  245.9 32.3 %collective-permute-done.3 = f32[64,32,128]{2,1,0:T(8,128)S(1)} collective-permute-done((f32[64,32,128]{2,1,0:T(8,128)S(1)}, f32[64,32,128]{2,1,0:T(8,128)S(1)}, u32[]{:S(2)}, u32[]{:S(2)}) %collective-permute-start.3) | collective-permute-done | bytes 1048608 | tf_op jit(solution)/shard_map/ppermute | solution.py:42
  278.2 12.3 %collective-permute-done.2 = f32[64,32,128]{2,1,0:T(8,128)S(1)} collective-permute-done((f32[64,32,128]{2,1,0:T(8,128)S(1)}, f32[64,32,128]{2,1,0:T(8,128)S(1)}, u32[]{:S(2)}, u32[]{:S(2)}) %collective-permute-start.2) | collective-permute-done | bytes 1048608 | tf_op jit(solution)/shard_map/ppermute | solution.py:42
  290.5 1.0 multiply_add_fusion
  291.5 1.6 add_bitcast_fusion
  (58 shorter events, 2.1 us)
Async XLA Ops:
  2.6 4.6 %copy-start.2 = (f32[32,3,128]{2,0,1:T(8,128)S(1)}, f32[32,3,128]{2,0,1:T(8,128)}, u32[]{:S(2)}) copy-start(f32[32,3,128]{2,0,1:T(8,128)} %param.12) | copy-start | bytes 147460
  2.6 26.0 %collective-permute-start.1 = (f32[65,32,128]{2,1,0:T(8,128)S(1)}, f32[65,32,128]{2,1,0:T(8,128)S(1)}, u32[]{:S(2)}, u32[]{:S(2)}) collective-permute-start(f32[65,32,128]{2,1,0:T(8,128)S(1)} %pad_maximum_fusion.9), channel_id=1, source_target_pairs={{0,31},{1,0},{2,1},{3,2},{4,3},{5,4},{6,5},{7,6},{8,7},{9,8},{10,9... | collective-permute-start | bytes 3194888 | tf_op jit(solution)/shard_map/ppermute | solution.py:42
  4.8 36.4 %collective-permute-start = (f32[65,32,128]{2,1,0:T(8,128)S(1)}, f32[65,32,128]{2,1,0:T(8,128)S(1)}, u32[]{:S(2)}, u32[]{:S(2)}) collective-permute-start(f32[65,32,128]{2,1,0:T(8,128)S(1)} %pad_maximum_fusion.8), channel_id=1, source_target_pairs={{0,1},{1,2},{2,3},{3,4},{4,5},{5,6},{6,7},{7,8},{8,9},{9,10},{10,1... | collective-permute-start | bytes 3194888 | tf_op jit(solution)/shard_map/ppermute | solution.py:42
  41.3 1.4 copy-start.1
  55.0 22.3 %copy-start.6 = (bf16[1,1,16,16]{3,2,1,0:T(8,128)(2,1)S(1)}, bf16[1,1,16,16]{3,2,1,0:T(8,128)(2,1)}, u32[]{:S(2)}) copy-start(bf16[1,1,16,16]{3,2,1,0:T(8,128)(2,1)} %param.17) | copy-start | bytes 1540
  55.0 22.9 %copy-start.4 = (f32[32,32]{1,0:T(8,128)S(1)}, f32[32,32]{1,0:T(8,128)}, u32[]{:S(2)}) copy-start(f32[32,32]{1,0:T(8,128)} %param.13) | copy-start | bytes 12292
  55.0 23.7 %copy-start.3 = (bf16[1024,32]{0,1:T(8,128)(2,1)S(1)}, bf16[1024,32]{0,1:T(8,128)(2,1)}, u32[]{:S(2)}) copy-start(bf16[1024,32]{0,1:T(8,128)(2,1)} %param.16) | copy-start | bytes 196612
  55.0 23.9 %copy-start.5 = (s32[1,1,256]{2,1,0:T(1,128)S(1)}, s32[1,1,256]{2,1,0:T(1,128)}, u32[]{:S(2)}) copy-start(s32[1,1,256]{2,1,0:T(1,128)} %param.19) | copy-start | bytes 3076
  55.0 23.9 %copy-start.7 = (s32[1,1,256]{2,1,0:T(1,128)S(1)}, s32[1,1,256]{2,1,0:T(1,128)}, u32[]{:S(2)}) copy-start(s32[1,1,256]{2,1,0:T(1,128)} %param.18) | copy-start | bytes 3076
  55.0 24.0 %copy-start.9 = (f32[32]{0:T(128)S(1)}, f32[32]{0:T(128)}, u32[]{:S(2)}) copy-start(f32[32]{0:T(128)} %param.21) | copy-start | bytes 388
  55.0 24.1 %slice-start = ((bf16[48,1024]{1,0:T(8,128)(2,1)}), bf16[16,1024]{1,0:T(8,128)(2,1)S(1)}, s32[]{:S(2)}) async-start(bf16[48,1024]{1,0:T(8,128)(2,1)} %param.14), calls=%async_computation.2 | async-start | bytes 65536 | tf_op jit(solution)/shard_map/slice | solution.py:122
  55.1 50.9 %all-to-all-start = ((f32[24,32,512]{2,1,0:T(8,128)}), f32[24,32,512]{2,1,0:T(8,128)S(1)}, u32[]{:S(2)}, u32[]{:S(2)}) async-start(f32[24,32,512]{2,1,0:T(8,128)} %copy.35), calls=%async_computation | async-start | bytes 3145728 | tf_op jit(solution)/shard_map/all_to_all | solution.py:251
  78.0 3.1 %slice-start.1 = ((bf16[48,1024]{1,0:T(8,128)(2,1)}), bf16[32,1024]{1,0:T(8,128)(2,1)S(1)}, s32[]{:S(2)}) async-start(bf16[48,1024]{1,0:T(8,128)(2,1)} %param.14), calls=%async_computation.3 | async-start | bytes 131072 | tf_op jit(solution)/shard_map/slice | solution.py:121
  140.4 1.6 copy-start.8
  153.0 1.7 copy-start
  215.6 62.6 %collective-permute-start.3 = (f32[64,32,128]{2,1,0:T(8,128)S(1)}, f32[64,32,128]{2,1,0:T(8,128)S(1)}, u32[]{:S(2)}, u32[]{:S(2)}) collective-permute-start(f32[64,32,128]{2,1,0:T(8,128)S(1)} %bitcast.78), channel_id=1, source_target_pairs={{0,31},{1,0},{2,1},{3,2},{4,3},{5,4},{6,5},{7,6},{8,7},{9,8},{10,9... | collective-permute-start | bytes 3145736 | tf_op jit(solution)/shard_map/ppermute | solution.py:42
  244.0 46.5 %collective-permute-start.2 = (f32[64,32,128]{2,1,0:T(8,128)S(1)}, f32[64,32,128]{2,1,0:T(8,128)S(1)}, u32[]{:S(2)}, u32[]{:S(2)}) collective-permute-start(f32[64,32,128]{2,1,0:T(8,128)S(1)} %bitcast.77), channel_id=1, source_target_pairs={{0,1},{1,2},{2,3},{3,4},{4,5},{5,6},{6,7},{7,8},{8,9},{9,10},{10,1... | collective-permute-start | bytes 3145736 | tf_op jit(solution)/shard_map/ppermute | solution.py:42

commit v6 on v2

--- a/solution.py
+++ b/solution.py
@@ -5,6 +5,7 @@
 import jax.numpy as jnp
 from jax import lax
 from jax.experimental import pallas as pl
+from jax.experimental.layout import Layout, with_layout_constraint
 from jax.experimental.pallas import tpu as pltpu
 from jax.sharding import PartitionSpec as P
 
@@ -112,6 +113,7 @@
 
 def network(packed, predictors, weighting, bias_in, bias_offset, bias_out, levels, rows=256):
     total_rows, lanes = packed.shape
+    assert total_rows % rows == 0
     parts = lanes // levels
     hid = bias_in.shape[1]
     channels = bias_out.shape[1]
@@ -248,6 +250,7 @@
     restored = jnp.transpose(restored, (2, 0, 4, 1, 3)).reshape(
         mem_local, lon_local, levels, lat_rows
     )
+    restored = with_layout_constraint(restored, Layout((0, 1, 2, 3)))
     padded, _ = exchange(restored)
     field = two_passes(padded, wind_padded)
     return jnp.transpose(field, (0, 2, 1, 3))

time: 295 us -> 298 us (1.010)
  the two profiles are of different devices: /device:TPU:128 before, /device:TPU:512 now
where the time goes in v6:
time: 298 us; the launch traced here: 297 us
  waiting for transfers between devices  102 us (34%)
  starting transfers between devices  56.9 us (19%)
  local copies, waits for them, and re-layouts  39.4 us (13%)
  blocking collectives  38.8 us (13%)
  Pallas kernels  26.2 us (9%)
  matrix products  20.4 us (7%)
  other arithmetic  11.7 us (4%)
    ppermute x4, waiting for transfers between devices, ring_shift(): return lax.ppermute(block, axis, pairs)  78.5 us
    all_to_all x1, blocking collectives, shards(): lax.all_to_all(returning, 'mem', split_axis=0, concat_axis=0, tiled=True)  38.8 us
    ppermute x4, starting transfers between devices, ring_shift(): return lax.ppermute(block, axis, pairs)  34.6 us
    pallas_call x1, Pallas kernels, network(): pl.pallas_call(network_kernel, out_shape=jax.ShapeDtypeStruct((total_rows...  26.2 us
    all_to_all x1, waiting for transfers between devices, shards(): lax.all_to_all(outgoing, 'mem', split_axis=0, concat_axis=0, tiled=True)  23.7 us
    all_to_all x1, starting transfers between devices, shards(): lax.all_to_all(outgoing, 'mem', split_axis=0, concat_axis=0, tiled=True)  22.3 us
    dot_general x6, matrix products, multiply(): return jnp.dot(mtx, vectors, precision=highest)  12.4 us
    reshape x2, local copies, waits for them, and re-layouts, shards(): jnp.transpose(outgoing, (1, 3, 0, 4, 2))  6.72 us
  transfers between devices with their start and end apart: 5, of which 5 were waited for; matrix products, arithmetic and copies ran while one was open for 2% of the time, Pallas kernels for 0%

profile of v6, /device:TPU:512, one launch (start us, length us, event | category | flops | bytes accessed | tf_op | source)
XLA Modules:
  0.0 297.0 jit_solution(16256281369513987466)
XLA Ops:
  0.0 0.7 fusion.24
  0.7 1.8 fusion.23
  2.7 2.1 collective-permute-start.1
  4.8 2.4 collective-permute-start
  7.2 21.5 %collective-permute-done.1 = f32[65,32,128]{2,1,0:T(8,128)S(1)} collective-permute-done((f32[65,32,128]{2,1,0:T(8,128)S(1)}, f32[65,32,128]{2,1,0:T(8,128)S(1)}, u32[]{:S(2)}, u32[]{:S(2)}) %collective-permute-start.1) | collective-permute-done | bytes 1064992 | tf_op jit(solution)/shard_map/ppermute | solution.py:42
  28.7 12.5 %collective-permute-done = f32[65,32,128]{2,1,0:T(8,128)S(1)} collective-permute-done((f32[65,32,128]{2,1,0:T(8,128)S(1)}, f32[65,32,128]{2,1,0:T(8,128)S(1)}, u32[]{:S(2)}, u32[]{:S(2)}) %collective-permute-start) | collective-permute-done | bytes 1064992 | tf_op jit(solution)/shard_map/ppermute | solution.py:42
  41.4 1.3 copy-done
  42.7 1.0 multiply_add_fusion.1
  43.8 0.5 multiply_add_fusion.2
  44.3 4.0 %copy.23 = f32[32,3,32,128]{2,3,1,0:T(8,128)} copy(f32[32,3,32,128]{3,2,1,0:T(8,128)S(1)} %multiply_add_fusion.2) | data formatting | bytes 3145728 | tf_op jit(solution)/shard_map/add | solution.py:47
  48.2 4.7 %reshape.234 = f32[24,32,512]{2,0,1:T(8,128)S(1)} reshape(f32[3,8,32,16,32]{4,3,1,0,2:T(8,128)} %bitcast.72) | data formatting | bytes 3145728 | tf_op jit(solution)/shard_map/reshape | solution.py:228
  52.9 2.1 copy.30
  55.0 22.3 %all-to-all-start = ((f32[24,32,512]{2,1,0:T(8,128)}), f32[24,32,512]{2,1,0:T(8,128)S(1)}, u32[]{:S(2)}, u32[]{:S(2)}) async-start(f32[24,32,512]{2,1,0:T(8,128)} %copy.30), calls=%async_computation | async-start | bytes 3145728 | tf_op jit(solution)/shard_map/all_to_all | solution.py:231
  78.0 0.7 copy.26.w_phys_ref
  79.1 0.9 broadcast_multiply_fusion.2.w_pred_ref
  80.1 1.1 broadcast_multiply_fusion.w_out_ref
  81.2 1.1 broadcast_multiply_fusion.1.w_prof_ref
  82.3 23.7 %all-to-all-done = f32[24,32,512]{2,1,0:T(8,128)S(1)} async-done(((f32[24,32,512]{2,1,0:T(8,128)}), f32[24,32,512]{2,1,0:T(8,128)S(1)}, u32[]{:S(2)}, u32[]{:S(2)}) %all-to-all-start) | async-done | bytes 1572896 | tf_op jit(solution)/shard_map/all_to_all | solution.py:231
  106.1 1.2 reshape_reshape.3.x_ref
  107.4 0.7 tile.11
  108.0 26.2 %shard_map.109 = f32[3072,128]{1,0:T(8,128)} custom-call(f32[3072,128]{1,0:T(8,128)} %reshape_reshape.3.x_ref, bf16[256,64]{1,0:T(8,128)(2,1)} %bitcast.90, bf16[4,128,1024]{2,1,0:T(8,128)(2,1)} %broadcast_multiply_fusion.1.w_prof_ref, bf16[4,64,1024]{2,1,0:T(8,128)(2,1)} %broadcast_multiply_fusion.2.w_pred_ref, f32[1,1024]{1,0:T(1,128)} %bitcast.100, ...), custom_call_target="tpu_custom_call" | custom-call | flops 8053063680 | bytes 3145728 | tf_op jit(solution)/shard_map/pallas_call | solution.py:135
  134.2 2.5 reshape.201
  136.8 1.9 copy.27
  138.7 2.0 gather_fusion
  140.6 1.3 select_reduce_fusion
  142.0 2.2 multiply_reduce_fusion
  144.9 0.5 add_divide_fusion
  145.7 2.1 convolution_reduce_fusion.5
  147.8 2.1 convolution_reduce_fusion.4
  149.9 2.1 convolution_reduce_fusion.3
  152.0 2.1 convolution_reduce_fusion.2
  154.1 2.1 convolution_reduce_fusion.1
  156.2 2.1 convolution_reduce_fusion
  158.3 0.4 bitcast_subtract_fusion
  158.7 2.1 fusion.6
  160.8 0.9 fusion.25
  161.6 2.1 fusion.3
  163.7 2.2 add_add_fusion
  165.9 38.8 %all_to_all.10 = f32[24,32,512]{2,1,0:T(8,128)S(1)} all-to-all(f32[24,32,512]{2,1,0:T(8,128)S(1)} %bitcast.79), channel_id=1, replica_groups=mesh['mem'=24,'lon'=32] {'mem'}, dimensions={0} | all-to-all | bytes 3145728 | tf_op jit(solution)/shard_map/all_to_all | solution.py:248
  204.8 3.8 %reshape.204 = f32[3,8,32,16,32]{4,3,2,1,0:T(8,128)} reshape(f32[24,32,512]{2,1,0:T(8,128)S(1)} %all_to_all.10) | data formatting | bytes 3145728 | tf_op jit(solution)/shard_map/reshape | solution.py:249
  208.5 6.4 %copy.28 = f32[32,3,32,8,16]{2,4,3,1,0:T(8,128)} copy(f32[32,3,32,8,16]{2,4,0,3,1:T(8,128)} %bitcast.70) | data formatting | bytes 3145728 | tf_op jit(solution)/shard_map/transpose | solution.py:250
  214.9 4.4 %copy.29 = f32[32,3,32,128]{3,2,1,0:T(8,128)S(1)} copy(f32[32,3,32,128]{2,3,1,0:T(8,128)} %bitcast.71) | data formatting | bytes 3145728 | tf_op jit(solution)/shard_map/reshape | solution.py:250
  219.5 28.2 %collective-permute-start.3 = (f32[64,32,128]{2,1,0:T(8,128)S(1)}, f32[64,32,128]{2,1,0:T(8,128)S(1)}, u32[]{:S(2)}, u32[]{:S(2)}) collective-permute-start(f32[64,32,128]{2,1,0:T(8,128)S(1)} %bitcast.85), channel_id=1, source_target_pairs={{0,31},{1,0},{2,1},{3,2},{4,3},{5,4},{6,5},{7,6},{8,7},{9,8},{10,9... | collective-permute-start | bytes 3145736 | tf_op jit(solution)/shard_map/ppermute | solution.py:42
  247.8 1.9 collective-permute-start.2
  249.7 32.3 %collective-permute-done.3 = f32[64,32,128]{2,1,0:T(8,128)S(1)} collective-permute-done((f32[64,32,128]{2,1,0:T(8,128)S(1)}, f32[64,32,128]{2,1,0:T(8,128)S(1)}, u32[]{:S(2)}, u32[]{:S(2)}) %collective-permute-start.3) | collective-permute-done | bytes 1048608 | tf_op jit(solution)/shard_map/ppermute | solution.py:42
  282.0 12.3 %collective-permute-done.2 = f32[64,32,128]{2,1,0:T(8,128)S(1)} collective-permute-done((f32[64,32,128]{2,1,0:T(8,128)S(1)}, f32[64,32,128]{2,1,0:T(8,128)S(1)}, u32[]{:S(2)}, u32[]{:S(2)}) %collective-permute-start.2) | collective-permute-done | bytes 1048608 | tf_op jit(solution)/shard_map/ppermute | solution.py:42
  294.3 1.0 multiply_add_fusion
  295.3 1.6 add_bitcast_fusion
  (69 shorter events, 2.2 us)
Async XLA Ops:
  2.6 4.6 %copy-start.1 = (f32[32,3,128]{2,0,1:T(8,128)S(1)}, f32[32,3,128]{2,0,1:T(8,128)}, u32[]{:S(2)}) copy-start(f32[32,3,128]{2,0,1:T(8,128)} %param.12) | copy-start | bytes 147460
  2.7 26.0 %collective-permute-start.1 = (f32[65,32,128]{2,1,0:T(8,128)S(1)}, f32[65,32,128]{2,1,0:T(8,128)S(1)}, u32[]{:S(2)}, u32[]{:S(2)}) collective-permute-start(f32[65,32,128]{2,1,0:T(8,128)S(1)} %pad_maximum_fusion.9), channel_id=1, source_target_pairs={{0,31},{1,0},{2,1},{3,2},{4,3},{5,4},{6,5},{7,6},{8,7},{9,8},{10,9... | collective-permute-start | bytes 3194888 | tf_op jit(solution)/shard_map/ppermute | solution.py:42
  4.8 36.4 %collective-permute-start = (f32[65,32,128]{2,1,0:T(8,128)S(1)}, f32[65,32,128]{2,1,0:T(8,128)S(1)}, u32[]{:S(2)}, u32[]{:S(2)}) collective-permute-start(f32[65,32,128]{2,1,0:T(8,128)S(1)} %pad_maximum_fusion.8), channel_id=1, source_target_pairs={{0,1},{1,2},{2,3},{3,4},{4,5},{5,6},{6,7},{7,8},{8,9},{9,10},{10,1... | collective-permute-start | bytes 3194888 | tf_op jit(solution)/shard_map/ppermute | solution.py:42
  41.3 1.4 copy-start
  54.9 22.4 %copy-start.5 = (bf16[1,1,16,16]{3,2,1,0:T(8,128)(2,1)S(1)}, bf16[1,1,16,16]{3,2,1,0:T(8,128)(2,1)}, u32[]{:S(2)}) copy-start(bf16[1,1,16,16]{3,2,1,0:T(8,128)(2,1)} %param.17) | copy-start | bytes 1540
  54.9 23.0 %copy-start.3 = (f32[32,32]{1,0:T(8,128)S(1)}, f32[32,32]{1,0:T(8,128)}, u32[]{:S(2)}) copy-start(f32[32,32]{1,0:T(8,128)} %param.13) | copy-start | bytes 12292
  54.9 23.8 %copy-start.2 = (bf16[1024,32]{0,1:T(8,128)(2,1)S(1)}, bf16[1024,32]{0,1:T(8,128)(2,1)}, u32[]{:S(2)}) copy-start(bf16[1024,32]{0,1:T(8,128)(2,1)} %param.16) | copy-start | bytes 196612
  54.9 24.0 %copy-start.4 = (s32[1,1,256]{2,1,0:T(1,128)S(1)}, s32[1,1,256]{2,1,0:T(1,128)}, u32[]{:S(2)}) copy-start(s32[1,1,256]{2,1,0:T(1,128)} %param.19) | copy-start | bytes 3076
  54.9 24.0 %copy-start.6 = (s32[1,1,256]{2,1,0:T(1,128)S(1)}, s32[1,1,256]{2,1,0:T(1,128)}, u32[]{:S(2)}) copy-start(s32[1,1,256]{2,1,0:T(1,128)} %param.18) | copy-start | bytes 3076
  55.0 24.0 %copy-start.8 = (f32[32]{0:T(128)S(1)}, f32[32]{0:T(128)}, u32[]{:S(2)}) copy-start(f32[32]{0:T(128)} %param.21) | copy-start | bytes 388
  55.0 24.2 %slice-start = ((bf16[48,1024]{1,0:T(8,128)(2,1)}), bf16[16,1024]{1,0:T(8,128)(2,1)S(1)}, s32[]{:S(2)}) async-start(bf16[48,1024]{1,0:T(8,128)(2,1)} %param.14), calls=%async_computation.2 | async-start | bytes 65536 | tf_op jit(solution)/shard_map/slice | solution.py:122
  55.0 51.0 %all-to-all-start = ((f32[24,32,512]{2,1,0:T(8,128)}), f32[24,32,512]{2,1,0:T(8,128)S(1)}, u32[]{:S(2)}, u32[]{:S(2)}) async-start(f32[24,32,512]{2,1,0:T(8,128)} %copy.30), calls=%async_computation | async-start | bytes 3145728 | tf_op jit(solution)/shard_map/all_to_all | solution.py:231
  78.0 3.1 %slice-start.1 = ((bf16[48,1024]{1,0:T(8,128)(2,1)}), bf16[32,1024]{1,0:T(8,128)(2,1)S(1)}, s32[]{:S(2)}) async-start(bf16[48,1024]{1,0:T(8,128)(2,1)} %param.14), calls=%async_computation.3 | async-start | bytes 131072 | tf_op jit(solution)/shard_map/slice | solution.py:121
  138.7 3.3 %copy-start.7 = (f32[1,1,256]{2,1,0:T(1,128)S(1)}, f32[1,1,256]{2,1,0:T(1,128)}, u32[]{:S(2)}) copy-start(f32[1,1,256]{2,1,0:T(1,128)} %param.20) | copy-start | bytes 3076
  219.5 62.5 %collective-permute-start.3 = (f32[64,32,128]{2,1,0:T(8,128)S(1)}, f32[64,32,128]{2,1,0:T(8,128)S(1)}, u32[]{:S(2)}, u32[]{:S(2)}) collective-permute-start(f32[64,32,128]{2,1,0:T(8,128)S(1)} %bitcast.85), channel_id=1, source_target_pairs={{0,31},{1,0},{2,1},{3,2},{4,3},{5,4},{6,5},{7,6},{8,7},{9,8},{10,9... | collective-permute-start | bytes 3145736 | tf_op jit(solution)/shard_map/ppermute | solution.py:42
  247.8 46.5 %collective-permute-start.2 = (f32[64,32,128]{2,1,0:T(8,128)S(1)}, f32[64,32,128]{2,1,0:T(8,128)S(1)}, u32[]{:S(2)}, u32[]{:S(2)}) collective-permute-start(f32[64,32,128]{2,1,0:T(8,128)S(1)} %bitcast.84), channel_id=1, source_target_pairs={{0,1},{1,2},{2,3},{3,4},{4,5},{5,6},{6,7},{7,8},{8,9},{9,10},{10,1... | collective-permute-start | bytes 3145736 | tf_op jit(solution)/shard_map/ppermute | solution.py:42

commit v7 on v4

--- a/solution.py
+++ b/solution.py
@@ -111,7 +111,7 @@
     return (eye[:, :, None, None] * matrix.astype(dtype)[None, None]).reshape(parts, parts * rows, cols)
 
 
-def network(packed, predictors, weighting, bias_in, bias_offset, bias_out, levels, rows=256):
+def network(packed, predictors, weighting, bias_in, bias_offset, bias_out, levels, rows=512):
     total_rows, lanes = packed.shape
     assert total_rows % rows == 0
     parts = lanes // levels

time: 287 us -> 290 us (1.010)
  no operation moved by 1% of the time
where the time goes in v7:
time: 290 us; the launch traced here: 289 us
  waiting for transfers between devices  102 us (35%)
  starting transfers between devices  56.9 us (20%)
  local copies, waits for them, and re-layouts  39.6 us (14%)
  blocking collectives  38.8 us (13%)
  Pallas kernels  28.6 us (10%)
  other arithmetic  12.3 us (4%)
  matrix products  9.41 us (3%)
    ppermute x4, waiting for transfers between devices, ring_shift(): return lax.ppermute(block, axis, pairs)  78.5 us
    all_to_all x1, blocking collectives, shards(): lax.all_to_all(returning, 'mem', split_axis=0, concat_axis=0, tiled=True)  38.8 us
    ppermute x4, starting transfers between devices, ring_shift(): return lax.ppermute(block, axis, pairs)  34.6 us
    pallas_call x1, Pallas kernels, network(): pl.pallas_call(network_kernel, out_shape=jax.ShapeDtypeStruct((total_rows...  28.6 us
    all_to_all x1, waiting for transfers between devices, shards(): lax.all_to_all(outgoing, 'mem', split_axis=0, concat_axis=0, tiled=True)  23.7 us
    all_to_all x1, starting transfers between devices, shards(): lax.all_to_all(outgoing, 'mem', split_axis=0, concat_axis=0, tiled=True)  22.3 us
    reshape x2, local copies, waits for them, and re-layouts, shards(): jnp.transpose(outgoing, (1, 3, 0, 4, 2))  6.72 us
    transpose x1, local copies, waits for them, and re-layouts, shards(): jnp.transpose(restored, (2, 0, 4, 1, 3))  6.39 us
  transfers between devices with their start and end apart: 5, of which 5 were waited for; matrix products, arithmetic and copies ran while one was open for 2% of the time, Pallas kernels for 0%

profile of v7, /device:TPU:512, one launch (start us, length us, event | category | flops | bytes accessed | tf_op | source)
XLA Modules:
  0.0 289.1 jit_solution(13457359248569397516)
XLA Ops:
  0.0 0.7 fusion.37
  0.7 1.8 fusion.36
  2.6 2.1 collective-permute-start.1
  4.8 2.4 collective-permute-start
  7.2 21.5 %collective-permute-done.1 = f32[65,32,128]{2,1,0:T(8,128)S(1)} collective-permute-done((f32[65,32,128]{2,1,0:T(8,128)S(1)}, f32[65,32,128]{2,1,0:T(8,128)S(1)}, u32[]{:S(2)}, u32[]{:S(2)}) %collective-permute-start.1) | collective-permute-done | bytes 1064992 | tf_op jit(solution)/shard_map/ppermute | solution.py:42
  28.7 12.5 %collective-permute-done = f32[65,32,128]{2,1,0:T(8,128)S(1)} collective-permute-done((f32[65,32,128]{2,1,0:T(8,128)S(1)}, f32[65,32,128]{2,1,0:T(8,128)S(1)}, u32[]{:S(2)}, u32[]{:S(2)}) %collective-permute-start) | collective-permute-done | bytes 1064992 | tf_op jit(solution)/shard_map/ppermute | solution.py:42
  41.4 1.3 copy-done.3
  42.7 1.0 multiply_add_fusion.1
  43.8 0.5 multiply_add_fusion.2
  44.2 4.0 %copy.23 = f32[32,3,32,128]{2,3,1,0:T(8,128)} copy(f32[32,3,32,128]{3,2,1,0:T(8,128)S(1)} %multiply_add_fusion.2) | data formatting | bytes 3145728 | tf_op jit(solution)/shard_map/add | solution.py:47
  48.2 4.7 %reshape.234 = f32[24,32,512]{2,0,1:T(8,128)S(1)} reshape(f32[3,8,32,16,32]{4,3,1,0,2:T(8,128)} %bitcast.72) | data formatting | bytes 3145728 | tf_op jit(solution)/shard_map/reshape | solution.py:231
  52.9 2.1 copy.30
  55.0 22.3 %all-to-all-start = ((f32[24,32,512]{2,1,0:T(8,128)}), f32[24,32,512]{2,1,0:T(8,128)S(1)}, u32[]{:S(2)}, u32[]{:S(2)}) async-start(f32[24,32,512]{2,1,0:T(8,128)} %copy.30), calls=%async_computation | async-start | bytes 3145728 | tf_op jit(solution)/shard_map/all_to_all | solution.py:234
  78.0 0.7 copy.26.w_phys_ref
  79.1 0.9 broadcast_multiply_fusion.2.w_pred_ref
  80.0 1.1 broadcast_multiply_fusion.w_out_ref
  81.1 1.1 broadcast_multiply_fusion.1.w_prof_ref
  82.2 23.7 %all-to-all-done = f32[24,32,512]{2,1,0:T(8,128)S(1)} async-done(((f32[24,32,512]{2,1,0:T(8,128)}), f32[24,32,512]{2,1,0:T(8,128)S(1)}, u32[]{:S(2)}, u32[]{:S(2)}) %all-to-all-start) | async-done | bytes 1572896 | tf_op jit(solution)/shard_map/all_to_all | solution.py:234
  106.0 1.3 reshape_reshape.3.x_ref
  107.3 0.3 copy-done
  107.6 0.7 tile.11
  108.3 28.6 %shard_map.109 = f32[3072,128]{1,0:T(8,128)} custom-call(f32[3072,128]{1,0:T(8,128)} %reshape_reshape.3.x_ref, bf16[512,64]{1,0:T(8,128)(2,1)} %bitcast.90, bf16[4,128,1024]{2,1,0:T(8,128)(2,1)} %broadcast_multiply_fusion.1.w_prof_ref, bf16[4,64,1024]{2,1,0:T(8,128)(2,1)} %broadcast_multiply_fusion.2.w_pred_ref, f32[1,1024]{1,0:T(1,128)} %bitcast.100, ...), custom_call_target="tpu_custom_call" | custom-call | flops 8053063680 | bytes 3145728 | tf_op jit(solution)/shard_map/pallas_call | solution.py:135
  136.9 2.6 reshape.213
  139.4 1.9 copy.27
  141.3 1.1 gather_fusion
  142.8 0.3 convolution_reduce_fusion
  143.2 0.3 fusion.11
  143.4 1.1 fusion.12
  145.2 1.9 add_divide_fusion
  147.9 0.3 fusion.15
  148.4 0.3 fusion.17
  149.0 0.3 fusion.19
  149.5 0.3 fusion.21
  150.2 0.9 fusion.38
  151.1 0.6 copy-done.2
  151.7 2.1 fusion.6
  153.8 2.1 fusion.3
  155.8 2.2 add_add_fusion
  158.1 38.8 %all_to_all.10 = f32[24,32,512]{2,1,0:T(8,128)S(1)} all-to-all(f32[24,32,512]{2,1,0:T(8,128)S(1)} %bitcast.79), channel_id=1, replica_groups=mesh['mem'=24,'lon'=32] {'mem'}, dimensions={0} | all-to-all | bytes 3145728 | tf_op jit(solution)/shard_map/all_to_all | solution.py:251
  196.9 3.8 %reshape.216 = f32[3,8,32,16,32]{4,3,2,1,0:T(8,128)} reshape(f32[24,32,512]{2,1,0:T(8,128)S(1)} %all_to_all.10) | data formatting | bytes 3145728 | tf_op jit(solution)/shard_map/reshape | solution.py:252
  200.6 6.4 %copy.28 = f32[32,3,32,8,16]{2,4,3,1,0:T(8,128)} copy(f32[32,3,32,8,16]{2,4,0,3,1:T(8,128)} %bitcast.70) | data formatting | bytes 3145728 | tf_op jit(solution)/shard_map/transpose | solution.py:253
  207.0 4.4 %copy.29 = f32[32,3,32,128]{3,2,1,0:T(8,128)S(1)} copy(f32[32,3,32,128]{2,3,1,0:T(8,128)} %bitcast.71) | data formatting | bytes 3145728 | tf_op jit(solution)/shard_map/reshape | solution.py:253
  211.6 28.3 %collective-permute-start.3 = (f32[64,32,128]{2,1,0:T(8,128)S(1)}, f32[64,32,128]{2,1,0:T(8,128)S(1)}, u32[]{:S(2)}, u32[]{:S(2)}) collective-permute-start(f32[64,32,128]{2,1,0:T(8,128)S(1)} %bitcast.85), channel_id=1, source_target_pairs={{0,31},{1,0},{2,1},{3,2},{4,3},{5,4},{6,5},{7,6},{8,7},{9,8},{10,9... | collective-permute-start | bytes 3145736 | tf_op jit(solution)/shard_map/ppermute | solution.py:42
  239.9 1.9 collective-permute-start.2
  241.8 32.3 %collective-permute-done.3 = f32[64,32,128]{2,1,0:T(8,128)S(1)} collective-permute-done((f32[64,32,128]{2,1,0:T(8,128)S(1)}, f32[64,32,128]{2,1,0:T(8,128)S(1)}, u32[]{:S(2)}, u32[]{:S(2)}) %collective-permute-start.3) | collective-permute-done | bytes 1048608 | tf_op jit(solution)/shard_map/ppermute | solution.py:42
  274.1 12.3 %collective-permute-done.2 = f32[64,32,128]{2,1,0:T(8,128)S(1)} collective-permute-done((f32[64,32,128]{2,1,0:T(8,128)S(1)}, f32[64,32,128]{2,1,0:T(8,128)S(1)}, u32[]{:S(2)}, u32[]{:S(2)}) %collective-permute-start.2) | collective-permute-done | bytes 1048608 | tf_op jit(solution)/shard_map/ppermute | solution.py:42
  286.4 1.0 multiply_add_fusion
  287.5 1.6 add_bitcast_fusion
  (75 shorter events, 3.9 us)
Async XLA Ops:
  2.6 4.6 %copy-start.4 = (f32[32,3,128]{2,0,1:T(8,128)S(1)}, f32[32,3,128]{2,0,1:T(8,128)}, u32[]{:S(2)}) copy-start(f32[32,3,128]{2,0,1:T(8,128)} %param.12) | copy-start | bytes 147460
  2.6 26.0 %collective-permute-start.1 = (f32[65,32,128]{2,1,0:T(8,128)S(1)}, f32[65,32,128]{2,1,0:T(8,128)S(1)}, u32[]{:S(2)}, u32[]{:S(2)}) collective-permute-start(f32[65,32,128]{2,1,0:T(8,128)S(1)} %pad_maximum_fusion.9), channel_id=1, source_target_pairs={{0,31},{1,0},{2,1},{3,2},{4,3},{5,4},{6,5},{7,6},{8,7},{9,8},{10,9... | collective-permute-start | bytes 3194888 | tf_op jit(solution)/shard_map/ppermute | solution.py:42
  4.8 36.4 %collective-permute-start = (f32[65,32,128]{2,1,0:T(8,128)S(1)}, f32[65,32,128]{2,1,0:T(8,128)S(1)}, u32[]{:S(2)}, u32[]{:S(2)}) collective-permute-start(f32[65,32,128]{2,1,0:T(8,128)S(1)} %pad_maximum_fusion.8), channel_id=1, source_target_pairs={{0,1},{1,2},{2,3},{3,4},{4,5},{5,6},{6,7},{7,8},{8,9},{9,10},{10,1... | collective-permute-start | bytes 3194888 | tf_op jit(solution)/shard_map/ppermute | solution.py:42
  41.3 1.4 copy-start.3
  54.9 22.4 %copy-start.8 = (bf16[1,1,16,16]{3,2,1,0:T(8,128)(2,1)S(1)}, bf16[1,1,16,16]{3,2,1,0:T(8,128)(2,1)}, u32[]{:S(2)}) copy-start(bf16[1,1,16,16]{3,2,1,0:T(8,128)(2,1)} %param.17) | copy-start | bytes 1540
  54.9 23.0 %copy-start.6 = (f32[32,32]{1,0:T(8,128)S(1)}, f32[32,32]{1,0:T(8,128)}, u32[]{:S(2)}) copy-start(f32[32,32]{1,0:T(8,128)} %param.13) | copy-start | bytes 12292
  54.9 23.8 %copy-start.5 = (bf16[1024,32]{0,1:T(8,128)(2,1)S(1)}, bf16[1024,32]{0,1:T(8,128)(2,1)}, u32[]{:S(2)}) copy-start(bf16[1024,32]{0,1:T(8,128)(2,1)} %param.16) | copy-start | bytes 196612
  54.9 24.0 %copy-start.7 = (s32[1,1,256]{2,1,0:T(1,128)S(1)}, s32[1,1,256]{2,1,0:T(1,128)}, u32[]{:S(2)}) copy-start(s32[1,1,256]{2,1,0:T(1,128)} %param.19) | copy-start | bytes 3076
  54.9 24.0 %copy-start.9 = (s32[1,1,256]{2,1,0:T(1,128)S(1)}, s32[1,1,256]{2,1,0:T(1,128)}, u32[]{:S(2)}) copy-start(s32[1,1,256]{2,1,0:T(1,128)} %param.18) | copy-start | bytes 3076
  54.9 24.1 %copy-start.11 = (f32[32]{0:T(128)S(1)}, f32[32]{0:T(128)}, u32[]{:S(2)}) copy-start(f32[32]{0:T(128)} %param.21) | copy-start | bytes 388
  54.9 24.2 %slice-start = ((bf16[48,1024]{1,0:T(8,128)(2,1)}), bf16[16,1024]{1,0:T(8,128)(2,1)S(1)}, s32[]{:S(2)}) async-start(bf16[48,1024]{1,0:T(8,128)(2,1)} %param.14), calls=%async_computation.2 | async-start | bytes 65536 | tf_op jit(solution)/shard_map/slice | solution.py:122
  55.0 51.0 %all-to-all-start = ((f32[24,32,512]{2,1,0:T(8,128)}), f32[24,32,512]{2,1,0:T(8,128)S(1)}, u32[]{:S(2)}, u32[]{:S(2)}) async-start(f32[24,32,512]{2,1,0:T(8,128)} %copy.30), calls=%async_computation | async-start | bytes 3145728 | tf_op jit(solution)/shard_map/all_to_all | solution.py:234
  78.0 3.1 %slice-start.1 = ((bf16[48,1024]{1,0:T(8,128)(2,1)}), bf16[32,1024]{1,0:T(8,128)(2,1)S(1)}, s32[]{:S(2)}) async-start(bf16[48,1024]{1,0:T(8,128)(2,1)} %param.14), calls=%async_computation.3 | async-start | bytes 131072 | tf_op jit(solution)/shard_map/slice | solution.py:121
  106.0 1.7 copy-start
  141.3 1.3 copy-start.10
  145.2 1.9 copy-start.1
  150.0 1.7 copy-start.2
  211.6 62.5 %collective-permute-start.3 = (f32[64,32,128]{2,1,0:T(8,128)S(1)}, f32[64,32,128]{2,1,0:T(8,128)S(1)}, u32[]{:S(2)}, u32[]{:S(2)}) collective-permute-start(f32[64,32,128]{2,1,0:T(8,128)S(1)} %bitcast.85), channel_id=1, source_target_pairs={{0,31},{1,0},{2,1},{3,2},{4,3},{5,4},{6,5},{7,6},{8,7},{9,8},{10,9... | collective-permute-start | bytes 3145736 | tf_op jit(solution)/shard_map/ppermute | solution.py:42
  239.9 46.5 %collective-permute-start.2 = (f32[64,32,128]{2,1,0:T(8,128)S(1)}, f32[64,32,128]{2,1,0:T(8,128)S(1)}, u32[]{:S(2)}, u32[]{:S(2)}) collective-permute-start(f32[64,32,128]{2,1,0:T(8,128)S(1)} %bitcast.84), channel_id=1, source_target_pairs={{0,1},{1,2},{2,3},{3,4},{4,5},{5,6},{6,7},{7,8},{8,9},{9,10},{10,1... | collective-permute-start | bytes 3145736 | tf_op jit(solution)/shard_map/ppermute | solution.py:42

commit v8 on v7

--- a/solution.py
+++ b/solution.py
@@ -111,7 +111,7 @@
     return (eye[:, :, None, None] * matrix.astype(dtype)[None, None]).reshape(parts, parts * rows, cols)
 
 
-def network(packed, predictors, weighting, bias_in, bias_offset, bias_out, levels, rows=512):
+def network(packed, predictors, weighting, bias_in, bias_offset, bias_out, levels, rows=128):
     total_rows, lanes = packed.shape
     assert total_rows % rows == 0
     parts = lanes // levels

time: 290 us -> 296 us (1.021)
  Pallas kernels: 28.6 us -> 34.9 us
    pallas_call x1, Pallas kernels: 28.6 us -> 34.9 us  [network(): pl.pallas_call(network_kernel, out_shape=jax.ShapeDtypeStruct((total_rows...]
where the time goes in v8:
time: 296 us; the launch traced here: 295 us
  waiting for transfers between devices  102 us (34%)
  starting transfers between devices  57 us (19%)
  local copies, waits for them, and re-layouts  39.5 us (13%)
  blocking collectives  38.8 us (13%)
  Pallas kernels  34.9 us (12%)
  other arithmetic  12.3 us (4%)
  matrix products  9.41 us (3%)
    ppermute x4, waiting for transfers between devices, ring_shift(): return lax.ppermute(block, axis, pairs)  78.5 us
    all_to_all x1, blocking collectives, shards(): lax.all_to_all(returning, 'mem', split_axis=0, concat_axis=0, tiled=True)  38.8 us
    pallas_call x1, Pallas kernels, network(): pl.pallas_call(network_kernel, out_shape=jax.ShapeDtypeStruct((total_rows...  34.9 us
    ppermute x4, starting transfers between devices, ring_shift(): return lax.ppermute(block, axis, pairs)  34.6 us
    all_to_all x1, waiting for transfers between devices, shards(): lax.all_to_all(outgoing, 'mem', split_axis=0, concat_axis=0, tiled=True)  23.7 us
    all_to_all x1, starting transfers between devices, shards(): lax.all_to_all(outgoing, 'mem', split_axis=0, concat_axis=0, tiled=True)  22.3 us
    reshape x2, local copies, waits for them, and re-layouts, shards(): jnp.transpose(outgoing, (1, 3, 0, 4, 2))  6.72 us
    transpose x1, local copies, waits for them, and re-layouts, shards(): jnp.transpose(restored, (2, 0, 4, 1, 3))  6.39 us
  transfers between devices with their start and end apart: 5, of which 5 were waited for; matrix products, arithmetic and copies ran while one was open for 2% of the time, Pallas kernels for 0%

profile of v8, /device:TPU:512, one launch (start us, length us, event | category | flops | bytes accessed | tf_op | source)
XLA Modules:
  0.0 295.4 jit_solution(12457017868733382177)
XLA Ops:
  0.0 0.7 fusion.37
  0.7 1.8 fusion.36
  2.6 2.1 collective-permute-start.1
  4.8 2.4 collective-permute-start
  7.2 21.5 %collective-permute-done.1 = f32[65,32,128]{2,1,0:T(8,128)S(1)} collective-permute-done((f32[65,32,128]{2,1,0:T(8,128)S(1)}, f32[65,32,128]{2,1,0:T(8,128)S(1)}, u32[]{:S(2)}, u32[]{:S(2)}) %collective-permute-start.1) | collective-permute-done | bytes 1064992 | tf_op jit(solution)/shard_map/ppermute | solution.py:42
  28.7 12.5 %collective-permute-done = f32[65,32,128]{2,1,0:T(8,128)S(1)} collective-permute-done((f32[65,32,128]{2,1,0:T(8,128)S(1)}, f32[65,32,128]{2,1,0:T(8,128)S(1)}, u32[]{:S(2)}, u32[]{:S(2)}) %collective-permute-start) | collective-permute-done | bytes 1064992 | tf_op jit(solution)/shard_map/ppermute | solution.py:42
  41.4 1.3 copy-done.3
  42.7 1.0 multiply_add_fusion.1
  43.8 0.5 multiply_add_fusion.2
  44.2 4.0 %copy.23 = f32[32,3,32,128]{2,3,1,0:T(8,128)} copy(f32[32,3,32,128]{3,2,1,0:T(8,128)S(1)} %multiply_add_fusion.2) | data formatting | bytes 3145728 | tf_op jit(solution)/shard_map/add | solution.py:47
  48.2 4.7 %reshape.234 = f32[24,32,512]{2,0,1:T(8,128)S(1)} reshape(f32[3,8,32,16,32]{4,3,1,0,2:T(8,128)} %bitcast.72) | data formatting | bytes 3145728 | tf_op jit(solution)/shard_map/reshape | solution.py:231
  52.9 2.1 copy.30
  55.0 22.3 %all-to-all-start = ((f32[24,32,512]{2,1,0:T(8,128)}), f32[24,32,512]{2,1,0:T(8,128)S(1)}, u32[]{:S(2)}, u32[]{:S(2)}) async-start(f32[24,32,512]{2,1,0:T(8,128)} %copy.30), calls=%async_computation | async-start | bytes 3145728 | tf_op jit(solution)/shard_map/all_to_all | solution.py:234
  78.0 0.7 copy.26.w_phys_ref
  79.1 0.9 broadcast_multiply_fusion.2.w_pred_ref
  80.0 1.1 broadcast_multiply_fusion.w_out_ref
  81.1 1.1 broadcast_multiply_fusion.1.w_prof_ref
  82.2 23.7 %all-to-all-done = f32[24,32,512]{2,1,0:T(8,128)S(1)} async-done(((f32[24,32,512]{2,1,0:T(8,128)}), f32[24,32,512]{2,1,0:T(8,128)S(1)}, u32[]{:S(2)}, u32[]{:S(2)}) %all-to-all-start) | async-done | bytes 1572896 | tf_op jit(solution)/shard_map/all_to_all | solution.py:234
  106.0 1.3 reshape_reshape.3.x_ref
  107.3 0.3 copy-done
  107.6 0.6 tile.11
  108.2 34.9 %shard_map.109 = f32[3072,128]{1,0:T(8,128)} custom-call(f32[3072,128]{1,0:T(8,128)} %reshape_reshape.3.x_ref, bf16[128,64]{1,0:T(8,128)(2,1)} %bitcast.90, bf16[4,128,1024]{2,1,0:T(8,128)(2,1)} %broadcast_multiply_fusion.1.w_prof_ref, bf16[4,64,1024]{2,1,0:T(8,128)(2,1)} %broadcast_multiply_fusion.2.w_pred_ref, f32[1,1024]{1,0:T(1,128)} %bitcast.100, ...), custom_call_target="tpu_custom_call" | custom-call | flops 8053063680 | bytes 3145728 | tf_op jit(solution)/shard_map/pallas_call | solution.py:135
  143.1 2.6 reshape.213
  145.7 1.9 copy.27
  147.6 1.1 gather_fusion
  149.1 0.3 convolution_reduce_fusion
  149.7 1.1 fusion.12
  151.5 1.9 add_divide_fusion
  153.6 0.3 fusion.13
  154.1 0.3 fusion.15
  154.7 0.3 fusion.17
  155.2 0.3 fusion.19
  155.7 0.3 fusion.21
  156.5 0.9 fusion.38
  157.4 0.6 copy-done.2
  158.0 2.1 fusion.6
  160.0 2.1 fusion.3
  162.1 2.2 add_add_fusion
  164.3 38.8 %all_to_all.10 = f32[24,32,512]{2,1,0:T(8,128)S(1)} all-to-all(f32[24,32,512]{2,1,0:T(8,128)S(1)} %bitcast.79), channel_id=1, replica_groups=mesh['mem'=24,'lon'=32] {'mem'}, dimensions={0} | all-to-all | bytes 3145728 | tf_op jit(solution)/shard_map/all_to_all | solution.py:251
  203.1 3.8 %reshape.216 = f32[3,8,32,16,32]{4,3,2,1,0:T(8,128)} reshape(f32[24,32,512]{2,1,0:T(8,128)S(1)} %all_to_all.10) | data formatting | bytes 3145728 | tf_op jit(solution)/shard_map/reshape | solution.py:252
  206.9 6.4 %copy.28 = f32[32,3,32,8,16]{2,4,3,1,0:T(8,128)} copy(f32[32,3,32,8,16]{2,4,0,3,1:T(8,128)} %bitcast.70) | data formatting | bytes 3145728 | tf_op jit(solution)/shard_map/transpose | solution.py:253
  213.3 4.4 %copy.29 = f32[32,3,32,128]{3,2,1,0:T(8,128)S(1)} copy(f32[32,3,32,128]{2,3,1,0:T(8,128)} %bitcast.71) | data formatting | bytes 3145728 | tf_op jit(solution)/shard_map/reshape | solution.py:253
  217.9 28.3 %collective-permute-start.3 = (f32[64,32,128]{2,1,0:T(8,128)S(1)}, f32[64,32,128]{2,1,0:T(8,128)S(1)}, u32[]{:S(2)}, u32[]{:S(2)}) collective-permute-start(f32[64,32,128]{2,1,0:T(8,128)S(1)} %bitcast.85), channel_id=1, source_target_pairs={{0,31},{1,0},{2,1},{3,2},{4,3},{5,4},{6,5},{7,6},{8,7},{9,8},{10,9... | collective-permute-start | bytes 3145736 | tf_op jit(solution)/shard_map/ppermute | solution.py:42
  246.2 1.9 collective-permute-start.2
  248.1 32.3 %collective-permute-done.3 = f32[64,32,128]{2,1,0:T(8,128)S(1)} collective-permute-done((f32[64,32,128]{2,1,0:T(8,128)S(1)}, f32[64,32,128]{2,1,0:T(8,128)S(1)}, u32[]{:S(2)}, u32[]{:S(2)}) %collective-permute-start.3) | collective-permute-done | bytes 1048608 | tf_op jit(solution)/shard_map/ppermute | solution.py:42
  280.4 12.3 %collective-permute-done.2 = f32[64,32,128]{2,1,0:T(8,128)S(1)} collective-permute-done((f32[64,32,128]{2,1,0:T(8,128)S(1)}, f32[64,32,128]{2,1,0:T(8,128)S(1)}, u32[]{:S(2)}, u32[]{:S(2)}) %collective-permute-start.2) | collective-permute-done | bytes 1048608 | tf_op jit(solution)/shard_map/ppermute | solution.py:42
  292.7 1.0 multiply_add_fusion
  293.8 1.6 add_bitcast_fusion
  (75 shorter events, 3.9 us)
Async XLA Ops:
  2.6 4.6 %copy-start.4 = (f32[32,3,128]{2,0,1:T(8,128)S(1)}, f32[32,3,128]{2,0,1:T(8,128)}, u32[]{:S(2)}) copy-start(f32[32,3,128]{2,0,1:T(8,128)} %param.12) | copy-start | bytes 147460
  2.6 26.0 %collective-permute-start.1 = (f32[65,32,128]{2,1,0:T(8,128)S(1)}, f32[65,32,128]{2,1,0:T(8,128)S(1)}, u32[]{:S(2)}, u32[]{:S(2)}) collective-permute-start(f32[65,32,128]{2,1,0:T(8,128)S(1)} %pad_maximum_fusion.9), channel_id=1, source_target_pairs={{0,31},{1,0},{2,1},{3,2},{4,3},{5,4},{6,5},{7,6},{8,7},{9,8},{10,9... | collective-permute-start | bytes 3194888 | tf_op jit(solution)/shard_map/ppermute | solution.py:42
  4.8 36.4 %collective-permute-start = (f32[65,32,128]{2,1,0:T(8,128)S(1)}, f32[65,32,128]{2,1,0:T(8,128)S(1)}, u32[]{:S(2)}, u32[]{:S(2)}) collective-permute-start(f32[65,32,128]{2,1,0:T(8,128)S(1)} %pad_maximum_fusion.8), channel_id=1, source_target_pairs={{0,1},{1,2},{2,3},{3,4},{4,5},{5,6},{6,7},{7,8},{8,9},{9,10},{10,1... | collective-permute-start | bytes 3194888 | tf_op jit(solution)/shard_map/ppermute | solution.py:42
  41.3 1.4 copy-start.3
  54.9 22.4 %copy-start.8 = (bf16[1,1,16,16]{3,2,1,0:T(8,128)(2,1)S(1)}, bf16[1,1,16,16]{3,2,1,0:T(8,128)(2,1)}, u32[]{:S(2)}) copy-start(bf16[1,1,16,16]{3,2,1,0:T(8,128)(2,1)} %param.17) | copy-start | bytes 1540
  54.9 23.0 %copy-start.6 = (f32[32,32]{1,0:T(8,128)S(1)}, f32[32,32]{1,0:T(8,128)}, u32[]{:S(2)}) copy-start(f32[32,32]{1,0:T(8,128)} %param.13) | copy-start | bytes 12292
  54.9 23.8 %copy-start.5 = (bf16[1024,32]{0,1:T(8,128)(2,1)S(1)}, bf16[1024,32]{0,1:T(8,128)(2,1)}, u32[]{:S(2)}) copy-start(bf16[1024,32]{0,1:T(8,128)(2,1)} %param.16) | copy-start | bytes 196612
  54.9 24.0 %copy-start.7 = (s32[1,1,256]{2,1,0:T(1,128)S(1)}, s32[1,1,256]{2,1,0:T(1,128)}, u32[]{:S(2)}) copy-start(s32[1,1,256]{2,1,0:T(1,128)} %param.19) | copy-start | bytes 3076
  54.9 24.0 %copy-start.9 = (s32[1,1,256]{2,1,0:T(1,128)S(1)}, s32[1,1,256]{2,1,0:T(1,128)}, u32[]{:S(2)}) copy-start(s32[1,1,256]{2,1,0:T(1,128)} %param.18) | copy-start | bytes 3076
  54.9 24.1 %copy-start.11 = (f32[32]{0:T(128)S(1)}, f32[32]{0:T(128)}, u32[]{:S(2)}) copy-start(f32[32]{0:T(128)} %param.21) | copy-start | bytes 388
  54.9 24.2 %slice-start = ((bf16[48,1024]{1,0:T(8,128)(2,1)}), bf16[16,1024]{1,0:T(8,128)(2,1)S(1)}, s32[]{:S(2)}) async-start(bf16[48,1024]{1,0:T(8,128)(2,1)} %param.14), calls=%async_computation.2 | async-start | bytes 65536 | tf_op jit(solution)/shard_map/slice | solution.py:122
  55.0 51.0 %all-to-all-start = ((f32[24,32,512]{2,1,0:T(8,128)}), f32[24,32,512]{2,1,0:T(8,128)S(1)}, u32[]{:S(2)}, u32[]{:S(2)}) async-start(f32[24,32,512]{2,1,0:T(8,128)} %copy.30), calls=%async_computation | async-start | bytes 3145728 | tf_op jit(solution)/shard_map/all_to_all | solution.py:234
  78.0 3.1 %slice-start.1 = ((bf16[48,1024]{1,0:T(8,128)(2,1)}), bf16[32,1024]{1,0:T(8,128)(2,1)S(1)}, s32[]{:S(2)}) async-start(bf16[48,1024]{1,0:T(8,128)(2,1)} %param.14), calls=%async_computation.3 | async-start | bytes 131072 | tf_op jit(solution)/shard_map/slice | solution.py:121
  106.0 1.7 copy-start
  147.6 1.3 copy-start.10
  151.5 1.9 copy-start.1
  156.3 1.7 copy-start.2
  217.9 62.5 %collective-permute-start.3 = (f32[64,32,128]{2,1,0:T(8,128)S(1)}, f32[64,32,128]{2,1,0:T(8,128)S(1)}, u32[]{:S(2)}, u32[]{:S(2)}) collective-permute-start(f32[64,32,128]{2,1,0:T(8,128)S(1)} %bitcast.85), channel_id=1, source_target_pairs={{0,31},{1,0},{2,1},{3,2},{4,3},{5,4},{6,5},{7,6},{8,7},{9,8},{10,9... | collective-permute-start | bytes 3145736 | tf_op jit(solution)/shard_map/ppermute | solution.py:42
  246.2 46.5 %collective-permute-start.2 = (f32[64,32,128]{2,1,0:T(8,128)S(1)}, f32[64,32,128]{2,1,0:T(8,128)S(1)}, u32[]{:S(2)}, u32[]{:S(2)}) collective-permute-start(f32[64,32,128]{2,1,0:T(8,128)S(1)} %bitcast.84), channel_id=1, source_target_pairs={{0,1},{1,2},{2,3},{3,4},{4,5},{5,6},{6,7},{7,8},{8,9},{9,10},{10,1... | collective-permute-start | bytes 3145736 | tf_op jit(solution)/shard_map/ppermute | solution.py:42

commit v9 on v4

--- a/solution.py
+++ b/solution.py
@@ -92,7 +92,9 @@
     return result
 
 
-def network_kernel(x_ref, pred_ref, w_prof_ref, w_pred_ref, offset_ref, w_out_ref, w_phys_ref, out_ref):
+def network_kernel(
+    x_ref, pred_ref, w_prof_ref, w_pred_ref, offset_ref, w_out_ref, w_phys_ref, out_ref, staged_ref
+):
     x = x_ref[...]
     narrow = x.astype(jnp.bfloat16)
     extra = pred_ref[...]
@@ -102,7 +104,13 @@
         pre = pre + jnp.dot(extra, w_pred_ref[part], preferred_element_type=jnp.float32)
         hidden = jnp.tanh(pre + offset_ref[...]).astype(jnp.bfloat16)
         total = total + jnp.dot(hidden, w_out_ref[part], preferred_element_type=jnp.float32)
-    out_ref[...] = total
+    rows, lanes = total.shape
+    groups = out_ref.shape[1] // lanes
+    staged_ref[...] = total
+    for group in range(groups):
+        out_ref[:, group * lanes : (group + 1) * lanes] = staged_ref[
+            pl.ds(group, rows // groups, stride=groups), :
+        ]
 
 
 def block_diagonal(matrix, parts, dtype):
@@ -134,7 +142,9 @@
     const3 = lambda i: (0, 0, 0)
     return pl.pallas_call(
         network_kernel,
-        out_shape=jax.ShapeDtypeStruct((total_rows, parts * channels), jnp.float32),
+        out_shape=jax.ShapeDtypeStruct(
+            (total_rows // column_groups, column_groups * parts * channels), jnp.float32
+        ),
         grid=(total_rows // rows,),
         in_specs=[
             pl.BlockSpec((rows, lanes), lambda i: (i, 0)),
@@ -145,7 +155,10 @@
             pl.BlockSpec((parts, hid, parts * channels), const3),
             pl.BlockSpec((lanes, parts * channels), const),
         ],
-        out_specs=pl.BlockSpec((rows, parts * channels), lambda i: (i, 0)),
+        out_specs=pl.BlockSpec(
+            (rows // column_groups, column_groups * parts * channels), lambda i: (i, 0)
+        ),
+        scratch_shapes=[pltpu.VMEM((rows, parts * channels), jnp.float32)],
         cost_estimate=pl.CostEstimate(
             flops=2 * total_rows * parts * hid * (lanes + parts * npred + parts * channels),
             transcendentals=total_rows * parts * hid,

time: 287 us -> 285 us (level)
    reshape x2 -> x0, local copies, waits for them, and re-layouts: 4.43 us -> none  [analyse(): table = evolved.reshape(members, columns * channels)]
where the time goes in v9:
time: 285 us; the launch traced here: 284 us
  waiting for transfers between devices  102 us (36%)
  starting transfers between devices  56.9 us (20%)
  blocking collectives  38.8 us (14%)
  local copies, waits for them, and re-layouts  37 us (13%)
  Pallas kernels  26.3 us (9%)
  other arithmetic  12.3 us (4%)
  matrix products  9.41 us (3%)
    ppermute x4, waiting for transfers between devices, ring_shift(): return lax.ppermute(block, axis, pairs)  78.5 us
    all_to_all x1, blocking collectives, shards(): lax.all_to_all(returning, 'mem', split_axis=0, concat_axis=0, tiled=True)  38.8 us
    ppermute x4, starting transfers between devices, ring_shift(): return lax.ppermute(block, axis, pairs)  34.6 us
    pallas_call x1, Pallas kernels, network(): pl.pallas_call(network_kernel, out_shape=jax.ShapeDtypeStruct((total_rows...  26.3 us
    all_to_all x1, waiting for transfers between devices, shards(): lax.all_to_all(outgoing, 'mem', split_axis=0, concat_axis=0, tiled=True)  23.7 us
    all_to_all x1, starting transfers between devices, shards(): lax.all_to_all(outgoing, 'mem', split_axis=0, concat_axis=0, tiled=True)  22.3 us
    reshape x2, local copies, waits for them, and re-layouts, shards(): jnp.transpose(outgoing, (1, 3, 0, 4, 2))  6.72 us
    transpose x1, local copies, waits for them, and re-layouts, shards(): jnp.transpose(restored, (2, 0, 4, 1, 3))  6.39 us
  transfers between devices with their start and end apart: 5, of which 5 were waited for; matrix products, arithmetic and copies ran while one was open for 2% of the time, Pallas kernels for 0%

profile of v9, /device:TPU:512, one launch (start us, length us, event | category | flops | bytes accessed | tf_op | source)
XLA Modules:
  0.0 284.2 jit_solution(11278813459350929940)
XLA Ops:
  0.0 0.7 fusion.37
  0.7 1.8 fusion.36
  2.6 2.1 collective-permute-start.1
  4.8 2.4 collective-permute-start
  7.2 21.5 %collective-permute-done.1 = f32[65,32,128]{2,1,0:T(8,128)S(1)} collective-permute-done((f32[65,32,128]{2,1,0:T(8,128)S(1)}, f32[65,32,128]{2,1,0:T(8,128)S(1)}, u32[]{:S(2)}, u32[]{:S(2)}) %collective-permute-start.1) | collective-permute-done | bytes 1064992 | tf_op jit(solution)/shard_map/ppermute | solution.py:42
  28.7 12.5 %collective-permute-done = f32[65,32,128]{2,1,0:T(8,128)S(1)} collective-permute-done((f32[65,32,128]{2,1,0:T(8,128)S(1)}, f32[65,32,128]{2,1,0:T(8,128)S(1)}, u32[]{:S(2)}, u32[]{:S(2)}) %collective-permute-start) | collective-permute-done | bytes 1064992 | tf_op jit(solution)/shard_map/ppermute | solution.py:42
  41.4 1.3 copy-done.3
  42.7 1.0 multiply_add_fusion.1
  43.8 0.5 multiply_add_fusion.2
  44.2 4.0 %copy.23 = f32[32,3,32,128]{2,3,1,0:T(8,128)} copy(f32[32,3,32,128]{3,2,1,0:T(8,128)S(1)} %multiply_add_fusion.2) | data formatting | bytes 3145728 | tf_op jit(solution)/shard_map/add | solution.py:47
  48.2 4.7 %reshape.230 = f32[24,32,512]{2,0,1:T(8,128)S(1)} reshape(f32[3,8,32,16,32]{4,3,1,0,2:T(8,128)} %bitcast.72) | data formatting | bytes 3145728 | tf_op jit(solution)/shard_map/reshape | solution.py:244
  52.9 2.1 copy.30
  55.0 22.3 %all-to-all-start = ((f32[24,32,512]{2,1,0:T(8,128)}), f32[24,32,512]{2,1,0:T(8,128)S(1)}, u32[]{:S(2)}, u32[]{:S(2)}) async-start(f32[24,32,512]{2,1,0:T(8,128)} %copy.30), calls=%async_computation | async-start | bytes 3145728 | tf_op jit(solution)/shard_map/all_to_all | solution.py:247
  78.0 0.7 copy.26.w_phys_ref
  79.1 0.9 broadcast_multiply_fusion.2.w_pred_ref
  80.0 1.1 broadcast_multiply_fusion.w_out_ref
  81.1 1.1 broadcast_multiply_fusion.1.w_prof_ref
  82.2 23.7 %all-to-all-done = f32[24,32,512]{2,1,0:T(8,128)S(1)} async-done(((f32[24,32,512]{2,1,0:T(8,128)}), f32[24,32,512]{2,1,0:T(8,128)S(1)}, u32[]{:S(2)}, u32[]{:S(2)}) %all-to-all-start) | async-done | bytes 1572896 | tf_op jit(solution)/shard_map/all_to_all | solution.py:247
  106.0 1.4 reshape_reshape.3.x_ref
  107.3 0.3 copy-done
  107.6 0.6 tile.11
  108.3 26.3 %shard_map.109 = f32[768,512]{1,0:T(8,128)} custom-call(f32[3072,128]{1,0:T(8,128)} %reshape_reshape.3.x_ref, bf16[256,64]{1,0:T(8,128)(2,1)} %bitcast.90, bf16[4,128,1024]{2,1,0:T(8,128)(2,1)} %broadcast_multiply_fusion.1.w_prof_ref, bf16[4,64,1024]{2,1,0:T(8,128)(2,1)} %broadcast_multiply_fusion.2.w_pred_ref, f32[1,1024]{1,0:T(1,128)} %bitcast.100, ...), custom_call_target="tpu_custom_call" | custom-call | flops 8053063680 | bytes 3145728 | tf_op jit(solution)/shard_map/pallas_call | solution.py:143
  134.6 1.9 copy.27
  136.4 1.1 gather_fusion
  138.0 0.3 convolution_reduce_fusion
  138.3 0.3 fusion.11
  138.6 1.1 fusion.12
  140.4 1.9 add_divide_fusion
  142.5 0.3 fusion.13
  143.0 0.3 fusion.15
  143.5 0.3 fusion.17
  144.1 0.3 fusion.19
  144.6 0.3 fusion.21
  145.4 0.9 fusion.38
  146.2 0.6 copy-done.2
  146.8 2.1 fusion.6
  148.9 2.1 fusion.3
  151.0 2.2 add_add_fusion
  153.2 38.8 %all_to_all.10 = f32[24,32,512]{2,1,0:T(8,128)S(1)} all-to-all(f32[24,32,512]{2,1,0:T(8,128)S(1)} %bitcast.79), channel_id=1, replica_groups=mesh['mem'=24,'lon'=32] {'mem'}, dimensions={0} | all-to-all | bytes 3145728 | tf_op jit(solution)/shard_map/all_to_all | solution.py:264
  192.0 3.8 %reshape.212 = f32[3,8,32,16,32]{4,3,2,1,0:T(8,128)} reshape(f32[24,32,512]{2,1,0:T(8,128)S(1)} %all_to_all.10) | data formatting | bytes 3145728 | tf_op jit(solution)/shard_map/reshape | solution.py:265
  195.8 6.4 %copy.28 = f32[32,3,32,8,16]{2,4,3,1,0:T(8,128)} copy(f32[32,3,32,8,16]{2,4,0,3,1:T(8,128)} %bitcast.70) | data formatting | bytes 3145728 | tf_op jit(solution)/shard_map/transpose | solution.py:266
  202.2 4.4 %copy.29 = f32[32,3,32,128]{3,2,1,0:T(8,128)S(1)} copy(f32[32,3,32,128]{2,3,1,0:T(8,128)} %bitcast.71) | data formatting | bytes 3145728 | tf_op jit(solution)/shard_map/reshape | solution.py:266
  206.8 28.2 %collective-permute-start.3 = (f32[64,32,128]{2,1,0:T(8,128)S(1)}, f32[64,32,128]{2,1,0:T(8,128)S(1)}, u32[]{:S(2)}, u32[]{:S(2)}) collective-permute-start(f32[64,32,128]{2,1,0:T(8,128)S(1)} %bitcast.85), channel_id=1, source_target_pairs={{0,31},{1,0},{2,1},{3,2},{4,3},{5,4},{6,5},{7,6},{8,7},{9,8},{10,9... | collective-permute-start | bytes 3145736 | tf_op jit(solution)/shard_map/ppermute | solution.py:42
  235.0 1.9 collective-permute-start.2
  237.0 32.3 %collective-permute-done.3 = f32[64,32,128]{2,1,0:T(8,128)S(1)} collective-permute-done((f32[64,32,128]{2,1,0:T(8,128)S(1)}, f32[64,32,128]{2,1,0:T(8,128)S(1)}, u32[]{:S(2)}, u32[]{:S(2)}) %collective-permute-start.3) | collective-permute-done | bytes 1048608 | tf_op jit(solution)/shard_map/ppermute | solution.py:42
  269.2 12.3 %collective-permute-done.2 = f32[64,32,128]{2,1,0:T(8,128)S(1)} collective-permute-done((f32[64,32,128]{2,1,0:T(8,128)S(1)}, f32[64,32,128]{2,1,0:T(8,128)S(1)}, u32[]{:S(2)}, u32[]{:S(2)}) %collective-permute-start.2) | collective-permute-done | bytes 1048608 | tf_op jit(solution)/shard_map/ppermute | solution.py:42
  281.5 1.0 multiply_add_fusion
  282.6 1.6 add_bitcast_fusion
  (74 shorter events, 3.6 us)
Async XLA Ops:
  2.6 4.6 %copy-start.4 = (f32[32,3,128]{2,0,1:T(8,128)S(1)}, f32[32,3,128]{2,0,1:T(8,128)}, u32[]{:S(2)}) copy-start(f32[32,3,128]{2,0,1:T(8,128)} %param.12) | copy-start | bytes 147460
  2.6 26.0 %collective-permute-start.1 = (f32[65,32,128]{2,1,0:T(8,128)S(1)}, f32[65,32,128]{2,1,0:T(8,128)S(1)}, u32[]{:S(2)}, u32[]{:S(2)}) collective-permute-start(f32[65,32,128]{2,1,0:T(8,128)S(1)} %pad_maximum_fusion.9), channel_id=1, source_target_pairs={{0,31},{1,0},{2,1},{3,2},{4,3},{5,4},{6,5},{7,6},{8,7},{9,8},{10,9... | collective-permute-start | bytes 3194888 | tf_op jit(solution)/shard_map/ppermute | solution.py:42
  4.8 36.4 %collective-permute-start = (f32[65,32,128]{2,1,0:T(8,128)S(1)}, f32[65,32,128]{2,1,0:T(8,128)S(1)}, u32[]{:S(2)}, u32[]{:S(2)}) collective-permute-start(f32[65,32,128]{2,1,0:T(8,128)S(1)} %pad_maximum_fusion.8), channel_id=1, source_target_pairs={{0,1},{1,2},{2,3},{3,4},{4,5},{5,6},{6,7},{7,8},{8,9},{9,10},{10,1... | collective-permute-start | bytes 3194888 | tf_op jit(solution)/shard_map/ppermute | solution.py:42
  41.3 1.4 copy-start.3
  54.9 22.4 %copy-start.8 = (bf16[1,1,16,16]{3,2,1,0:T(8,128)(2,1)S(1)}, bf16[1,1,16,16]{3,2,1,0:T(8,128)(2,1)}, u32[]{:S(2)}) copy-start(bf16[1,1,16,16]{3,2,1,0:T(8,128)(2,1)} %param.17) | copy-start | bytes 1540
  54.9 23.0 %copy-start.6 = (f32[32,32]{1,0:T(8,128)S(1)}, f32[32,32]{1,0:T(8,128)}, u32[]{:S(2)}) copy-start(f32[32,32]{1,0:T(8,128)} %param.13) | copy-start | bytes 12292
  54.9 23.8 %copy-start.5 = (bf16[1024,32]{0,1:T(8,128)(2,1)S(1)}, bf16[1024,32]{0,1:T(8,128)(2,1)}, u32[]{:S(2)}) copy-start(bf16[1024,32]{0,1:T(8,128)(2,1)} %param.16) | copy-start | bytes 196612
  54.9 24.0 %copy-start.7 = (s32[1,1,256]{2,1,0:T(1,128)S(1)}, s32[1,1,256]{2,1,0:T(1,128)}, u32[]{:S(2)}) copy-start(s32[1,1,256]{2,1,0:T(1,128)} %param.19) | copy-start | bytes 3076
  54.9 24.0 %copy-start.9 = (s32[1,1,256]{2,1,0:T(1,128)S(1)}, s32[1,1,256]{2,1,0:T(1,128)}, u32[]{:S(2)}) copy-start(s32[1,1,256]{2,1,0:T(1,128)} %param.18) | copy-start | bytes 3076
  54.9 24.1 %copy-start.11 = (f32[32]{0:T(128)S(1)}, f32[32]{0:T(128)}, u32[]{:S(2)}) copy-start(f32[32]{0:T(128)} %param.21) | copy-start | bytes 388
  54.9 24.2 %slice-start = ((bf16[48,1024]{1,0:T(8,128)(2,1)}), bf16[16,1024]{1,0:T(8,128)(2,1)S(1)}, s32[]{:S(2)}) async-start(bf16[48,1024]{1,0:T(8,128)(2,1)} %param.14), calls=%async_computation.2 | async-start | bytes 65536 | tf_op jit(solution)/shard_map/slice | solution.py:130
  55.0 51.0 %all-to-all-start = ((f32[24,32,512]{2,1,0:T(8,128)}), f32[24,32,512]{2,1,0:T(8,128)S(1)}, u32[]{:S(2)}, u32[]{:S(2)}) async-start(f32[24,32,512]{2,1,0:T(8,128)} %copy.30), calls=%async_computation | async-start | bytes 3145728 | tf_op jit(solution)/shard_map/all_to_all | solution.py:247
  78.0 3.1 %slice-start.1 = ((bf16[48,1024]{1,0:T(8,128)(2,1)}), bf16[32,1024]{1,0:T(8,128)(2,1)S(1)}, s32[]{:S(2)}) async-start(bf16[48,1024]{1,0:T(8,128)(2,1)} %param.14), calls=%async_computation.3 | async-start | bytes 131072 | tf_op jit(solution)/shard_map/slice | solution.py:129
  106.0 1.7 copy-start
  136.4 1.3 copy-start.10
  140.4 1.9 copy-start.1
  145.2 1.7 copy-start.2
  206.8 62.4 %collective-permute-start.3 = (f32[64,32,128]{2,1,0:T(8,128)S(1)}, f32[64,32,128]{2,1,0:T(8,128)S(1)}, u32[]{:S(2)}, u32[]{:S(2)}) collective-permute-start(f32[64,32,128]{2,1,0:T(8,128)S(1)} %bitcast.85), channel_id=1, source_target_pairs={{0,31},{1,0},{2,1},{3,2},{4,3},{5,4},{6,5},{7,6},{8,7},{9,8},{10,9... | collective-permute-start | bytes 3145736 | tf_op jit(solution)/shard_map/ppermute | solution.py:42
  235.0 46.5 %collective-permute-start.2 = (f32[64,32,128]{2,1,0:T(8,128)S(1)}, f32[64,32,128]{2,1,0:T(8,128)S(1)}, u32[]{:S(2)}, u32[]{:S(2)}) collective-permute-start(f32[64,32,128]{2,1,0:T(8,128)S(1)} %bitcast.84), channel_id=1, source_target_pairs={{0,1},{1,2},{2,3},{3,4},{4,5},{5,6},{6,7},{7,8},{8,9},{9,10},{10,1... | collective-permute-start | bytes 3145736 | tf_op jit(solution)/shard_map/ppermute | solution.py:42

commit v10 on v9

--- a/solution.py
+++ b/solution.py
@@ -93,7 +93,7 @@
 
 
 def network_kernel(
-    x_ref, pred_ref, w_prof_ref, w_pred_ref, offset_ref, w_out_ref, w_phys_ref, out_ref, staged_ref
+    x_ref, pred_ref, w_prof_ref, w_out_ref, w_phys_ref, out_ref, staged_ref
 ):
     x = x_ref[...]
     narrow = x.astype(jnp.bfloat16)
@@ -101,8 +101,7 @@
     total = jnp.dot(x, w_phys_ref[...], precision=highest, preferred_element_type=jnp.float32)
     for part in range(w_prof_ref.shape[0]):
         pre = jnp.dot(narrow, w_prof_ref[part], preferred_element_type=jnp.float32)
-        pre = pre + jnp.dot(extra, w_pred_ref[part], preferred_element_type=jnp.float32)
-        hidden = jnp.tanh(pre + offset_ref[...]).astype(jnp.bfloat16)
+        hidden = jnp.tanh(pre + extra[part]).astype(jnp.bfloat16)
         total = total + jnp.dot(hidden, w_out_ref[part], preferred_element_type=jnp.float32)
     rows, lanes = total.shape
     groups = out_ref.shape[1] // lanes
@@ -127,7 +126,6 @@
     channels = bias_out.shape[1]
     npred = predictors.shape[1]
     w_prof = block_diagonal(bias_in[:levels], parts, jnp.bfloat16)
-    w_pred = block_diagonal(bias_in[levels:], parts, jnp.bfloat16)
     out_parts = block_diagonal(bias_out.T, parts, jnp.bfloat16)
     w_out = jnp.transpose(out_parts.reshape(parts, parts, channels, hid), (0, 3, 1, 2)).reshape(
         parts, hid, parts * channels
@@ -135,9 +133,9 @@
     phys_parts = block_diagonal(weighting.T, parts, jnp.float32)
     w_phys = jnp.transpose(phys_parts, (1, 0, 2)).reshape(parts * levels, parts * channels)
     column_groups = predictors.shape[0] // parts
-    pred_tiled = jnp.tile(
-        predictors.reshape(column_groups, parts * npred), (rows // column_groups, 1)
-    )
+    pred_term = jnp.dot(predictors, bias_in[levels:], preferred_element_type=jnp.float32)
+    pred_term = (pred_term + bias_offset).reshape(column_groups, parts, hid)
+    pred_tiled = jnp.tile(jnp.transpose(pred_term, (1, 0, 2)), (1, rows // column_groups, 1))
     const = lambda i: (0, 0)
     const3 = lambda i: (0, 0, 0)
     return pl.pallas_call(
@@ -148,10 +146,8 @@
         grid=(total_rows // rows,),
         in_specs=[
             pl.BlockSpec((rows, lanes), lambda i: (i, 0)),
-            pl.BlockSpec((rows, parts * npred), const),
+            pl.BlockSpec((parts, rows, hid), const3),
             pl.BlockSpec((parts, lanes, hid), const3),
-            pl.BlockSpec((parts, parts * npred, hid), const3),
-            pl.BlockSpec((1, hid), const),
             pl.BlockSpec((parts, hid, parts * channels), const3),
             pl.BlockSpec((lanes, parts * channels), const),
         ],
@@ -164,7 +160,7 @@
             transcendentals=total_rows * parts * hid,
             bytes_accessed=total_rows * (lanes + parts * channels) * 4,
         ),
-    )(packed, pred_tiled, w_prof, w_pred, bias_offset.reshape(1, hid), w_out, w_phys)
+    )(packed, pred_tiled, w_prof, w_out, w_phys)
 
 
 def analyse(

time: 285 us -> 283 us (level)
  local copies, waits for them, and re-layouts: 37 us -> 45.8 us
  waiting for transfers between devices: 102 us -> 94.7 us
  Pallas kernels: 26.3 us -> 20.5 us
  matrix products: 9.41 us -> 12.9 us
    another operation x2, local copies, waits for them, and re-layouts: 0.72 us -> 8.4 us  [network(): jnp.tile(jnp.transpose(pred_term, (1, 0, 2)), (1, rows // column_groups, 1))]
    all_to_all x1, waiting for transfers between devices: 23.7 us -> 16.2 us  [shards(): lax.all_to_all(outgoing, 'mem', split_axis=0, concat_axis=0, tiled=True)]
    pallas_call x1, Pallas kernels: 26.3 us -> 20.5 us  [network(): pl.pallas_call(network_kernel, out_shape=jax.ShapeDtypeStruct((total_rows...]
    dot_general x3, matrix products: 6.33 us -> 9.68 us  [multiply_fast(): return jnp.dot(mtx, vectors, precision=lax.Precision.HIGH)]
  transfers between devices with their start and end apart: 5 -> 5, of which waited for: 5 -> 5; matrix products, arithmetic and copies ran while one was open for 2% -> 4% of each run, Pallas kernels for 0% -> 0%
where the time goes in v10:
time: 283 us; the launch traced here: 282 us
  waiting for transfers between devices  94.7 us (33%)
  starting transfers between devices  57 us (20%)
  local copies, waits for them, and re-layouts  45.8 us (16%)
  blocking collectives  38.8 us (14%)
  Pallas kernels  20.5 us (7%)
  matrix products  12.9 us (5%)
  other arithmetic  11.5 us (4%)
    ppermute x4, waiting for transfers between devices, ring_shift(): return lax.ppermute(block, axis, pairs)  78.5 us
    all_to_all x1, blocking collectives, shards(): lax.all_to_all(returning, 'mem', split_axis=0, concat_axis=0, tiled=True)  38.8 us
    ppermute x4, starting transfers between devices, ring_shift(): return lax.ppermute(block, axis, pairs)  34.6 us
    all_to_all x1, starting transfers between devices, shards(): lax.all_to_all(outgoing, 'mem', split_axis=0, concat_axis=0, tiled=True)  22.4 us
    pallas_call x1, Pallas kernels, network(): pl.pallas_call(network_kernel, out_shape=jax.ShapeDtypeStruct((total_rows...  20.5 us
    all_to_all x1, waiting for transfers between devices, shards(): lax.all_to_all(outgoing, 'mem', split_axis=0, concat_axis=0, tiled=True)  16.2 us
    dot_general x3, matrix products, multiply_fast(): return jnp.dot(mtx, vectors, precision=lax.Precision.HIGH)  9.68 us
    another operation x2, local copies, waits for them, and re-layouts, network(): jnp.tile(jnp.transpose(pred_term, (1, 0, 2)), (1, rows // column_groups, 1))  8.4 us
  transfers between devices with their start and end apart: 5, of which 5 were waited for; matrix products, arithmetic and copies ran while one was open for 4% of the time, Pallas kernels for 0%

profile of v10, /device:TPU:512, one launch (start us, length us, event | category | flops | bytes accessed | tf_op | source)
XLA Modules:
  0.0 282.4 jit_solution(15412467047050977378)
XLA Ops:
  0.0 0.7 fusion.39
  0.8 1.8 fusion.38
  2.7 2.1 collective-permute-start.1
  4.8 2.4 collective-permute-start
  7.2 21.5 %collective-permute-done.1 = f32[65,32,128]{2,1,0:T(8,128)S(1)} collective-permute-done((f32[65,32,128]{2,1,0:T(8,128)S(1)}, f32[65,32,128]{2,1,0:T(8,128)S(1)}, u32[]{:S(2)}, u32[]{:S(2)}) %collective-permute-start.1) | collective-permute-done | bytes 1064992 | tf_op jit(solution)/shard_map/ppermute | solution.py:42
  28.7 12.5 %collective-permute-done = f32[65,32,128]{2,1,0:T(8,128)S(1)} collective-permute-done((f32[65,32,128]{2,1,0:T(8,128)S(1)}, f32[65,32,128]{2,1,0:T(8,128)S(1)}, u32[]{:S(2)}, u32[]{:S(2)}) %collective-permute-start) | collective-permute-done | bytes 1064992 | tf_op jit(solution)/shard_map/ppermute | solution.py:42
  41.4 1.3 copy-done.7
  42.7 1.0 multiply_add_fusion.1
  43.8 0.5 multiply_add_fusion.2
  44.2 4.0 %copy.25 = f32[32,3,32,128]{2,3,1,0:T(8,128)} copy(f32[32,3,32,128]{3,2,1,0:T(8,128)S(1)} %multiply_add_fusion.2) | data formatting | bytes 3145728 | tf_op jit(solution)/shard_map/add | solution.py:47
  48.2 4.7 %reshape.227 = f32[24,32,512]{2,0,1:T(8,128)S(1)} reshape(f32[3,8,32,16,32]{4,3,1,0,2:T(8,128)} %bitcast.71) | data formatting | bytes 3145728 | tf_op jit(solution)/shard_map/reshape | solution.py:240
  52.9 2.1 copy.33
  54.9 22.4 %all-to-all-start = ((f32[24,32,512]{2,1,0:T(8,128)}), f32[24,32,512]{2,1,0:T(8,128)S(1)}, u32[]{:S(2)}, u32[]{:S(2)}) async-start(f32[24,32,512]{2,1,0:T(8,128)} %copy.33), calls=%async_computation | async-start | bytes 3145728 | tf_op jit(solution)/shard_map/all_to_all | solution.py:243
  77.5 3.0 %tile.4 = f32[4,64,4,1024]{3,2,1,0:T(4,128)} broadcast(f32[4,4,1024]{2,1,0:T(4,128)S(1)} %copy.27), dimensions={0,2,3} | broadcast | bytes 4259840 | tf_op jit(solution)/shard_map/tile | solution.py:138
  80.6 5.4 %tile.10.pred_ref = f32[4,256,1024]{2,1,0:T(8,128)} reshape(f32[4,64,4,1024]{3,2,1,0:T(4,128)} %tile.4) | data formatting | bytes 8388608 | tf_op jit(solution)/shard_map/tile | solution.py:138
  86.7 0.7 copy.29.w_phys_ref
  87.5 1.1 broadcast_multiply_fusion.1.w_prof_ref
  88.7 1.1 broadcast_multiply_fusion.w_out_ref
  89.8 16.2 %all-to-all-done = f32[24,32,512]{2,1,0:T(8,128)S(1)} async-done(((f32[24,32,512]{2,1,0:T(8,128)}), f32[24,32,512]{2,1,0:T(8,128)S(1)}, u32[]{:S(2)}, u32[]{:S(2)}) %all-to-all-start) | async-done | bytes 1572896 | tf_op jit(solution)/shard_map/all_to_all | solution.py:243
  106.0 1.3 reshape_reshape.3.x_ref
  107.3 0.3 copy-done.2
  107.6 20.5 %shard_map.109 = f32[768,512]{1,0:T(8,128)} custom-call(f32[3072,128]{1,0:T(8,128)} %reshape_reshape.3.x_ref, f32[4,256,1024]{2,1,0:T(8,128)} %tile.10.pred_ref, bf16[4,128,1024]{2,1,0:T(8,128)(2,1)} %broadcast_multiply_fusion.1.w_prof_ref, bf16[4,1024,128]{2,1,0:T(8,128)(2,1)} %broadcast_multiply_fusion.w_out_ref, f32[128,128]{1,0:T(8,128)} %copy.29.w_phys_ref), custom_call_target="tpu_custom_call" | custom-call | flops 8053063680 | bytes 3145728 | tf_op jit(solution)/shard_map/pallas_call | solution.py:141
  128.2 1.9 copy.30
  130.0 1.1 gather_fusion
  131.6 0.3 convolution_reduce_fusion
  132.2 1.1 fusion.12
  133.9 1.9 add_divide_fusion
  136.3 1.5 copy-done.6
  137.7 2.1 fusion.6
  139.8 3.2 %fusion.3 = f32[768,512]{1,0:T(8,128)} fusion(f32[768,768]{1,0:T(8,128)S(1)} %copy-done.6, f32[768,512]{1,0:T(8,128)S(1)} %fusion.6, f32[768,512]{1,0:T(8,128)S(1)} %bitcast_subtract_fusion), kind=kOutput, calls=%fused_computation.32 | convolution fusion | flops 1812725760 | bytes 7077888 | tf_op jit(solution)/shard_map/dot_general | solution.py:205
  143.0 0.3 fusion.13
  143.6 0.3 fusion.15
  144.1 0.3 fusion.17
  144.7 0.3 fusion.19
  145.2 0.3 fusion.21
  145.8 0.3 copy-done.5
  146.1 0.9 fusion.40
  146.9 4.4 %add_add_fusion = f32[768,512]{1,0:T(8,128)S(1)} fusion(f32[768,512]{1,0:T(8,128)S(1)} %copy-done.5, f32[768,768]{1,0:T(8,128)} %add_divide_fusion, f32[768,512]{1,0:T(8,128)} %fusion.3, f32[512]{0:T(512)S(1)} %bitcast.96, f32[]{:T(128)S(6)} %sqrt.3, f32[512]{0:T(512)S(1)} %broadcast_multiply_fusion.6), kind=kOutput, calls=%fused_computation.28 | convolution fusion | flops 1814691840 | bytes 7081988 | tf_op jit(solution)/shard_map/dot_general | solution.py:205
  151.3 38.8 %all_to_all.10 = f32[24,32,512]{2,1,0:T(8,128)S(1)} all-to-all(f32[24,32,512]{2,1,0:T(8,128)S(1)} %bitcast.78), channel_id=1, replica_groups=mesh['mem'=24,'lon'=32] {'mem'}, dimensions={0} | all-to-all | bytes 3145728 | tf_op jit(solution)/shard_map/all_to_all | solution.py:260
  190.1 3.8 %reshape.209 = f32[3,8,32,16,32]{4,3,2,1,0:T(8,128)} reshape(f32[24,32,512]{2,1,0:T(8,128)S(1)} %all_to_all.10) | data formatting | bytes 3145728 | tf_op jit(solution)/shard_map/reshape | solution.py:261
  193.9 6.4 %copy.31 = f32[32,3,32,8,16]{2,4,3,1,0:T(8,128)} copy(f32[32,3,32,8,16]{2,4,0,3,1:T(8,128)} %bitcast.69) | data formatting | bytes 3145728 | tf_op jit(solution)/shard_map/transpose | solution.py:262
  200.3 4.4 %copy.32 = f32[32,3,32,128]{3,2,1,0:T(8,128)S(1)} copy(f32[32,3,32,128]{2,3,1,0:T(8,128)} %bitcast.70) | data formatting | bytes 3145728 | tf_op jit(solution)/shard_map/reshape | solution.py:262
  204.9 28.2 %collective-permute-start.3 = (f32[64,32,128]{2,1,0:T(8,128)S(1)}, f32[64,32,128]{2,1,0:T(8,128)S(1)}, u32[]{:S(2)}, u32[]{:S(2)}) collective-permute-start(f32[64,32,128]{2,1,0:T(8,128)S(1)} %bitcast.84), channel_id=1, source_target_pairs={{0,31},{1,0},{2,1},{3,2},{4,3},{5,4},{6,5},{7,6},{8,7},{9,8},{10,9... | collective-permute-start | bytes 3145736 | tf_op jit(solution)/shard_map/ppermute | solution.py:42
  233.2 1.9 collective-permute-start.2
  235.1 32.3 %collective-permute-done.3 = f32[64,32,128]{2,1,0:T(8,128)S(1)} collective-permute-done((f32[64,32,128]{2,1,0:T(8,128)S(1)}, f32[64,32,128]{2,1,0:T(8,128)S(1)}, u32[]{:S(2)}, u32[]{:S(2)}) %collective-permute-start.3) | collective-permute-done | bytes 1048608 | tf_op jit(solution)/shard_map/ppermute | solution.py:42
  267.4 12.3 %collective-permute-done.2 = f32[64,32,128]{2,1,0:T(8,128)S(1)} collective-permute-done((f32[64,32,128]{2,1,0:T(8,128)S(1)}, f32[64,32,128]{2,1,0:T(8,128)S(1)}, u32[]{:S(2)}, u32[]{:S(2)}) %collective-permute-start.2) | collective-permute-done | bytes 1048608 | tf_op jit(solution)/shard_map/ppermute | solution.py:42
  279.7 1.0 multiply_add_fusion
  280.7 1.6 add_bitcast_fusion
  (81 shorter events, 3.8 us)
Async XLA Ops:
  0.0 77.3 %copy-start = (bf16[1,1,16,16]{3,2,1,0:T(8,128)(2,1)S(1)}, bf16[1,1,16,16]{3,2,1,0:T(8,128)(2,1)}, u32[]{:S(2)}) copy-start(bf16[1,1,16,16]{3,2,1,0:T(8,128)(2,1)} %param.17) | copy-start | bytes 1540
  2.6 4.6 %copy-start.8 = (f32[32,3,128]{2,0,1:T(8,128)S(1)}, f32[32,3,128]{2,0,1:T(8,128)}, u32[]{:S(2)}) copy-start(f32[32,3,128]{2,0,1:T(8,128)} %param.12) | copy-start | bytes 147460
  2.7 26.0 %collective-permute-start.1 = (f32[65,32,128]{2,1,0:T(8,128)S(1)}, f32[65,32,128]{2,1,0:T(8,128)S(1)}, u32[]{:S(2)}, u32[]{:S(2)}) collective-permute-start(f32[65,32,128]{2,1,0:T(8,128)S(1)} %pad_maximum_fusion.9), channel_id=1, source_target_pairs={{0,31},{1,0},{2,1},{3,2},{4,3},{5,4},{6,5},{7,6},{8,7},{9,8},{10,9... | collective-permute-start | bytes 3194888 | tf_op jit(solution)/shard_map/ppermute | solution.py:42
  4.8 36.4 %collective-permute-start = (f32[65,32,128]{2,1,0:T(8,128)S(1)}, f32[65,32,128]{2,1,0:T(8,128)S(1)}, u32[]{:S(2)}, u32[]{:S(2)}) collective-permute-start(f32[65,32,128]{2,1,0:T(8,128)S(1)} %pad_maximum_fusion.8), channel_id=1, source_target_pairs={{0,1},{1,2},{2,3},{3,4},{4,5},{5,6},{6,7},{7,8},{8,9},{9,10},{10,1... | collective-permute-start | bytes 3194888 | tf_op jit(solution)/shard_map/ppermute | solution.py:42
  41.3 1.4 copy-start.7
  54.9 22.4 %copy-start.9 = (bf16[48,1024]{1,0:T(8,128)(2,1)S(1)}, bf16[48,1024]{1,0:T(8,128)(2,1)}, u32[]{:S(2)}) copy-start(bf16[48,1024]{1,0:T(8,128)(2,1)} %param.14) | copy-start | bytes 294916
  54.9 22.4 %copy-start.14 = (f32[1024]{0:T(1024)S(1)}, f32[1024]{0:T(1024)}, u32[]{:S(2)}) copy-start(f32[1024]{0:T(1024)} %param.15) | copy-start | bytes 12292
  54.9 51.0 %all-to-all-start = ((f32[24,32,512]{2,1,0:T(8,128)}), f32[24,32,512]{2,1,0:T(8,128)S(1)}, u32[]{:S(2)}, u32[]{:S(2)}) async-start(f32[24,32,512]{2,1,0:T(8,128)} %copy.33), calls=%async_computation | async-start | bytes 3145728 | tf_op jit(solution)/shard_map/all_to_all | solution.py:243
  80.6 5.6 %copy-start.10 = (bf16[1024,32]{0,1:T(8,128)(2,1)S(1)}, bf16[1024,32]{0,1:T(8,128)(2,1)}, u32[]{:S(2)}) copy-start(bf16[1024,32]{0,1:T(8,128)(2,1)} %param.16) | copy-start | bytes 196612
  80.6 5.8 %copy-start.11 = (f32[32,32]{1,0:T(8,128)S(1)}, f32[32,32]{1,0:T(8,128)}, u32[]{:S(2)}) copy-start(f32[32,32]{1,0:T(8,128)} %param.13) | copy-start | bytes 12292
  80.6 6.8 %copy-start.12 = (s32[1,1,256]{2,1,0:T(1,128)S(1)}, s32[1,1,256]{2,1,0:T(1,128)}, u32[]{:S(2)}) copy-start(s32[1,1,256]{2,1,0:T(1,128)} %param.19) | copy-start | bytes 3076
  80.6 6.8 %copy-start.13 = (s32[1,1,256]{2,1,0:T(1,128)S(1)}, s32[1,1,256]{2,1,0:T(1,128)}, u32[]{:S(2)}) copy-start(s32[1,1,256]{2,1,0:T(1,128)} %param.18) | copy-start | bytes 3076
  80.6 6.8 %copy-start.16 = (f32[32]{0:T(128)S(1)}, f32[32]{0:T(128)}, u32[]{:S(2)}) copy-start(f32[32]{0:T(128)} %param.21) | copy-start | bytes 388
  80.6 6.9 %slice-start = ((bf16[48,1024]{1,0:T(8,128)(2,1)}), bf16[32,1024]{1,0:T(8,128)(2,1)S(1)}, s32[]{:S(2)}) async-start(bf16[48,1024]{1,0:T(8,128)(2,1)} %param.14), calls=%async_computation.2 | async-start | bytes 131072 | tf_op jit(solution)/shard_map/slice | solution.py:128
  106.0 1.7 copy-start.2
  130.0 1.3 copy-start.15
  133.9 2.0 copy-start.3
  136.1 1.7 copy-start.6
  137.7 2.1 copy-start.4
  144.7 1.4 copy-start.5
  204.9 62.5 %collective-permute-start.3 = (f32[64,32,128]{2,1,0:T(8,128)S(1)}, f32[64,32,128]{2,1,0:T(8,128)S(1)}, u32[]{:S(2)}, u32[]{:S(2)}) collective-permute-start(f32[64,32,128]{2,1,0:T(8,128)S(1)} %bitcast.84), channel_id=1, source_target_pairs={{0,31},{1,0},{2,1},{3,2},{4,3},{5,4},{6,5},{7,6},{8,7},{9,8},{10,9... | collective-permute-start | bytes 3145736 | tf_op jit(solution)/shard_map/ppermute | solution.py:42
  233.2 46.5 %collective-permute-start.2 = (f32[64,32,128]{2,1,0:T(8,128)S(1)}, f32[64,32,128]{2,1,0:T(8,128)S(1)}, u32[]{:S(2)}, u32[]{:S(2)}) collective-permute-start(f32[64,32,128]{2,1,0:T(8,128)S(1)} %bitcast.83), channel_id=1, source_target_pairs={{0,1},{1,2},{2,3},{3,4},{4,5},{5,6},{6,7},{7,8},{8,9},{9,10},{10,1... | collective-permute-start | bytes 3145736 | tf_op jit(solution)/shard_map/ppermute | solution.py:42
  280.7 1.6 copy-start.1
